TPU v7x, 1024 devices: a whole 4x8x16 slice. The times are simulated.
1024 devices in a mesh: seq: 128 (over z, x, core), head: 8 (over y).
Axes of the slice: x: 4, y: 8, z: 16, core: 2. Of those that a mesh axis runs over, the one named last changes fastest.
Arguments:
- queries: bfloat16 [65536, 2048], P(('seq', 'head')), may hold values from -6 to 6
- key_vectors: bfloat16 [65536, 2048], P(('seq', 'head')), may hold values from -6 to 6
- value_vectors: bfloat16 [65536, 2048], P(('seq', 'head')), may hold values from -6 to 6
- grad_output: bfloat16 [65536, 2048], P(('seq', 'head')), may hold values from -6 to 6
- level_weights: int32 [9, 16, 65536], P(None, 'head', 'seq'), may hold values from 0 to 127
Outputs:
- output: bfloat16 [65536, 2048], P('seq', 'head')
- grad_query: bfloat16 [65536, 2048], P('seq', 'head')
- grad_key: bfloat16 [65536, 2048], P('seq', 'head')
- grad_value: bfloat16 [65536, 2048], P('seq', 'head')
All inputs are finite; a program needn't handle non-finite values.
Results may differ from a plain program's by a relative error of at most 0.0057.
Values may be sent and summed in bfloat16 or wider, within the bound.
No kernel may reach another device: no remote copies, remote signals or barrier semaphores. Data moves between devices by JAX's collectives and lax.ppermute only.
A program may use at most 32 MiB of HBM per device.

v0:
```python
import jax
import jax.numpy as jnp
import numpy as np
from jax import lax
from jax.sharding import PartitionSpec as P

SPAN = 256


def swapped(value, axis, distance):
    mask = 2**distance
    pairs = [(source, source ^ mask) for source in range(lax.axis_size(axis))]
    return lax.ppermute(value, axis, pairs)


def bucket_table(per_dev, local_levels):
    level_table = np.zeros((local_levels, per_dev, per_dev), np.float32)
    for target in range(per_dev):
        begin_at = target >> 1 << 1
        end_at = target >> 0 << 0
        level_table[0, target, begin_at:end_at] = 1.0
    return jnp.asarray(level_table)


def body(queries, key_vectors, value_vectors, grad_output, level_weights):
    query_in, key_in, value_in, cotan_in = (
        lax.all_to_all(queries, "head", split_axis=1, concat_axis=0, tiled=True),
        lax.all_to_all(key_vectors, "head", split_axis=1, concat_axis=0, tiled=True),
        lax.all_to_all(value_vectors, "head", split_axis=1, concat_axis=0, tiled=True),
        lax.all_to_all(grad_output, "head", split_axis=1, concat_axis=0, tiled=True),
    )
    tokens_dev = query_in.shape[0]
    heads_local = level_weights.shape[1]
    head_size = query_in.shape[1] // heads_local
    levels_all = level_weights.shape[0]
    per_dev = tokens_dev // SPAN
    local_levels = per_dev.bit_length() - 1
    cross_levels = lax.axis_size("seq").bit_length() - 1

    def split_spans(matrix):
        return matrix.reshape(per_dev, SPAN, heads_local, head_size)

    query_rows = split_spans(query_in)
    key_rows = split_spans(key_in)
    value_rows = split_spans(value_in)
    cotan_rows = split_spans(cotan_in)
    gain_list = [(head_size * SPAN) ** (-0.5)] + [
        (head_size * 2**tree_level * SPAN) ** (-0.5) for tree_level in range(levels_all - 1)
    ]
    level_gains = jnp.array(gain_list, jnp.float32)
    weights = (level_weights.astype(jnp.float32) / 64.0 * level_gains[:, None, None]).reshape(
        levels_all, heads_local, per_dev, SPAN
    )
    intra_w = jnp.transpose(weights[0], (1, 0, 2))[:, :, :, None]
    inter_w = jnp.transpose(weights[1:], (2, 0, 3, 1))[..., None]
    position = jnp.arange(SPAN, dtype=jnp.int32)
    causal = position[:, None] >= position[None, :]
    scores = jnp.einsum("bthp,buhp->bhtu", query_rows, key_rows, preferred_element_type=jnp.float32)
    attention = jnp.where(causal, scores * intra_w, 0.0).astype(jnp.bfloat16)
    cotan_scores = jnp.einsum(
        "bthr,buhr->bhtu", cotan_rows, value_rows, preferred_element_type=jnp.float32
    )
    grad_scores = jnp.where(causal, cotan_scores * intra_w, 0.0).astype(jnp.bfloat16)
    output = jnp.einsum(
        "bhtu,buhr->bthr", attention, value_rows, preferred_element_type=jnp.float32
    )
    grad_query = jnp.einsum(
        "bhtu,buhp->bthp", grad_scores, key_rows, preferred_element_type=jnp.float32
    )
    grad_key = jnp.einsum(
        "bhtu,bthp->buhp", grad_scores, query_rows, preferred_element_type=jnp.float32
    )
    grad_value = jnp.einsum(
        "bhtu,bthr->buhr", attention, cotan_rows, preferred_element_type=jnp.float32
    )
    states = jnp.einsum("buhp,buhr->bhpr", key_rows, value_rows, preferred_element_type=jnp.float32)
    seq_index = lax.axis_index("seq")
    upper_bits = (jnp.right_shift(seq_index, jnp.arange(cross_levels, dtype=jnp.int32)) % 2).astype(
        jnp.float32
    )
    running = jnp.sum(states, axis=0)
    cross_list = []
    for tree_bit in range(cross_levels):
        partner = swapped(running, "seq", tree_bit)
        cross_list.append(partner * upper_bits[tree_bit])
        running = running + partner
    level_table = bucket_table(per_dev, local_levels)
    local_buckets = jnp.einsum(
        "mji,ihpr->jmhpr", level_table, states, precision=lax.Precision.HIGHEST
    )
    cross_stack = jnp.stack(cross_list)
    cross_buckets = jnp.broadcast_to(cross_stack[None], (per_dev,) + cross_stack.shape)
    buckets = jnp.concatenate([local_buckets, cross_buckets], axis=1).astype(jnp.bfloat16)
    inter_out = jnp.einsum(
        "bthp,bmhpr->bmthr", query_rows, buckets, preferred_element_type=jnp.float32
    )
    output = output + jnp.sum(inter_w * inter_out, axis=1)
    inter_grad = jnp.einsum(
        "bmhpr,bthr->bmthp", buckets, cotan_rows, preferred_element_type=jnp.float32
    )
    grad_query = grad_query + jnp.sum(inter_w * inter_grad, axis=1)
    weighted = (inter_w * cotan_rows[:, None]).astype(jnp.bfloat16)
    level_grads = jnp.einsum(
        "bthp,bmthr->bmhpr", query_rows, weighted, preferred_element_type=jnp.float32
    )
    local_grad = jnp.einsum(
        "mji,jmhpr->ihpr",
        level_table,
        level_grads[:, :local_levels],
        precision=lax.Precision.HIGHEST,
    )
    masked = jnp.sum(level_grads[:, local_levels:], axis=0) * upper_bits[:, None, None, None]
    pending = masked
    device_grad = jnp.zeros_like(running)
    for tree_bit in range(cross_levels):
        arrived = swapped(pending, "seq", tree_bit)
        device_grad = device_grad + (1.0 - upper_bits[tree_bit]) * arrived[0]
        pending = pending[1:] + arrived[1:]
    state_grad = (local_grad + device_grad[None]).astype(jnp.bfloat16)
    grad_key = grad_key + jnp.einsum(
        "buhr,bhpr->buhp", value_rows, state_grad, preferred_element_type=jnp.float32
    )
    grad_value = grad_value + jnp.einsum(
        "buhp,bhpr->buhr", key_rows, state_grad, preferred_element_type=jnp.float32
    )

    def merge_rows(matrix):
        return matrix.reshape(tokens_dev, heads_local * head_size).astype(jnp.bfloat16)

    return (
        merge_rows(output),
        merge_rows(grad_query),
        merge_rows(grad_key),
        merge_rows(grad_value),
    )


def solution(mesh):
    placed = (
        P(("seq", "head"), None),
        P(("seq", "head"), None),
        P(("seq", "head"), None),
        P(("seq", "head"), None),
        P(None, "head", "seq"),
    )
    return jax.shard_map(
        body,
        mesh=mesh,
        in_specs=placed,
        out_specs=(P("seq", "head"), P("seq", "head"), P("seq", "head"), P("seq", "head")),
        check_vma=False,
    )
```

profile of v0, /device:TPU:1, one launch (start us, length us, event | category | flops | bytes accessed | tf_op | source)
XLA Modules:
  0.0 257.8 jit_solution(4858767519541726082)
XLA Ops:
  2.4 7.7 %all-to-all-start = ((bf16[64,8,256]{2,0,1:T(8,128)(2,1)}), bf16[64,8,256]{2,0,1:T(8,128)(2,1)S(1)}, u32[]{:S(2)}, u32[]{:S(2)}) async-start(bf16[64,8,256]{2,0,1:T(8,128)(2,1)} %bitcast.125), calls=%async_computation | async-start | bytes 524288 | tf_op jit(solution)/shard_map/all_to_all | solution.py:27
  11.7 7.7 %all-to-all-done = bf16[64,8,256]{2,0,1:T(8,128)(2,1)S(1)} async-done(((bf16[64,8,256]{2,0,1:T(8,128)(2,1)}), bf16[64,8,256]{2,0,1:T(8,128)(2,1)S(1)}, u32[]{:S(2)}, u32[]{:S(2)}) %all-to-all-start) | async-done | bytes 262176 | tf_op jit(solution)/shard_map/all_to_all | solution.py:27
  19.4 3.4 %all-to-all-start.1 = ((bf16[64,8,256]{2,0,1:T(8,128)(2,1)}), bf16[64,8,256]{2,0,1:T(8,128)(2,1)S(1)}, u32[]{:S(2)}, u32[]{:S(2)}) async-start(bf16[64,8,256]{2,0,1:T(8,128)(2,1)} %bitcast.124), calls=%async_computation.1 | async-start | bytes 524288 | tf_op jit(solution)/shard_map/all_to_all | solution.py:28
  23.5 8.9 %all-to-all-done.1 = bf16[64,8,256]{2,0,1:T(8,128)(2,1)S(1)} async-done(((bf16[64,8,256]{2,0,1:T(8,128)(2,1)}), bf16[64,8,256]{2,0,1:T(8,128)(2,1)S(1)}, u32[]{:S(2)}, u32[]{:S(2)}) %all-to-all-start.1) | async-done | bytes 262176 | tf_op jit(solution)/shard_map/all_to_all | solution.py:28
  32.5 3.4 %all-to-all-start.2 = ((bf16[64,8,256]{2,0,1:T(8,128)(2,1)}), bf16[64,8,256]{2,0,1:T(8,128)(2,1)S(1)}, u32[]{:S(2)}, u32[]{:S(2)}) async-start(bf16[64,8,256]{2,0,1:T(8,128)(2,1)} %bitcast.123), calls=%async_computation.2 | async-start | bytes 524288 | tf_op jit(solution)/shard_map/all_to_all | solution.py:29
  36.6 9.9 %all-to-all-done.2 = bf16[64,8,256]{2,0,1:T(8,128)(2,1)S(1)} async-done(((bf16[64,8,256]{2,0,1:T(8,128)(2,1)}), bf16[64,8,256]{2,0,1:T(8,128)(2,1)S(1)}, u32[]{:S(2)}, u32[]{:S(2)}) %all-to-all-start.2) | async-done | bytes 262176 | tf_op jit(solution)/shard_map/all_to_all | solution.py:29
  46.6 3.4 %all-to-all-start.3 = ((bf16[64,8,256]{2,0,1:T(8,128)(2,1)}), bf16[64,8,256]{2,0,1:T(8,128)(2,1)S(1)}, u32[]{:S(2)}, u32[]{:S(2)}) async-start(bf16[64,8,256]{2,0,1:T(8,128)(2,1)} %bitcast.122), calls=%async_computation.3 | async-start | bytes 524288 | tf_op jit(solution)/shard_map/all_to_all | solution.py:30
  55.5 5.9 %all-to-all-done.3 = bf16[64,8,256]{2,0,1:T(8,128)(2,1)S(1)} async-done(((bf16[64,8,256]{2,0,1:T(8,128)(2,1)}), bf16[64,8,256]{2,0,1:T(8,128)(2,1)S(1)}, u32[]{:S(2)}, u32[]{:S(2)}) %all-to-all-start.3) | async-done | bytes 262176 | tf_op jit(solution)/shard_map/all_to_all | solution.py:30
  62.4 16.1 %collective-permute-start = (f32[2,128,128]{2,1,0:T(8,128)S(1)}, f32[2,128,128]{2,1,0:T(8,128)}, u32[]{:S(2)}, u32[]{:S(2)}) collective-permute-start(f32[2,128,128]{2,1,0:T(8,128)S(1)} %get-tuple-element.11), channel_id=1, source_target_pairs={{0,8},{8,0},{16,24},{24,16},{32,40},{40,32},{48,56},{56,48},{64,72... | collective-permute-start | bytes 393224 | tf_op jit(solution)/shard_map/ppermute | solution.py:13
  79.7 1.9 collective-permute-start.7
  85.0 1.9 collective-permute-start.8
  94.2 3.4 %collective-permute-start.1 = (f32[2,128,128]{2,1,0:T(8,128)S(1)}, f32[2,128,128]{2,1,0:T(8,128)S(1)}, u32[]{:S(2)}, u32[]{:S(2)}) collective-permute-start(f32[2,128,128]{2,1,0:T(8,128)S(1)} %add.94), channel_id=1, source_target_pairs={{0,16},{8,24},{16,0},{24,8},{32,48},{40,56},{48,32},{56,40},{64,80... | collective-permute-start | bytes 393224 | tf_op jit(solution)/shard_map/ppermute | solution.py:13
  97.5 2.2 bitcast_dynamic-update-slice_fusion.6
  99.7 9.0 %collective-permute-done.1 = f32[2,128,128]{2,1,0:T(8,128)S(1)} collective-permute-done((f32[2,128,128]{2,1,0:T(8,128)S(1)}, f32[2,128,128]{2,1,0:T(8,128)S(1)}, u32[]{:S(2)}, u32[]{:S(2)}) %collective-permute-start.1) | collective-permute-done | bytes 131104 | tf_op jit(solution)/shard_map/ppermute | solution.py:13
  108.7 1.9 collective-permute-start.2
  111.8 4.1 %collective-permute-done.2 = f32[2,128,128]{2,1,0:T(8,128)S(1)} collective-permute-done((f32[2,128,128]{2,1,0:T(8,128)S(1)}, f32[2,128,128]{2,1,0:T(8,128)S(1)}, u32[]{:S(2)}, u32[]{:S(2)}) %collective-permute-start.2) | collective-permute-done | bytes 131104 | tf_op jit(solution)/shard_map/ppermute | solution.py:13
  115.9 1.9 collective-permute-start.3
  119.0 2.5 collective-permute-start.9
  122.8 1.9 collective-permute-start.4
  125.9 5.3 %collective-permute-done.4 = f32[2,128,128]{2,1,0:T(8,128)S(1)} collective-permute-done((f32[2,128,128]{2,1,0:T(8,128)S(1)}, f32[2,128,128]{2,1,0:T(8,128)S(1)}, u32[]{:S(2)}, u32[]{:S(2)}) %collective-permute-start.4) | collective-permute-done | bytes 131104 | tf_op jit(solution)/shard_map/ppermute | solution.py:13
  131.2 6.4 %collective-permute-start.5 = (f32[2,128,128]{2,1,0:T(8,128)S(1)}, f32[2,128,128]{2,1,0:T(8,128)S(1)}, u32[]{:S(2)}, u32[]{:S(2)}) collective-permute-start(f32[2,128,128]{2,1,0:T(8,128)S(1)} %add.98), channel_id=1, source_target_pairs={{0,256},{8,264},{16,272},{24,280},{32,288},{40,296},{48,304},{56,3... | collective-permute-start | bytes 393224 | tf_op jit(solution)/shard_map/ppermute | solution.py:13
  138.8 9.7 %collective-permute-done.5 = f32[2,128,128]{2,1,0:T(8,128)S(1)} collective-permute-done((f32[2,128,128]{2,1,0:T(8,128)S(1)}, f32[2,128,128]{2,1,0:T(8,128)S(1)}, u32[]{:S(2)}, u32[]{:S(2)}) %collective-permute-start.5) | collective-permute-done | bytes 131104 | tf_op jit(solution)/shard_map/ppermute | solution.py:13
  148.6 13.9 %collective-permute-start.6 = (f32[2,128,128]{2,1,0:T(8,128)S(1)}, f32[2,128,128]{2,1,0:T(8,128)S(1)}, u32[]{:S(2)}, u32[]{:S(2)}) collective-permute-start(f32[2,128,128]{2,1,0:T(8,128)S(1)} %add.99), channel_id=1, source_target_pairs={{0,512},{8,520},{16,528},{24,536},{32,544},{40,552},{48,560},{56,5... | collective-permute-start | bytes 393224 | tf_op jit(solution)/shard_map/ppermute | solution.py:13
  163.5 1.9 collective-permute-start.10
  173.9 7.3 %collective-permute-done.10 = f32[4,2,128,128]{2,3,0,1:T(8,128)} collective-permute-done((f32[4,2,128,128]{2,3,0,1:T(8,128)}, f32[4,2,128,128]{2,3,0,1:T(8,128)}, u32[]{:S(2)}, u32[]{:S(2)}) %collective-permute-start.10) | collective-permute-done | bytes 524320 | tf_op jit(solution)/shard_map/ppermute | solution.py:13
  181.2 1.9 slice_add_fusion.3
  183.1 1.9 collective-permute-start.11
  186.7 17.9 %collective-permute-done.11 = f32[3,2,128,128]{2,3,0,1:T(8,128)S(1)} collective-permute-done((f32[3,2,128,128]{2,3,0,1:T(8,128)}, f32[3,2,128,128]{2,3,0,1:T(8,128)S(1)}, u32[]{:S(2)}, u32[]{:S(2)}) %collective-permute-start.11) | collective-permute-done | bytes 393248 | tf_op jit(solution)/shard_map/ppermute | solution.py:13
  205.6 4.7 %collective-permute-start.12 = (f32[2,2,128,128]{2,3,0,1:T(8,128)S(1)}, f32[2,2,128,128]{2,3,0,1:T(8,128)S(1)}, u32[]{:S(2)}, u32[]{:S(2)}) collective-permute-start(f32[2,2,128,128]{2,3,0,1:T(8,128)S(1)} %slice_add_fusion.4), channel_id=1, source_target_pairs={{0,256},{8,264},{16,272},{24,280},{32,288},{40,296},{48,304},{56,3... | collective-permute-start | bytes 786440 | tf_op jit(solution)/shard_map/ppermute | solution.py:13
  210.8 27.5 %collective-permute-done.12 = f32[2,2,128,128]{2,3,0,1:T(8,128)S(1)} collective-permute-done((f32[2,2,128,128]{2,3,0,1:T(8,128)S(1)}, f32[2,2,128,128]{2,3,0,1:T(8,128)S(1)}, u32[]{:S(2)}, u32[]{:S(2)}) %collective-permute-start.12) | collective-permute-done | bytes 262176 | tf_op jit(solution)/shard_map/ppermute | solution.py:13
  238.4 1.9 collective-permute-start.13
  241.2 12.3 %collective-permute-done.13 = f32[1,2,128,128]{2,3,0,1:T(8,128)S(1)} collective-permute-done((f32[1,2,128,128]{2,3,0,1:T(8,128)S(1)}, f32[1,2,128,128]{2,3,0,1:T(8,128)S(1)}, u32[]{:S(2)}, u32[]{:S(2)}) %collective-permute-start.13) | collective-permute-done | bytes 131104 | tf_op jit(solution)/shard_map/ppermute | solution.py:13
  (106 shorter events, 42.5 us)
Async XLA Ops:
  0.6 22.2 %copy-start.6 = (bf16[64,2048]{1,0:T(8,128)(2,1)S(1)}, bf16[64,2048]{1,0:T(8,128)(2,1)}, u32[]{:S(2)}) copy-start(bf16[64,2048]{1,0:T(8,128)(2,1)} %param.9) | copy-start | bytes 786436
  0.6 35.3 %copy-start.7 = (bf16[64,2048]{1,0:T(8,128)(2,1)S(1)}, bf16[64,2048]{1,0:T(8,128)(2,1)}, u32[]{:S(2)}) copy-start(bf16[64,2048]{1,0:T(8,128)(2,1)} %param.10) | copy-start | bytes 786436
  0.7 49.3 %copy-start.14 = (s32[9,2,512]{2,1,0:T(2,128)S(1)}, s32[9,2,512]{2,1,0:T(2,128)}, u32[]{:S(2)}) copy-start(s32[9,2,512]{2,1,0:T(2,128)} %param.11) | copy-start | bytes 110596
  0.7 49.3 %copy-start.15 = (f32[9]{0:T(128)S(1)}, f32[9]{0:T(128)}, u32[]{:S(2)}) copy-start(f32[9]{0:T(128)} %constant.41) | copy-start | bytes 112
  2.4 17.0 %all-to-all-start = ((bf16[64,8,256]{2,0,1:T(8,128)(2,1)}), bf16[64,8,256]{2,0,1:T(8,128)(2,1)S(1)}, u32[]{:S(2)}, u32[]{:S(2)}) async-start(bf16[64,8,256]{2,0,1:T(8,128)(2,1)} %bitcast.125), calls=%async_computation | async-start | bytes 524288 | tf_op jit(solution)/shard_map/all_to_all | solution.py:27
  19.4 13.1 %all-to-all-start.1 = ((bf16[64,8,256]{2,0,1:T(8,128)(2,1)}), bf16[64,8,256]{2,0,1:T(8,128)(2,1)S(1)}, u32[]{:S(2)}, u32[]{:S(2)}) async-start(bf16[64,8,256]{2,0,1:T(8,128)(2,1)} %bitcast.124), calls=%async_computation.1 | async-start | bytes 524288 | tf_op jit(solution)/shard_map/all_to_all | solution.py:28
  32.5 14.1 %all-to-all-start.2 = ((bf16[64,8,256]{2,0,1:T(8,128)(2,1)}), bf16[64,8,256]{2,0,1:T(8,128)(2,1)S(1)}, u32[]{:S(2)}, u32[]{:S(2)}) async-start(bf16[64,8,256]{2,0,1:T(8,128)(2,1)} %bitcast.123), calls=%async_computation.2 | async-start | bytes 524288 | tf_op jit(solution)/shard_map/all_to_all | solution.py:29
  46.6 14.8 %all-to-all-start.3 = ((bf16[64,8,256]{2,0,1:T(8,128)(2,1)}), bf16[64,8,256]{2,0,1:T(8,128)(2,1)S(1)}, u32[]{:S(2)}, u32[]{:S(2)}) async-start(bf16[64,8,256]{2,0,1:T(8,128)(2,1)} %bitcast.122), calls=%async_computation.3 | async-start | bytes 524288 | tf_op jit(solution)/shard_map/all_to_all | solution.py:30
  55.2 23.5 %copy-start.9 = (f32[8,2,2,256]{3,0,1,2:T(8,128)}, f32[8,2,2,256]{3,0,1,2:T(8,128)S(1)}, u32[]{:S(2)}) copy-start(f32[8,2,2,256]{3,0,1,2:T(8,128)S(1)} %copy.190) | copy-start | bytes 98308
  62.4 30.8 %collective-permute-start = (f32[2,128,128]{2,1,0:T(8,128)S(1)}, f32[2,128,128]{2,1,0:T(8,128)}, u32[]{:S(2)}, u32[]{:S(2)}) collective-permute-start(f32[2,128,128]{2,1,0:T(8,128)S(1)} %get-tuple-element.11), channel_id=1, source_target_pairs={{0,8},{8,0},{16,24},{24,16},{32,40},{40,32},{48,56},{56,48},{64,72... | collective-permute-start | bytes 393224 | tf_op jit(solution)/shard_map/ppermute | solution.py:13
  79.7 4.4 %collective-permute-start.7 = (f32[7,2,128,128]{2,3,0,1:T(8,128)S(1)}, f32[7,2,128,128]{2,3,0,1:T(8,128)S(1)}, u32[]{:S(2)}, u32[]{:S(2)}) collective-permute-start(f32[7,2,128,128]{2,3,0,1:T(8,128)S(1)} %broadcast_multiply_fusion), channel_id=1, source_target_pairs={{0,8},{8,0},{16,24},{24,16},{32,40},{40,32},{48,56},{56,48},{64,72... | collective-permute-start | bytes 2752520 | tf_op jit(solution)/shard_map/ppermute | solution.py:13
  83.0 3.9 %copy-start.5 = (f32[2,2,128,128]{3,2,1,0:T(8,128)S(1)}, f32[2,2,128,128]{3,2,1,0:T(8,128)}, u32[]{:S(2)}) copy-start(f32[2,2,128,128]{3,2,1,0:T(8,128)} %get-tuple-element.12) | copy-start | bytes 786436
  85.0 32.9 %collective-permute-start.8 = (f32[6,2,128,128]{2,3,0,1:T(8,128)S(1)}, f32[6,2,128,128]{2,3,0,1:T(8,128)}, u32[]{:S(2)}, u32[]{:S(2)}) collective-permute-start(f32[6,2,128,128]{2,3,0,1:T(8,128)S(1)} %slice_add_fusion), channel_id=1, source_target_pairs={{0,16},{8,24},{16,0},{24,8},{32,48},{40,56},{48,32},{56,40},{64,80... | collective-permute-start | bytes 2359304 | tf_op jit(solution)/shard_map/ppermute | solution.py:13
  94.2 14.5 %collective-permute-start.1 = (f32[2,128,128]{2,1,0:T(8,128)S(1)}, f32[2,128,128]{2,1,0:T(8,128)S(1)}, u32[]{:S(2)}, u32[]{:S(2)}) collective-permute-start(f32[2,128,128]{2,1,0:T(8,128)S(1)} %add.94), channel_id=1, source_target_pairs={{0,16},{8,24},{16,0},{24,8},{32,48},{40,56},{48,32},{56,40},{64,80... | collective-permute-start | bytes 393224 | tf_op jit(solution)/shard_map/ppermute | solution.py:13
  108.7 7.2 %collective-permute-start.2 = (f32[2,128,128]{2,1,0:T(8,128)S(1)}, f32[2,128,128]{2,1,0:T(8,128)S(1)}, u32[]{:S(2)}, u32[]{:S(2)}) collective-permute-start(f32[2,128,128]{2,1,0:T(8,128)S(1)} %add.95), channel_id=1, source_target_pairs={{0,32},{8,40},{16,48},{24,56},{32,0},{40,8},{48,16},{56,24},{64,96... | collective-permute-start | bytes 393224 | tf_op jit(solution)/shard_map/ppermute | solution.py:13
  115.9 6.8 %collective-permute-start.3 = (f32[2,128,128]{2,1,0:T(8,128)S(1)}, f32[2,128,128]{2,1,0:T(8,128)S(1)}, u32[]{:S(2)}, u32[]{:S(2)}) collective-permute-start(f32[2,128,128]{2,1,0:T(8,128)S(1)} %add.96), channel_id=1, source_target_pairs={{0,64},{8,72},{16,80},{24,88},{32,96},{40,104},{48,112},{56,120},{... | collective-permute-start | bytes 393224 | tf_op jit(solution)/shard_map/ppermute | solution.py:13
  119.0 43.5 %collective-permute-start.9 = (f32[5,2,128,128]{2,3,0,1:T(8,128)S(1)}, f32[5,2,128,128]{2,3,0,1:T(8,128)S(1)}, u32[]{:S(2)}, u32[]{:S(2)}) collective-permute-start(f32[5,2,128,128]{2,3,0,1:T(8,128)S(1)} %slice_add_fusion.1), channel_id=1, source_target_pairs={{0,32},{8,40},{16,48},{24,56},{32,0},{40,8},{48,16},{56,24},{64,96... | collective-permute-start | bytes 1966088 | tf_op jit(solution)/shard_map/ppermute | solution.py:13
  122.8 8.4 %collective-permute-start.4 = (f32[2,128,128]{2,1,0:T(8,128)S(1)}, f32[2,128,128]{2,1,0:T(8,128)S(1)}, u32[]{:S(2)}, u32[]{:S(2)}) collective-permute-start(f32[2,128,128]{2,1,0:T(8,128)S(1)} %add.97), channel_id=1, source_target_pairs={{0,128},{8,136},{16,144},{24,152},{32,160},{40,168},{48,176},{56,1... | collective-permute-start | bytes 393224 | tf_op jit(solution)/shard_map/ppermute | solution.py:13
  131.2 17.4 %collective-permute-start.5 = (f32[2,128,128]{2,1,0:T(8,128)S(1)}, f32[2,128,128]{2,1,0:T(8,128)S(1)}, u32[]{:S(2)}, u32[]{:S(2)}) collective-permute-start(f32[2,128,128]{2,1,0:T(8,128)S(1)} %add.98), channel_id=1, source_target_pairs={{0,256},{8,264},{16,272},{24,280},{32,288},{40,296},{48,304},{56,3... | collective-permute-start | bytes 393224 | tf_op jit(solution)/shard_map/ppermute | solution.py:13
  148.6 22.5 %copy-start.10 = (f32[8,2,2,256]{3,0,1,2:T(8,128)S(1)}, f32[8,2,2,256]{3,0,1,2:T(8,128)}, u32[]{:S(2)}) copy-start(f32[8,2,2,256]{3,0,1,2:T(8,128)} %copy-done.9) | copy-start | bytes 98308
  148.6 22.5 %copy-start.12 = (bf16[2,1,2,128,128]{3,4,1,2,0:T(8,128)(2,1)S(1)}, bf16[2,1,2,128,128]{3,4,1,2,0:T(8,128)(2,1)}, u32[]{:S(2)}) copy-start(bf16[2,1,2,128,128]{3,4,1,2,0:T(8,128)(2,1)} %copy.87) | copy-start | bytes 393220
  148.6 18.8 %collective-permute-start.6 = (f32[2,128,128]{2,1,0:T(8,128)S(1)}, f32[2,128,128]{2,1,0:T(8,128)S(1)}, u32[]{:S(2)}, u32[]{:S(2)}) collective-permute-start(f32[2,128,128]{2,1,0:T(8,128)S(1)} %add.99), channel_id=1, source_target_pairs={{0,512},{8,520},{16,528},{24,536},{32,544},{40,552},{48,560},{56,5... | collective-permute-start | bytes 393224 | tf_op jit(solution)/shard_map/ppermute | solution.py:13
  162.5 4.8 %copy-start.4 = (f32[5,2,128,128]{2,3,0,1:T(8,128)}, f32[5,2,128,128]{2,3,0,1:T(8,128)S(1)}, u32[]{:S(2)}) copy-start(f32[5,2,128,128]{2,3,0,1:T(8,128)S(1)} %collective-permute-done.9) | copy-start | bytes 1966084
  163.5 17.7 %collective-permute-start.10 = (f32[4,2,128,128]{2,3,0,1:T(8,128)}, f32[4,2,128,128]{2,3,0,1:T(8,128)}, u32[]{:S(2)}, u32[]{:S(2)}) collective-permute-start(f32[4,2,128,128]{2,3,0,1:T(8,128)} %slice_add_fusion.2), channel_id=1, source_target_pairs={{0,64},{8,72},{16,80},{24,88},{32,96},{40,104},{48,112},{56,120},{... | collective-permute-start | bytes 1572872 | tf_op jit(solution)/shard_map/ppermute | solution.py:13
  173.9 11.8 %copy-start.3 = (bf16[2,7,2,128,128]{3,4,1,2,0:T(8,128)(2,1)S(1)}, bf16[2,7,2,128,128]{3,4,1,2,0:T(8,128)(2,1)}, u32[]{:S(2)}) copy-start(bf16[2,7,2,128,128]{3,4,1,2,0:T(8,128)(2,1)} %copy-done.2) | copy-start | bytes 2752516
  173.9 11.8 %copy-start.11 = (f32[8,2,2,256]{3,0,1,2:T(8,128)S(1)}, f32[8,2,2,256]{3,0,1,2:T(8,128)}, u32[]{:S(2)}) copy-start(f32[8,2,2,256]{3,0,1,2:T(8,128)} %copy-done.9) | copy-start | bytes 98308
  173.9 11.8 %copy-start.13 = (bf16[2,1,2,128,128]{3,4,1,2,0:T(8,128)(2,1)S(1)}, bf16[2,1,2,128,128]{3,4,1,2,0:T(8,128)(2,1)}, u32[]{:S(2)}) copy-start(bf16[2,1,2,128,128]{3,4,1,2,0:T(8,128)(2,1)} %copy.87) | copy-start | bytes 393220
  183.1 21.4 %collective-permute-start.11 = (f32[3,2,128,128]{2,3,0,1:T(8,128)}, f32[3,2,128,128]{2,3,0,1:T(8,128)S(1)}, u32[]{:S(2)}, u32[]{:S(2)}) collective-permute-start(f32[3,2,128,128]{2,3,0,1:T(8,128)} %slice_add_fusion.3), channel_id=1, source_target_pairs={{0,128},{8,136},{16,144},{24,152},{32,160},{40,168},{48,176},{56,1... | collective-permute-start | bytes 1179656 | tf_op jit(solution)/shard_map/ppermute | solution.py:13
  205.6 49.2 %copy-start.8 = (f32[2,2,128,128]{3,0,2,1:T(2,128)S(1)}, f32[2,2,128,128]{3,0,2,1:T(2,128)}, u32[]{:S(2)}) copy-start(f32[2,2,128,128]{3,0,2,1:T(2,128)} %copy.103) | copy-start | bytes 786436
  205.6 32.8 %collective-permute-start.12 = (f32[2,2,128,128]{2,3,0,1:T(8,128)S(1)}, f32[2,2,128,128]{2,3,0,1:T(8,128)S(1)}, u32[]{:S(2)}, u32[]{:S(2)}) collective-permute-start(f32[2,2,128,128]{2,3,0,1:T(8,128)S(1)} %slice_add_fusion.4), channel_id=1, source_target_pairs={{0,256},{8,264},{16,272},{24,280},{32,288},{40,296},{48,304},{56,3... | collective-permute-start | bytes 786440 | tf_op jit(solution)/shard_map/ppermute | solution.py:13
  210.5 45.4 %copy-start = (f32[2,256,2,128]{3,1,2,0:T(8,128)S(1)}, f32[2,256,2,128]{3,1,2,0:T(8,128)}, u32[]{:S(2)}) copy-start(f32[2,256,2,128]{3,1,2,0:T(8,128)} %convolution_bitcast_fusion.3) | copy-start | bytes 1572868
  238.4 15.1 %collective-permute-start.13 = (f32[1,2,128,128]{2,3,0,1:T(8,128)S(1)}, f32[1,2,128,128]{2,3,0,1:T(8,128)S(1)}, u32[]{:S(2)}, u32[]{:S(2)}) collective-permute-start(f32[1,2,128,128]{2,3,0,1:T(8,128)S(1)} %slice_add_fusion.5), channel_id=1, source_target_pairs={{0,512},{8,520},{16,528},{24,536},{32,544},{40,552},{48,560},{56,5... | collective-permute-start | bytes 393224 | tf_op jit(solution)/shard_map/ppermute | solution.py:13
  (3 other events, 5.8 us)
where the time goes:
time: 259 us; the launch traced here: 258 us
  waiting for transfers between devices  127 us (49%)
  starting transfers between devices  80.1 us (31%)
  local copies, waits for them, and re-layouts  17.9 us (7%)
  other arithmetic  17.3 us (7%)
  matrix products  9.94 us (4%)
  between operations  5.6 us (2%)
    ppermute x14, waiting for transfers between devices, swapped(): return lax.ppermute(value, axis, pairs)  94.5 us
    ppermute x14, starting transfers between devices, swapped(): return lax.ppermute(value, axis, pairs)  62.2 us
    all_to_all x1, waiting for transfers between devices, body(): lax.all_to_all(value_vectors, 'head', split_axis=1, concat_axis=0, tiled=...  9.94 us
    all_to_all x1, waiting for transfers between devices, body(): lax.all_to_all(key_vectors, 'head', split_axis=1, concat_axis=0, tiled=True)  8.94 us
    unnamed x6, other arithmetic  8.32 us
    all_to_all x1, waiting for transfers between devices, body(): lax.all_to_all(queries, 'head', split_axis=1, concat_axis=0, tiled=True)  7.66 us
    all_to_all x1, starting transfers between devices, body(): lax.all_to_all(queries, 'head', split_axis=1, concat_axis=0, tiled=True)  7.65 us
    all_to_all x1, waiting for transfers between devices, body(): lax.all_to_all(grad_output, 'head', split_axis=1, concat_axis=0, tiled=True)  5.92 us
  transfers between devices with their start and end apart: 18, of which 14 were waited for; matrix products, arithmetic and copies ran while one was open for 13% of the time, Pallas kernels for 0%

commit v1 on v0

--- a/solution.py
+++ b/solution.py
@@ -23,12 +23,9 @@
 
 
 def body(queries, key_vectors, value_vectors, grad_output, level_weights):
-    query_in, key_in, value_in, cotan_in = (
-        lax.all_to_all(queries, "head", split_axis=1, concat_axis=0, tiled=True),
-        lax.all_to_all(key_vectors, "head", split_axis=1, concat_axis=0, tiled=True),
-        lax.all_to_all(value_vectors, "head", split_axis=1, concat_axis=0, tiled=True),
-        lax.all_to_all(grad_output, "head", split_axis=1, concat_axis=0, tiled=True),
-    )
+    stacked = jnp.stack([queries, key_vectors, value_vectors, grad_output], axis=1)
+    exchanged = lax.all_to_all(stacked, "head", split_axis=2, concat_axis=0, tiled=True)
+    query_in, key_in, value_in, cotan_in = (exchanged[:, index] for index in range(4))
     tokens_dev = query_in.shape[0]
     heads_local = level_weights.shape[1]
     head_size = query_in.shape[1] // heads_local
@@ -78,12 +75,22 @@
     upper_bits = (jnp.right_shift(seq_index, jnp.arange(cross_levels, dtype=jnp.int32)) % 2).astype(
         jnp.float32
     )
+    weighted = (inter_w * cotan_rows[:, None]).astype(jnp.bfloat16)
+    level_grads = jnp.einsum(
+        "bthp,bmthr->bmhpr", query_rows, weighted, preferred_element_type=jnp.float32
+    )
     running = jnp.sum(states, axis=0)
+    pending = jnp.sum(level_grads[:, local_levels:], axis=0) * upper_bits[:, None, None, None]
+    device_grad = jnp.zeros_like(running)
     cross_list = []
     for tree_bit in range(cross_levels):
-        partner = swapped(running, "seq", tree_bit)
+        packet = jnp.concatenate([running[None], pending], axis=0)
+        arrived = swapped(packet, "seq", tree_bit)
+        partner = arrived[0]
         cross_list.append(partner * upper_bits[tree_bit])
         running = running + partner
+        device_grad = device_grad + (1.0 - upper_bits[tree_bit]) * arrived[1]
+        pending = pending[1:] + arrived[2:]
     level_table = bucket_table(per_dev, local_levels)
     local_buckets = jnp.einsum(
         "mji,ihpr->jmhpr", level_table, states, precision=lax.Precision.HIGHEST
@@ -99,23 +106,12 @@
         "bmhpr,bthr->bmthp", buckets, cotan_rows, preferred_element_type=jnp.float32
     )
     grad_query = grad_query + jnp.sum(inter_w * inter_grad, axis=1)
-    weighted = (inter_w * cotan_rows[:, None]).astype(jnp.bfloat16)
-    level_grads = jnp.einsum(
-        "bthp,bmthr->bmhpr", query_rows, weighted, preferred_element_type=jnp.float32
-    )
     local_grad = jnp.einsum(
         "mji,jmhpr->ihpr",
         level_table,
         level_grads[:, :local_levels],
         precision=lax.Precision.HIGHEST,
     )
-    masked = jnp.sum(level_grads[:, local_levels:], axis=0) * upper_bits[:, None, None, None]
-    pending = masked
-    device_grad = jnp.zeros_like(running)
-    for tree_bit in range(cross_levels):
-        arrived = swapped(pending, "seq", tree_bit)
-        device_grad = device_grad + (1.0 - upper_bits[tree_bit]) * arrived[0]
-        pending = pending[1:] + arrived[1:]
     state_grad = (local_grad + device_grad[None]).astype(jnp.bfloat16)
     grad_key = grad_key + jnp.einsum(
         "buhr,bhpr->buhp", value_rows, state_grad, preferred_element_type=jnp.float32

time: 259 us -> 248 us (0.958)
  starting transfers between devices: 80.1 us -> 69.4 us
  waiting for transfers between devices: 127 us -> 119 us
  local copies, waits for them, and re-layouts: 17.9 us -> 23.4 us
    all_to_all x4 -> x1, waiting for transfers between devices: 32.5 us -> 16 us  [body(): lax.all_to_all(stacked, 'head', split_axis=2, concat_axis=0, tiled=True)]
    all_to_all x4 -> x1, starting transfers between devices: 17.9 us -> 7.65 us  [body(): lax.all_to_all(stacked, 'head', split_axis=2, concat_axis=0, tiled=True)]
    ppermute x14 -> x7, waiting for transfers between devices: 94.5 us -> 103 us  [swapped(): return lax.ppermute(value, axis, pairs)]
    unnamed x34 -> x58, local copies, waits for them, and re-layouts: 1.86 us -> 6.89 us
    add x6 -> x5, other arithmetic: 5.14 us -> 1.26 us  [body(): pending = pending[1:] + arrived[2:]]
    all_to_all x4 -> x1, local copies, waits for them, and re-layouts: 4.83 us -> 1.24 us  [body(): lax.all_to_all(stacked, 'head', split_axis=2, concat_axis=0, tiled=True)]
    another operation x3 -> x11, local copies, waits for them, and re-layouts: 3.79 us -> 7.24 us  [the longest x5 3.8 us: split_spans(): return matrix.reshape(per_dev, SPAN, heads_local, head_size)]
    unnamed x6 -> x5, other arithmetic: 8.32 us -> 7.68 us
  transfers between devices with their start and end apart: 18 -> 8, of which waited for: 14 -> 8; matrix products, arithmetic and copies ran while one was open for 13% -> 5% of each run, Pallas kernels for 0% -> 0%
where the time goes in v1:
time: 248 us; the launch traced here: 247 us
  waiting for transfers between devices  119 us (48%)
  starting transfers between devices  69.4 us (28%)
  local copies, waits for them, and re-layouts  23.4 us (9%)
  other arithmetic  17.1 us (7%)
  matrix products  12.4 us (5%)
  between operations  5.66 us (2%)
    ppermute x7, waiting for transfers between devices, swapped(): return lax.ppermute(value, axis, pairs)  103 us
    ppermute x7, starting transfers between devices, swapped(): return lax.ppermute(value, axis, pairs)  61.7 us
    all_to_all x1, waiting for transfers between devices, body(): lax.all_to_all(stacked, 'head', split_axis=2, concat_axis=0, tiled=True)  16 us
    unnamed x5, other arithmetic  7.68 us
    all_to_all x1, starting transfers between devices, body(): lax.all_to_all(stacked, 'head', split_axis=2, concat_axis=0, tiled=True)  7.65 us
    unnamed x58, local copies, waits for them, and re-layouts  6.89 us
  transfers between devices with their start and end apart: 8, of which 8 were waited for; matrix products, arithmetic and copies ran while one was open for 5% of the time, Pallas kernels for 0%

profile of v1, /device:TPU:1, one launch (start us, length us, event | category | flops | bytes accessed | tf_op | source)
XLA Modules:
  0.0 246.7 jit_solution(16722880337113865320)
XLA Ops:
  0.6 1.3 pad_maximum_fusion
  2.0 1.4 copy.164
  3.4 2.7 %reshape.69 = bf16[8,2,32768]{2,1,0:T(2,128)(2,1)} reshape(bf16[2048,4,64]{2,1,0:T(4,128)(2,1)S(1)} %bitcast.108) | data formatting | bytes 2097152
  6.1 7.7 %all-to-all-start = ((bf16[8,2,32768]{2,1,0:T(2,128)(2,1)}), bf16[8,2,32768]{2,1,0:T(2,128)(2,1)S(1)}, u32[]{:S(2)}, u32[]{:S(2)}) async-start(bf16[8,2,32768]{2,1,0:T(2,128)(2,1)} %reshape.69), calls=%async_computation | async-start | bytes 2097152 | tf_op jit(solution)/shard_map/all_to_all | solution.py:27
  14.5 16.0 %all-to-all-done = bf16[8,2,32768]{2,1,0:T(2,128)(2,1)S(1)} async-done(((bf16[8,2,32768]{2,1,0:T(2,128)(2,1)}), bf16[8,2,32768]{2,1,0:T(2,128)(2,1)S(1)}, u32[]{:S(2)}, u32[]{:S(2)}) %all-to-all-start) | async-done | bytes 1048608 | tf_op jit(solution)/shard_map/all_to_all | solution.py:27
  30.5 1.4 reshape.70
  31.9 1.2 copy.207
  36.1 1.5 copy.177
  40.7 1.9 fusion.45
  42.7 15.1 %collective-permute-start = (f32[8,2,128,128]{3,2,1,0:T(8,128)S(1)}, f32[8,2,128,128]{3,2,1,0:T(8,128)S(1)}, u32[]{:S(2)}, u32[]{:S(2)}) collective-permute-start(f32[8,2,128,128]{3,2,1,0:T(8,128)S(1)} %pad_maximum_fusion.1), channel_id=1, source_target_pairs={{0,8},{8,0},{16,24},{24,16},{32,40},{40,32},{48,56},{56,48},{64,72... | collective-permute-start | bytes 3145736 | tf_op jit(solution)/shard_map/ppermute | solution.py:13
  57.7 2.3 collective-permute-done
  61.0 2.8 %collective-permute-start.1 = (f32[7,2,128,128]{3,2,1,0:T(8,128)S(1)}, f32[7,2,128,128]{3,2,1,0:T(8,128)S(1)}, u32[]{:S(2)}, u32[]{:S(2)}) collective-permute-start(f32[7,2,128,128]{3,2,1,0:T(8,128)S(1)} %pad_maximum_fusion.5), channel_id=1, source_target_pairs={{0,16},{8,24},{16,0},{24,8},{32,48},{40,56},{48,32},{56,40},{64,80... | collective-permute-start | bytes 2752520 | tf_op jit(solution)/shard_map/ppermute | solution.py:13
  63.8 20.6 %collective-permute-done.1 = f32[7,2,128,128]{3,2,1,0:T(8,128)S(1)} collective-permute-done((f32[7,2,128,128]{3,2,1,0:T(8,128)S(1)}, f32[7,2,128,128]{3,2,1,0:T(8,128)S(1)}, u32[]{:S(2)}, u32[]{:S(2)}) %collective-permute-start.1) | collective-permute-done | bytes 917536 | tf_op jit(solution)/shard_map/ppermute | solution.py:13
  84.6 4.4 %collective-permute-start.2 = (f32[6,2,128,128]{3,2,1,0:T(8,128)S(1)}, f32[6,2,128,128]{3,2,1,0:T(8,128)S(1)}, u32[]{:S(2)}, u32[]{:S(2)}) collective-permute-start(f32[6,2,128,128]{3,2,1,0:T(8,128)S(1)} %pad_maximum_fusion.6), channel_id=1, source_target_pairs={{0,32},{8,40},{16,48},{24,56},{32,0},{40,8},{48,16},{56,24},{64,96... | collective-permute-start | bytes 2359304 | tf_op jit(solution)/shard_map/ppermute | solution.py:13
  89.0 16.9 %collective-permute-done.2 = f32[6,2,128,128]{3,2,1,0:T(8,128)S(1)} collective-permute-done((f32[6,2,128,128]{3,2,1,0:T(8,128)S(1)}, f32[6,2,128,128]{3,2,1,0:T(8,128)S(1)}, u32[]{:S(2)}, u32[]{:S(2)}) %collective-permute-start.2) | collective-permute-done | bytes 786464 | tf_op jit(solution)/shard_map/ppermute | solution.py:13
  106.0 3.9 %collective-permute-start.3 = (f32[5,2,128,128]{3,2,1,0:T(8,128)S(1)}, f32[5,2,128,128]{3,2,1,0:T(8,128)S(1)}, u32[]{:S(2)}, u32[]{:S(2)}) collective-permute-start(f32[5,2,128,128]{3,2,1,0:T(8,128)S(1)} %pad_maximum_fusion.7), channel_id=1, source_target_pairs={{0,64},{8,72},{16,80},{24,88},{32,96},{40,104},{48,112},{56,120},{... | collective-permute-start | bytes 1966088 | tf_op jit(solution)/shard_map/ppermute | solution.py:13
  110.5 12.3 %collective-permute-done.3 = f32[5,2,128,128]{3,2,1,0:T(8,128)S(1)} collective-permute-done((f32[5,2,128,128]{3,2,1,0:T(8,128)S(1)}, f32[5,2,128,128]{3,2,1,0:T(8,128)S(1)}, u32[]{:S(2)}, u32[]{:S(2)}) %collective-permute-start.3) | collective-permute-done | bytes 655392 | tf_op jit(solution)/shard_map/ppermute | solution.py:13
  124.4 5.8 %collective-permute-start.4 = (f32[4,2,128,128]{3,2,1,0:T(8,128)}, f32[4,2,128,128]{3,2,1,0:T(8,128)}, u32[]{:S(2)}, u32[]{:S(2)}) collective-permute-start(f32[4,2,128,128]{3,2,1,0:T(8,128)} %pad_maximum_fusion.8), channel_id=1, source_target_pairs={{0,128},{8,136},{16,144},{24,152},{32,160},{40,168},{48,176},{56,1... | collective-permute-start | bytes 1572872 | tf_op jit(solution)/shard_map/ppermute | solution.py:13
  137.6 1.3 fusion.9
  139.0 2.3 fusion.8
  141.3 11.9 %collective-permute-done.4 = f32[4,2,128,128]{3,2,1,0:T(8,128)} collective-permute-done((f32[4,2,128,128]{3,2,1,0:T(8,128)}, f32[4,2,128,128]{3,2,1,0:T(8,128)}, u32[]{:S(2)}, u32[]{:S(2)}) %collective-permute-start.4) | collective-permute-done | bytes 524320 | tf_op jit(solution)/shard_map/ppermute | solution.py:13
  155.2 10.8 %collective-permute-start.5 = (f32[3,2,128,128]{3,2,1,0:T(8,128)S(1)}, f32[3,2,128,128]{3,2,1,0:T(8,128)S(1)}, u32[]{:S(2)}, u32[]{:S(2)}) collective-permute-start(f32[3,2,128,128]{3,2,1,0:T(8,128)S(1)} %pad_maximum_fusion.9), channel_id=1, source_target_pairs={{0,256},{8,264},{16,272},{24,280},{32,288},{40,296},{48,304},{56,3... | collective-permute-start | bytes 1179656 | tf_op jit(solution)/shard_map/ppermute | solution.py:13
  166.9 32.9 %collective-permute-done.5 = f32[3,2,128,128]{3,2,1,0:T(8,128)S(1)} collective-permute-done((f32[3,2,128,128]{3,2,1,0:T(8,128)S(1)}, f32[3,2,128,128]{3,2,1,0:T(8,128)S(1)}, u32[]{:S(2)}, u32[]{:S(2)}) %collective-permute-start.5) | collective-permute-done | bytes 393248 | tf_op jit(solution)/shard_map/ppermute | solution.py:13
  200.6 19.0 %collective-permute-start.6 = (f32[2,2,128,128]{3,2,1,0:T(8,128)S(1)}, f32[2,2,128,128]{3,2,1,0:T(8,128)S(1)}, u32[]{:S(2)}, u32[]{:S(2)}) collective-permute-start(f32[2,2,128,128]{3,2,1,0:T(8,128)S(1)} %pad_maximum_fusion.10), channel_id=1, source_target_pairs={{0,512},{8,520},{16,528},{24,536},{32,544},{40,552},{48,560},{56,5... | collective-permute-start | bytes 786440 | tf_op jit(solution)/shard_map/ppermute | solution.py:13
  221.7 1.3 fusion.47
  223.0 6.1 %collective-permute-done.6 = f32[2,2,128,128]{3,2,1,0:T(8,128)S(1)} collective-permute-done((f32[2,2,128,128]{3,2,1,0:T(8,128)S(1)}, f32[2,2,128,128]{3,2,1,0:T(8,128)S(1)}, u32[]{:S(2)}, u32[]{:S(2)}) %collective-permute-start.6) | collective-permute-done | bytes 262176 | tf_op jit(solution)/shard_map/ppermute | solution.py:13
  229.0 2.0 fusion.32
  233.1 1.5 multiply_dynamic-update-slice_fusion.4
  234.6 1.6 multiply_dynamic-update-slice_fusion.3
  236.2 1.6 multiply_dynamic-update-slice_fusion.2
  237.7 1.6 multiply_dynamic-update-slice_fusion.1
  239.3 1.5 multiply_dynamic-update-slice_fusion
  (116 shorter events, 26.9 us)
Async XLA Ops:
  3.4 10.4 %copy-start.25 = (s32[9,2,512]{2,1,0:T(2,128)S(1)}, s32[9,2,512]{2,1,0:T(2,128)}, u32[]{:S(2)}) copy-start(s32[9,2,512]{2,1,0:T(2,128)} %param.11) | copy-start | bytes 110596
  3.4 10.4 %copy-start.26 = (f32[9]{0:T(128)S(1)}, f32[9]{0:T(128)}, u32[]{:S(2)}) copy-start(f32[9]{0:T(128)} %constant.41) | copy-start | bytes 112
  6.1 24.4 %all-to-all-start = ((bf16[8,2,32768]{2,1,0:T(2,128)(2,1)}), bf16[8,2,32768]{2,1,0:T(2,128)(2,1)S(1)}, u32[]{:S(2)}, u32[]{:S(2)}) async-start(bf16[8,2,32768]{2,1,0:T(2,128)(2,1)} %reshape.69), calls=%async_computation | async-start | bytes 2097152 | tf_op jit(solution)/shard_map/all_to_all | solution.py:27
  13.8 19.4 %copy-start.21 = (f32[9,2,512]{2,1,0:T(2,128)}, f32[9,2,512]{2,1,0:T(2,128)S(1)}, u32[]{:S(2)}) copy-start(f32[9,2,512]{2,1,0:T(2,128)S(1)} %convert_multiply_fusion) | copy-start | bytes 110596
  33.2 1.2 copy-start.22
  34.4 1.8 copy-start
  42.7 17.4 %collective-permute-start = (f32[8,2,128,128]{3,2,1,0:T(8,128)S(1)}, f32[8,2,128,128]{3,2,1,0:T(8,128)S(1)}, u32[]{:S(2)}, u32[]{:S(2)}) collective-permute-start(f32[8,2,128,128]{3,2,1,0:T(8,128)S(1)} %pad_maximum_fusion.1), channel_id=1, source_target_pairs={{0,8},{8,0},{16,24},{24,16},{32,40},{40,32},{48,56},{56,48},{64,72... | collective-permute-start | bytes 3145736 | tf_op jit(solution)/shard_map/ppermute | solution.py:13
  60.0 1.0 copy-start.8
  61.0 23.4 %collective-permute-start.1 = (f32[7,2,128,128]{3,2,1,0:T(8,128)S(1)}, f32[7,2,128,128]{3,2,1,0:T(8,128)S(1)}, u32[]{:S(2)}, u32[]{:S(2)}) collective-permute-start(f32[7,2,128,128]{3,2,1,0:T(8,128)S(1)} %pad_maximum_fusion.5), channel_id=1, source_target_pairs={{0,16},{8,24},{16,0},{24,8},{32,48},{40,56},{48,32},{56,40},{64,80... | collective-permute-start | bytes 2752520 | tf_op jit(solution)/shard_map/ppermute | solution.py:13
  84.4 21.5 %copy-start.9 = (f32[7,2,128,128]{3,2,1,0:T(8,128)}, f32[7,2,128,128]{3,2,1,0:T(8,128)S(1)}, u32[]{:S(2)}) copy-start(f32[7,2,128,128]{3,2,1,0:T(8,128)S(1)} %collective-permute-done.1) | copy-start | bytes 2752516
  84.6 21.2 %collective-permute-start.2 = (f32[6,2,128,128]{3,2,1,0:T(8,128)S(1)}, f32[6,2,128,128]{3,2,1,0:T(8,128)S(1)}, u32[]{:S(2)}, u32[]{:S(2)}) collective-permute-start(f32[6,2,128,128]{3,2,1,0:T(8,128)S(1)} %pad_maximum_fusion.6), channel_id=1, source_target_pairs={{0,32},{8,40},{16,48},{24,56},{32,0},{40,8},{48,16},{56,24},{64,96... | collective-permute-start | bytes 2359304 | tf_op jit(solution)/shard_map/ppermute | solution.py:13
  105.8 17.0 %copy-start.12 = (f32[6,2,128,128]{3,2,1,0:T(8,128)}, f32[6,2,128,128]{3,2,1,0:T(8,128)S(1)}, u32[]{:S(2)}) copy-start(f32[6,2,128,128]{3,2,1,0:T(8,128)S(1)} %collective-permute-done.2) | copy-start | bytes 2359300
  105.9 30.8 %copy-start.1 = (bf16[2,256,2,128]{3,2,1,0:T(2,128)(2,1)S(1)}, bf16[2,256,2,128]{3,2,1,0:T(2,128)(2,1)}, u32[]{:S(2)}) copy-start(bf16[2,256,2,128]{3,2,1,0:T(2,128)(2,1)} %copy-done) | copy-start | bytes 786436
  106.0 16.8 %collective-permute-start.3 = (f32[5,2,128,128]{3,2,1,0:T(8,128)S(1)}, f32[5,2,128,128]{3,2,1,0:T(8,128)S(1)}, u32[]{:S(2)}, u32[]{:S(2)}) collective-permute-start(f32[5,2,128,128]{3,2,1,0:T(8,128)S(1)} %pad_maximum_fusion.7), channel_id=1, source_target_pairs={{0,64},{8,72},{16,80},{24,88},{32,96},{40,104},{48,112},{56,120},{... | collective-permute-start | bytes 1966088 | tf_op jit(solution)/shard_map/ppermute | solution.py:13
  122.8 1.6 copy-start.16
  122.8 16.1 %copy-start.4 = (bf16[2,256,2,128]{3,2,1,0:T(2,128)(2,1)S(1)}, bf16[2,256,2,128]{3,2,1,0:T(2,128)(2,1)}, u32[]{:S(2)}) copy-start(bf16[2,256,2,128]{3,2,1,0:T(2,128)(2,1)} %copy-done.3) | copy-start | bytes 786436
  124.4 28.8 %collective-permute-start.4 = (f32[4,2,128,128]{3,2,1,0:T(8,128)}, f32[4,2,128,128]{3,2,1,0:T(8,128)}, u32[]{:S(2)}, u32[]{:S(2)}) collective-permute-start(f32[4,2,128,128]{3,2,1,0:T(8,128)} %pad_maximum_fusion.8), channel_id=1, source_target_pairs={{0,128},{8,136},{16,144},{24,152},{32,160},{40,168},{48,176},{56,1... | collective-permute-start | bytes 1572872 | tf_op jit(solution)/shard_map/ppermute | solution.py:13
  137.6 16.5 %copy-start.11 = (f32[1,2,128,128]{3,2,1,0:T(8,128)S(1)}, f32[1,2,128,128]{3,2,1,0:T(8,128)}, u32[]{:S(2)}) copy-start(f32[1,2,128,128]{3,2,1,0:T(8,128)} %copy-done.10) | copy-start | bytes 393220
  139.0 28.0 %copy-start.5 = (bf16[2,2,256,256]{3,2,1,0:T(8,128)(2,1)}, bf16[2,2,256,256]{3,2,1,0:T(8,128)(2,1)S(1)}, u32[]{:S(2)}) copy-start(bf16[2,2,256,256]{3,2,1,0:T(8,128)(2,1)S(1)} %fusion.9) | copy-start | bytes 1572868
  139.0 27.7 %copy-start.14 = (bf16[2,256,2,128]{1,3,2,0:T(8,128)(2,1)S(1)}, bf16[2,256,2,128]{1,3,2,0:T(8,128)(2,1)}, u32[]{:S(2)}) copy-start(bf16[2,256,2,128]{1,3,2,0:T(8,128)(2,1)} %copy.189) | copy-start | bytes 786436
  154.2 65.5 %copy-start.18 = (f32[2,2,128,128]{3,2,1,0:T(8,128)S(1)}, f32[2,2,128,128]{3,2,1,0:T(8,128)}, u32[]{:S(2)}) copy-start(f32[2,2,128,128]{3,2,1,0:T(8,128)} %get-tuple-element.20) | copy-start | bytes 786436
  154.2 65.5 %copy-start.27 = (f32[2,2,1,1]{1,0,3,2:T(2,128)S(1)}, f32[2,2,1,1]{1,0,3,2:T(2,128)}, u32[]{:S(2)}) copy-start(f32[2,2,1,1]{1,0,3,2:T(2,128)} %constant.43) | copy-start | bytes 52
  155.2 66.5 %copy-start.13 = (bf16[2,256,2,128]{1,3,2,0:T(8,128)(2,1)S(1)}, bf16[2,256,2,128]{1,3,2,0:T(8,128)(2,1)}, u32[]{:S(2)}) copy-start(bf16[2,256,2,128]{1,3,2,0:T(8,128)(2,1)} %copy.195) | copy-start | bytes 786436
  155.2 44.6 %collective-permute-start.5 = (f32[3,2,128,128]{3,2,1,0:T(8,128)S(1)}, f32[3,2,128,128]{3,2,1,0:T(8,128)S(1)}, u32[]{:S(2)}, u32[]{:S(2)}) collective-permute-start(f32[3,2,128,128]{3,2,1,0:T(8,128)S(1)} %pad_maximum_fusion.9), channel_id=1, source_target_pairs={{0,256},{8,264},{16,272},{24,280},{32,288},{40,296},{48,304},{56,3... | collective-permute-start | bytes 1179656 | tf_op jit(solution)/shard_map/ppermute | solution.py:13
  166.7 54.1 %copy-start.15 = (f32[2,2,128,128]{2,3,1,0:T(8,128)S(1)}, f32[2,2,128,128]{2,3,1,0:T(8,128)}, u32[]{:S(2)}) copy-start(f32[2,2,128,128]{2,3,1,0:T(8,128)} %slice_bitcast_fusion) | copy-start | bytes 786436
  200.6 28.4 %collective-permute-start.6 = (f32[2,2,128,128]{3,2,1,0:T(8,128)S(1)}, f32[2,2,128,128]{3,2,1,0:T(8,128)S(1)}, u32[]{:S(2)}, u32[]{:S(2)}) collective-permute-start(f32[2,2,128,128]{3,2,1,0:T(8,128)S(1)} %pad_maximum_fusion.10), channel_id=1, source_target_pairs={{0,512},{8,520},{16,528},{24,536},{32,544},{40,552},{48,560},{56,5... | collective-permute-start | bytes 786440 | tf_op jit(solution)/shard_map/ppermute | solution.py:13
  229.0 2.0 copy-start.19
  232.2 8.6 %copy-start.20 = (f32[2,2,128,128]{3,2,1,0:T(8,128)S(1)}, f32[2,2,128,128]{3,2,1,0:T(8,128)}, u32[]{:S(2)}) copy-start(f32[2,2,128,128]{3,2,1,0:T(8,128)} %copy-done.19) | copy-start | bytes 786436
  232.9 9.1 %copy-start.23 = (f32[8,2,2,256]{3,0,1,2:T(8,128)S(1)}, f32[8,2,2,256]{3,0,1,2:T(8,128)}, u32[]{:S(2)}) copy-start(f32[8,2,2,256]{3,0,1,2:T(8,128)} %copy.246) | copy-start | bytes 98308
  232.9 9.1 %copy-start.24 = (bf16[2,1,2,128,128]{3,4,1,2,0:T(8,128)(2,1)S(1)}, bf16[2,1,2,128,128]{3,4,1,2,0:T(8,128)(2,1)}, u32[]{:S(2)}) copy-start(bf16[2,1,2,128,128]{3,4,1,2,0:T(8,128)(2,1)} %copy.179) | copy-start | bytes 393220
  242.0 1.0 copy-start.7
  243.4 1.1 copy-start.6
  (4 other events, 3.3 us)

commit v2 on v1

--- a/solution.py
+++ b/solution.py
@@ -2,7 +2,7 @@
 import jax.numpy as jnp
 import numpy as np
 from jax import lax
-from jax.sharding import PartitionSpec as P
+from jax.sharding import Mesh, PartitionSpec as P
 
 SPAN = 256
 
@@ -15,10 +15,11 @@
 
 def bucket_table(per_dev, local_levels):
     level_table = np.zeros((local_levels, per_dev, per_dev), np.float32)
-    for target in range(per_dev):
-        begin_at = target >> 1 << 1
-        end_at = target >> 0 << 0
-        level_table[0, target, begin_at:end_at] = 1.0
+    for level in range(local_levels):
+        for target in range(per_dev):
+            begin_at = target >> (level + 1) << (level + 1)
+            end_at = target >> level << level
+            level_table[level, target, begin_at:end_at] = 1.0
     return jnp.asarray(level_table)
 
 
@@ -32,7 +33,7 @@
     levels_all = level_weights.shape[0]
     per_dev = tokens_dev // SPAN
     local_levels = per_dev.bit_length() - 1
-    cross_levels = lax.axis_size("seq").bit_length() - 1
+    cross_levels = (lax.axis_size("z") * 8).bit_length() - 1
 
     def split_spans(matrix):
         return matrix.reshape(per_dev, SPAN, heads_local, head_size)
@@ -71,7 +72,9 @@
         "bhtu,bthr->buhr", attention, cotan_rows, preferred_element_type=jnp.float32
     )
     states = jnp.einsum("buhp,buhr->bhpr", key_rows, value_rows, preferred_element_type=jnp.float32)
-    seq_index = lax.axis_index("seq")
+    core_index = lax.axis_index("core")
+    x_index = lax.axis_index("x")
+    seq_index = (lax.axis_index("z") * 4 + x_index) * 2 + core_index
     upper_bits = (jnp.right_shift(seq_index, jnp.arange(cross_levels, dtype=jnp.int32)) % 2).astype(
         jnp.float32
     )
@@ -81,16 +84,66 @@
     )
     running = jnp.sum(states, axis=0)
     pending = jnp.sum(level_grads[:, local_levels:], axis=0) * upper_bits[:, None, None, None]
-    device_grad = jnp.zeros_like(running)
-    cross_list = []
-    for tree_bit in range(cross_levels):
+    packet = jnp.concatenate([running[None], pending], axis=0)
+    arrived = swapped(packet, "core", 0)
+    cross_first = arrived[0] * upper_bits[0]
+    grad_first = (1.0 - upper_bits[0]) * arrived[1]
+    running = lax.dynamic_index_in_dim(running + arrived[0], core_index, 0, keepdims=False)
+    pending = lax.dynamic_index_in_dim(pending[1:] + arrived[2:], core_index, 1, keepdims=False)
+    packet = jnp.concatenate([running[None], pending], axis=0)
+    arrived = swapped(packet, "x", 0)
+    cross_x1 = arrived[0] * upper_bits[1]
+    grad_x1 = (1.0 - upper_bits[1]) * arrived[1]
+
+    def halved(matrix):
+        shaped = matrix.reshape(matrix.shape[:-2] + (2, 2, head_size // 4, head_size))
+        return lax.dynamic_index_in_dim(shaped, x_index % 2, shaped.ndim - 3, keepdims=False)
+
+    running = halved(running + arrived[0])
+    pending = halved(pending[1:] + arrived[2:])
+    packet = jnp.concatenate([running[None], pending], axis=0)
+    arrived = swapped(packet, "x", 1)
+    cross_x2 = arrived[0] * upper_bits[2]
+    grad_x2 = (1.0 - upper_bits[2]) * arrived[1]
+
+    def quartered(matrix):
+        return lax.dynamic_index_in_dim(matrix, x_index // 2, matrix.ndim - 3, keepdims=False)
+
+    running = quartered(running + arrived[0])
+    pending = quartered(pending[1:] + arrived[2:])
+    grad_z = jnp.zeros_like(running)
+    cross_z = []
+    for z_bit in range(cross_levels - 3):
+        tree_bit = z_bit + 3
         packet = jnp.concatenate([running[None], pending], axis=0)
-        arrived = swapped(packet, "seq", tree_bit)
-        partner = arrived[0]
-        cross_list.append(partner * upper_bits[tree_bit])
-        running = running + partner
-        device_grad = device_grad + (1.0 - upper_bits[tree_bit]) * arrived[1]
+        arrived = swapped(packet, "z", z_bit)
+        cross_z.append(arrived[0] * upper_bits[tree_bit])
+        grad_z = grad_z + (1.0 - upper_bits[tree_bit]) * arrived[1]
+        running = running + arrived[0]
         pending = pending[1:] + arrived[2:]
+
+    quarter = head_size // 4
+    pieces = jnp.concatenate(
+        [
+            jnp.stack([cross_x1, grad_x1]).reshape(8, quarter, head_size),
+            jnp.stack([cross_x2, grad_x2]).reshape(4, quarter, head_size),
+            jnp.stack(cross_z + [grad_z]),
+        ]
+    )
+    gathered = lax.all_gather(pieces, ("x", "core")).reshape((4, 2) + pieces.shape)
+    own = lax.dynamic_index_in_dim(gathered, x_index, 0, keepdims=False)
+    level_one = own[:, :8].reshape(2, 2, head_size, head_size)
+    pair_first = lax.dynamic_index_in_dim(gathered, x_index - x_index % 2, 0, keepdims=False)
+    pair_second = lax.dynamic_index_in_dim(gathered, x_index - x_index % 2 + 1, 0, keepdims=False)
+    level_two = jnp.stack(
+        [pair_first[:, 8:12].reshape(2, 2, 2, quarter, head_size), pair_second[:, 8:12].reshape(2, 2, 2, quarter, head_size)],
+        axis=3,
+    ).reshape(2, 2, head_size, head_size)
+    z_levels = gathered[:, :, 12:].transpose(1, 2, 0, 3, 4).reshape(2, -1, head_size, head_size)
+    device_grad = grad_first + level_one[:, 1] + level_two[:, 1] + z_levels[:, -1]
+    cross_list = [cross_first, level_one[:, 0], level_two[:, 0]] + [
+        z_levels[:, level] for level in range(cross_levels - 3)
+    ]
     level_table = bucket_table(per_dev, local_levels)
     local_buckets = jnp.einsum(
         "mji,ihpr->jmhpr", level_table, states, precision=lax.Precision.HIGHEST
@@ -132,17 +185,20 @@
 
 
 def solution(mesh):
+    seq_size, head_count = mesh.devices.shape
+    split_mesh = Mesh(mesh.devices.reshape(seq_size // 8, 4, 2, head_count), ("z", "x", "core", "head"))
+    seq_axes = ("z", "x", "core")
     placed = (
-        P(("seq", "head"), None),
-        P(("seq", "head"), None),
-        P(("seq", "head"), None),
-        P(("seq", "head"), None),
-        P(None, "head", "seq"),
+        P(seq_axes + ("head",), None),
+        P(seq_axes + ("head",), None),
+        P(seq_axes + ("head",), None),
+        P(seq_axes + ("head",), None),
+        P(None, "head", seq_axes),
     )
     return jax.shard_map(
         body,
-        mesh=mesh,
+        mesh=split_mesh,
         in_specs=placed,
-        out_specs=(P("seq", "head"), P("seq", "head"), P("seq", "head"), P("seq", "head")),
+        out_specs=(P(seq_axes, "head"),) * 4,
         check_vma=False,
     )

time: 248 us -> 214 us (0.86)
  waiting for transfers between devices: 119 us -> 63.1 us
  local copies, waits for them, and re-layouts: 23.4 us -> 38.8 us
  between operations: 5.66 us -> 19.3 us
  starting transfers between devices: 69.4 us -> 64 us
  other arithmetic: 17.1 us -> 13.5 us
    ppermute x7, waiting for transfers between devices: 103 us -> 20.6 us  [swapped(): return lax.ppermute(value, axis, pairs)]
    all_gather x0 -> x1, waiting for transfers between devices: none -> 26.6 us  [body(): lax.all_gather(pieces, ('x', 'core')).reshape((4, 2) + pieces.shape)]
    unnamed x58 -> x56, local copies, waits for them, and re-layouts: 6.89 us -> 15.6 us
    unnamed x5 -> x1, other arithmetic: 7.68 us -> 0.61 us
    ppermute x7, starting transfers between devices: 61.7 us -> 56.3 us  [swapped(): return lax.ppermute(value, axis, pairs)]
    add x6 -> x9, other arithmetic: 1.07 us -> 5.33 us  [the longest x3 1.87 us: body(): running = running + arrived[0]]
    another operation x3 -> x6, local copies, waits for them, and re-layouts: 1.14 us -> 5.4 us
    squeeze x0 -> x3, local copies, waits for them, and re-layouts: none -> 2.58 us  [the longest x1 1.58 us: body(): lax.dynamic_index_in_dim(gathered, x_index - x_index % 2, 0, keepdims=False)]
  transfers between devices with their start and end apart: 8 -> 9, of which waited for: 8 -> 8; matrix products, arithmetic and copies ran while one was open for 5% -> 5% of each run, Pallas kernels for 0% -> 0%
where the time goes in v2:
time: 214 us; the launch traced here: 212 us
  starting transfers between devices  64 us (30%)
  waiting for transfers between devices  63.1 us (29%)
  local copies, waits for them, and re-layouts  38.8 us (18%)
  between operations  19.3 us (9%)
  matrix products  13.6 us (6%)
  other arithmetic  13.5 us (6%)
    ppermute x7, starting transfers between devices, swapped(): return lax.ppermute(value, axis, pairs)  56.3 us
    all_gather x1, waiting for transfers between devices, body(): lax.all_gather(pieces, ('x', 'core')).reshape((4, 2) + pieces.shape)  26.6 us
    ppermute x7, waiting for transfers between devices, swapped(): return lax.ppermute(value, axis, pairs)  20.6 us
    all_to_all x1, waiting for transfers between devices, body(): lax.all_to_all(stacked, 'head', split_axis=2, concat_axis=0, tiled=True)  15.9 us
    unnamed x56, local copies, waits for them, and re-layouts  15.6 us
    all_to_all x1, starting transfers between devices, body(): lax.all_to_all(stacked, 'head', split_axis=2, concat_axis=0, tiled=True)  7.65 us
  transfers between devices with their start and end apart: 9, of which 8 were waited for; matrix products, arithmetic and copies ran while one was open for 5% of the time, Pallas kernels for 0%

profile of v2, /device:TPU:1, one launch (start us, length us, event | category | flops | bytes accessed | tf_op | source)
XLA Modules:
  0.0 212.3 jit_solution(158334275471138655)
XLA Ops:
  8.5 1.4 copy.252
  9.9 2.6 %reshape.104 = bf16[8,2,32768]{2,1,0:T(2,128)(2,1)} reshape(bf16[2048,4,64]{2,1,0:T(4,128)(2,1)S(1)} %bitcast.207) | data formatting | bytes 2097152
  12.6 7.7 %all-to-all-start = ((bf16[8,2,32768]{2,1,0:T(2,128)(2,1)}), bf16[8,2,32768]{2,1,0:T(2,128)(2,1)S(1)}, u32[]{:S(2)}, u32[]{:S(2)}) async-start(bf16[8,2,32768]{2,1,0:T(2,128)(2,1)} %reshape.104), calls=%async_computation | async-start | bytes 2097152 | tf_op jit(solution)/shard_map/all_to_all | solution.py:28
  21.1 15.9 %all-to-all-done = bf16[8,2,32768]{2,1,0:T(2,128)(2,1)S(1)} async-done(((bf16[8,2,32768]{2,1,0:T(2,128)(2,1)}), bf16[8,2,32768]{2,1,0:T(2,128)(2,1)S(1)}, u32[]{:S(2)}, u32[]{:S(2)}) %all-to-all-start) | async-done | bytes 1048608 | tf_op jit(solution)/shard_map/all_to_all | solution.py:28
  37.0 1.4 reshape.105
  46.9 2.1 fusion.52
  50.7 15.1 %collective-permute-start = (f32[8,2,128,128]{3,2,0,1:T(8,128)}, f32[8,2,128,128]{3,2,0,1:T(8,128)}, u32[]{:S(2)}, u32[]{:S(2)}) collective-permute-start(f32[8,2,128,128]{3,2,0,1:T(8,128)} %pad_maximum_fusion.1), channel_id=1, source_target_pairs={{0,8},{8,0},{1,9},{9,1},{2,10},{10,2},{3,11},{11,3},{4,12},{12,4},... | collective-permute-start | bytes 3145736 | tf_op jit(solution)/shard_map/ppermute | solution.py:13
  65.8 2.6 %collective-permute-done = f32[8,2,128,128]{3,2,0,1:T(8,128)} collective-permute-done((f32[8,2,128,128]{3,2,0,1:T(8,128)}, f32[8,2,128,128]{3,2,0,1:T(8,128)}, u32[]{:S(2)}, u32[]{:S(2)}) %collective-permute-start) | collective-permute-done | bytes 1048608 | tf_op jit(solution)/shard_map/ppermute | solution.py:13
  71.5 2.8 %collective-permute-start.1 = (f32[7,128,128]{2,1,0:T(8,128)S(1)}, f32[7,128,128]{2,1,0:T(8,128)}, u32[]{:S(2)}, u32[]{:S(2)}) collective-permute-start(f32[7,128,128]{2,1,0:T(8,128)S(1)} %pad_maximum_fusion.5), channel_id=1, source_target_pairs={{0,16},{16,0},{32,48},{48,32},{1,17},{17,1},{33,49},{49,33},{2,18}... | collective-permute-start | bytes 1376264 | tf_op jit(solution)/shard_map/ppermute | solution.py:13
  76.3 8.9 %collective-permute-done.1 = f32[7,128,128]{2,1,0:T(8,128)} collective-permute-done((f32[7,128,128]{2,1,0:T(8,128)S(1)}, f32[7,128,128]{2,1,0:T(8,128)}, u32[]{:S(2)}, u32[]{:S(2)}) %collective-permute-start.1) | collective-permute-done | bytes 458784 | tf_op jit(solution)/shard_map/ppermute | solution.py:13
  85.3 1.5 slice_add_fusion.1
  87.9 4.5 %collective-permute-start.2 = (f32[6,2,32,128]{3,2,0,1:T(8,128)S(1)}, f32[6,2,32,128]{3,2,0,1:T(8,128)S(1)}, u32[]{:S(2)}, u32[]{:S(2)}) collective-permute-start(f32[6,2,32,128]{3,2,0,1:T(8,128)S(1)} %pad_maximum_fusion.7), channel_id=1, source_target_pairs={{0,32},{16,48},{32,0},{48,16},{1,33},{17,49},{33,1},{49,17},{2,34}... | collective-permute-start | bytes 589832 | tf_op jit(solution)/shard_map/ppermute | solution.py:13
  92.5 4.2 %collective-permute-done.2 = f32[6,2,32,128]{3,2,0,1:T(8,128)S(1)} collective-permute-done((f32[6,2,32,128]{3,2,0,1:T(8,128)S(1)}, f32[6,2,32,128]{3,2,0,1:T(8,128)S(1)}, u32[]{:S(2)}, u32[]{:S(2)}) %collective-permute-start.2) | collective-permute-done | bytes 196640 | tf_op jit(solution)/shard_map/ppermute | solution.py:13
  97.3 3.7 %collective-permute-start.3 = (f32[5,32,128]{2,1,0:T(8,128)S(1)}, f32[5,32,128]{2,1,0:T(8,128)S(1)}, u32[]{:S(2)}, u32[]{:S(2)}) collective-permute-start(f32[5,32,128]{2,1,0:T(8,128)S(1)} %pad_maximum_fusion.9), channel_id=1, source_target_pairs={{0,64},{64,0},{128,192},{192,128},{256,320},{320,256},{384,448},{4... | collective-permute-start | bytes 245768 | tf_op jit(solution)/shard_map/ppermute | solution.py:13
  101.1 1.8 collective-permute-done.3
  103.6 5.8 %collective-permute-start.4 = (f32[4,32,128]{2,1,0:T(8,128)S(1)}, f32[4,32,128]{2,1,0:T(8,128)S(1)}, u32[]{:S(2)}, u32[]{:S(2)}) collective-permute-start(f32[4,32,128]{2,1,0:T(8,128)S(1)} %pad_maximum_fusion.11), channel_id=1, source_target_pairs={{0,128},{64,192},{128,0},{192,64},{256,384},{320,448},{384,256},{4... | collective-permute-start | bytes 196616 | tf_op jit(solution)/shard_map/ppermute | solution.py:13
  109.4 1.6 collective-permute-done.4
  111.7 10.6 %collective-permute-start.5 = (f32[3,32,128]{2,1,0:T(8,128)S(1)}, f32[3,32,128]{2,1,0:T(8,128)S(1)}, u32[]{:S(2)}, u32[]{:S(2)}) collective-permute-start(f32[3,32,128]{2,1,0:T(8,128)S(1)} %pad_maximum_fusion.12), channel_id=1, source_target_pairs={{0,256},{64,320},{128,384},{192,448},{256,0},{320,64},{384,128},{4... | collective-permute-start | bytes 147464 | tf_op jit(solution)/shard_map/ppermute | solution.py:13
  122.3 1.5 collective-permute-done.5
  124.4 13.7 %collective-permute-start.6 = (f32[2,32,128]{2,1,0:T(8,128)S(1)}, f32[2,32,128]{2,1,0:T(8,128)S(1)}, u32[]{:S(2)}, u32[]{:S(2)}) collective-permute-start(f32[2,32,128]{2,1,0:T(8,128)S(1)} %pad_maximum_fusion.13), channel_id=1, source_target_pairs={{0,512},{64,576},{128,640},{192,704},{256,768},{320,832},{384,896}... | collective-permute-start | bytes 98312 | tf_op jit(solution)/shard_map/ppermute | solution.py:13
  145.7 1.8 copy.290
  147.5 2.1 fusion.19
  153.2 26.6 %all-gather.3.cloned.1.call-done = f32[136,32,128]{2,1,0:T(8,128)} async-done(((f32[17,32,128]{2,1,0:T(8,128)}), f32[136,32,128]{2,1,0:T(8,128)}) %all-gather.3.cloned.1.call-update) | async-done | bytes 2228240 | tf_op jit(solution)/shard_map/all_gather | solution.py:133
  181.0 1.6 dynamic-slice_bitcast_fusion.1
  183.7 2.2 %fusion.33 = (f32[2,128,128]{2,1,0:T(8,128)S(1)}, bf16[7,2,128,128]{3,2,0,1:T(8,128)(2,1)}) fusion(f32[2,5,128,128]{3,2,1,0:T(8,128)S(1)} %bitcast.216, f32[2,2,128,128]{3,2,1,0:T(8,128)S(1)} %bitcast.226, f32[2,2,128,128]{3,2,1,0:T(8,128)S(1)} %bitcast.228, f32[8,2,128,128]{3,2,0,1:T(8,128)} %collective-permute-done, f32[]{:T(128)S(6)} %sub.38, f32[]{:T(128)} %bitcast.20), kind=kLoop, calls=%fused_computation.66 | loop fusion | flops 163839 | bytes 917512 | tf_op jit(solution)/shard_map/add | solution.py:168
  189.1 1.5 fusion.41
  190.6 1.5 fusion.40
  192.1 1.5 fusion.39
  193.7 1.5 fusion.38
  195.2 1.5 fusion.37
  196.7 1.5 fusion.36
  201.2 2.0 fusion
  (133 shorter events, 38.0 us)
Async XLA Ops:
  9.9 10.4 %copy-start.20 = (s32[9,2,512]{2,1,0:T(2,128)S(1)}, s32[9,2,512]{2,1,0:T(2,128)}, u32[]{:S(2)}) copy-start(s32[9,2,512]{2,1,0:T(2,128)} %param.11) | copy-start | bytes 110596
  9.9 10.4 %copy-start.21 = (f32[9]{0:T(128)S(1)}, f32[9]{0:T(128)}, u32[]{:S(2)}) copy-start(f32[9]{0:T(128)} %constant.113) | copy-start | bytes 112
  12.6 24.4 %all-to-all-start = ((bf16[8,2,32768]{2,1,0:T(2,128)(2,1)}), bf16[8,2,32768]{2,1,0:T(2,128)(2,1)S(1)}, u32[]{:S(2)}, u32[]{:S(2)}) async-start(bf16[8,2,32768]{2,1,0:T(2,128)(2,1)} %reshape.104), calls=%async_computation | async-start | bytes 2097152 | tf_op jit(solution)/shard_map/all_to_all | solution.py:28
  20.2 159.7 %all-gather.3.cloned.1.call-start = ((), (), s32[]{:S(2)}) async-start(), calls=%async_computation.1 | async-start | bytes 2506752 | tf_op jit(solution)/shard_map/all_gather | solution.py:133
  21.0 19.8 %copy-start.16 = (f32[8,2,2,256]{3,0,1,2:T(8,128)}, f32[8,2,2,256]{3,0,1,2:T(8,128)S(1)}, u32[]{:S(2)}) copy-start(f32[8,2,2,256]{3,0,1,2:T(8,128)S(1)} %copy.362) | copy-start | bytes 98308
  40.8 0.7 copy-start.1
  42.2 1.4 copy-start.8
  43.7 0.9 copy-start.4
  46.9 18.9 %copy-start = (f32[7,2,128,128]{3,2,0,1:T(8,128)}, f32[7,2,128,128]{3,2,0,1:T(8,128)S(1)}, u32[]{:S(2)}) copy-start(f32[7,2,128,128]{3,2,0,1:T(8,128)S(1)} %broadcast_multiply_fusion) | copy-start | bytes 2752516
  49.0 0.6 copy-start.10
  50.7 17.7 %collective-permute-start = (f32[8,2,128,128]{3,2,0,1:T(8,128)}, f32[8,2,128,128]{3,2,0,1:T(8,128)}, u32[]{:S(2)}, u32[]{:S(2)}) collective-permute-start(f32[8,2,128,128]{3,2,0,1:T(8,128)} %pad_maximum_fusion.1), channel_id=1, source_target_pairs={{0,8},{8,0},{1,9},{9,1},{2,10},{10,2},{3,11},{11,3},{4,12},{12,4},... | collective-permute-start | bytes 3145736 | tf_op jit(solution)/shard_map/ppermute | solution.py:13
  68.4 3.0 %slice-start = ((f32[7,2,128,128]{3,2,0,1:T(8,128)}), f32[6,2,128,128]{3,2,0,1:T(8,128)S(1)}, s32[]{:S(2)}) async-start(f32[7,2,128,128]{3,2,0,1:T(8,128)} %copy-done), calls=%async_computation.2 | async-start | bytes 1572864 | tf_op jit(solution)/shard_map/slice | solution.py:92
  71.5 13.7 %collective-permute-start.1 = (f32[7,128,128]{2,1,0:T(8,128)S(1)}, f32[7,128,128]{2,1,0:T(8,128)}, u32[]{:S(2)}, u32[]{:S(2)}) collective-permute-start(f32[7,128,128]{2,1,0:T(8,128)S(1)} %pad_maximum_fusion.5), channel_id=1, source_target_pairs={{0,16},{16,0},{32,48},{48,32},{1,17},{17,1},{33,49},{49,33},{2,18}... | collective-permute-start | bytes 1376264 | tf_op jit(solution)/shard_map/ppermute | solution.py:13
  87.9 56.3 %copy-start.2 = (bf16[2,256,2,128]{3,2,1,0:T(2,128)(2,1)S(1)}, bf16[2,256,2,128]{3,2,1,0:T(2,128)(2,1)}, u32[]{:S(2)}) copy-start(bf16[2,256,2,128]{3,2,1,0:T(2,128)(2,1)} %copy-done.1) | copy-start | bytes 786436
  87.9 8.7 %collective-permute-start.2 = (f32[6,2,32,128]{3,2,0,1:T(8,128)S(1)}, f32[6,2,32,128]{3,2,0,1:T(8,128)S(1)}, u32[]{:S(2)}, u32[]{:S(2)}) collective-permute-start(f32[6,2,32,128]{3,2,0,1:T(8,128)S(1)} %pad_maximum_fusion.7), channel_id=1, source_target_pairs={{0,32},{16,48},{32,0},{48,16},{1,33},{17,49},{33,1},{49,17},{2,34}... | collective-permute-start | bytes 589832 | tf_op jit(solution)/shard_map/ppermute | solution.py:13
  96.6 50.9 %copy-start.22 = (f32[2,2,1,1]{1,0,3,2:T(2,128)S(1)}, f32[2,2,1,1]{1,0,3,2:T(2,128)}, u32[]{:S(2)}) copy-start(f32[2,2,1,1]{1,0,3,2:T(2,128)} %constant.115) | copy-start | bytes 52
  97.3 5.5 %collective-permute-start.3 = (f32[5,32,128]{2,1,0:T(8,128)S(1)}, f32[5,32,128]{2,1,0:T(8,128)S(1)}, u32[]{:S(2)}, u32[]{:S(2)}) collective-permute-start(f32[5,32,128]{2,1,0:T(8,128)S(1)} %pad_maximum_fusion.9), channel_id=1, source_target_pairs={{0,64},{64,0},{128,192},{192,128},{256,320},{320,256},{384,448},{4... | collective-permute-start | bytes 245768 | tf_op jit(solution)/shard_map/ppermute | solution.py:13
  103.6 7.5 %collective-permute-start.4 = (f32[4,32,128]{2,1,0:T(8,128)S(1)}, f32[4,32,128]{2,1,0:T(8,128)S(1)}, u32[]{:S(2)}, u32[]{:S(2)}) collective-permute-start(f32[4,32,128]{2,1,0:T(8,128)S(1)} %pad_maximum_fusion.11), channel_id=1, source_target_pairs={{0,128},{64,192},{128,0},{192,64},{256,384},{320,448},{384,256},{4... | collective-permute-start | bytes 196616 | tf_op jit(solution)/shard_map/ppermute | solution.py:13
  111.7 12.1 %collective-permute-start.5 = (f32[3,32,128]{2,1,0:T(8,128)S(1)}, f32[3,32,128]{2,1,0:T(8,128)S(1)}, u32[]{:S(2)}, u32[]{:S(2)}) collective-permute-start(f32[3,32,128]{2,1,0:T(8,128)S(1)} %pad_maximum_fusion.12), channel_id=1, source_target_pairs={{0,256},{64,320},{128,384},{192,448},{256,0},{320,64},{384,128},{4... | collective-permute-start | bytes 147464 | tf_op jit(solution)/shard_map/ppermute | solution.py:13
  124.4 16.2 %collective-permute-start.6 = (f32[2,32,128]{2,1,0:T(8,128)S(1)}, f32[2,32,128]{2,1,0:T(8,128)S(1)}, u32[]{:S(2)}, u32[]{:S(2)}) collective-permute-start(f32[2,32,128]{2,1,0:T(8,128)S(1)} %pad_maximum_fusion.13), channel_id=1, source_target_pairs={{0,512},{64,576},{128,640},{192,704},{256,768},{320,832},{384,896}... | collective-permute-start | bytes 98312 | tf_op jit(solution)/shard_map/ppermute | solution.py:13
  141.2 0.7 copy-start.13
  142.6 8.9 %copy-start.5 = (bf16[2,256,2,128]{3,2,1,0:T(2,128)(2,1)S(1)}, bf16[2,256,2,128]{3,2,1,0:T(2,128)(2,1)}, u32[]{:S(2)}) copy-start(bf16[2,256,2,128]{3,2,1,0:T(2,128)(2,1)} %copy-done.4) | copy-start | bytes 786436
  145.7 5.9 %copy-start.7 = (bf16[2,256,2,128]{1,3,2,0:T(8,128)(2,1)S(1)}, bf16[2,256,2,128]{1,3,2,0:T(8,128)(2,1)}, u32[]{:S(2)}) copy-start(bf16[2,256,2,128]{1,3,2,0:T(8,128)(2,1)} %copy.289) | copy-start | bytes 786436
  145.7 5.9 %copy-start.19 = (pred[256,256]{1,0:T(8,128)(4,1)S(1)}, pred[256,256]{1,0:T(8,128)(4,1)}, u32[]{:S(2)}) copy-start(pred[256,256]{1,0:T(8,128)(4,1)} %iota_compare_fusion) | copy-start | bytes 196612
  182.6 3.4 %copy-start.14 = (f32[2,2,128,128]{3,0,2,1:T(2,128)S(1)}, f32[2,2,128,128]{3,0,2,1:T(2,128)}, u32[]{:S(2)}) copy-start(f32[2,2,128,128]{3,0,2,1:T(2,128)} %copy.290) | copy-start | bytes 786436
  182.7 4.3 %copy-start.11 = (f32[2,2,2,2,32,128]{5,4,3,2,1,0:T(8,128)}, f32[2,2,2,2,32,128]{5,4,3,2,1,0:T(8,128)S(1)}, u32[]{:S(2)}) copy-start(f32[2,2,2,2,32,128]{5,4,3,2,1,0:T(8,128)S(1)} %copy.271) | copy-start | bytes 786436
  182.7 4.4 %copy-start.12 = (f32[2,8,32,128]{3,2,1,0:T(8,128)}, f32[2,8,32,128]{3,2,1,0:T(8,128)S(1)}, u32[]{:S(2)}) copy-start(f32[2,8,32,128]{3,2,1,0:T(8,128)S(1)} %slice.278) | copy-start | bytes 786436
  182.8 0.9 copy-start.6
  188.7 11.1 %copy-start.17 = (f32[8,2,2,256]{3,0,1,2:T(8,128)S(1)}, f32[8,2,2,256]{3,0,1,2:T(8,128)}, u32[]{:S(2)}) copy-start(f32[8,2,2,256]{3,0,1,2:T(8,128)} %copy-done.16) | copy-start | bytes 98308
  188.7 11.1 %copy-start.18 = (bf16[2,1,2,128,128]{3,4,1,2,0:T(8,128)(2,1)S(1)}, bf16[2,1,2,128,128]{3,4,1,2,0:T(8,128)(2,1)}, u32[]{:S(2)}) copy-start(bf16[2,1,2,128,128]{3,4,1,2,0:T(8,128)(2,1)} %copy.279) | copy-start | bytes 393220
  199.8 0.9 copy-start.9
  201.1 2.2 %copy-start.3 = (bf16[2,256,2,128]{1,3,2,0:T(8,128)(2,1)S(1)}, bf16[2,256,2,128]{1,3,2,0:T(8,128)(2,1)}, u32[]{:S(2)}) copy-start(bf16[2,256,2,128]{1,3,2,0:T(8,128)(2,1)} %copy.260) | copy-start | bytes 786436
  (1 other events, 0.6 us)
Sparse Core Ops, SparseCore 0:
  142.1 37.7 all-gather.2

commit v3 on v2

--- a/solution.py
+++ b/solution.py
@@ -21,6 +21,16 @@
             end_at = target >> level << level
             level_table[level, target, begin_at:end_at] = 1.0
     return jnp.asarray(level_table)
+
+
+def z_table(groups):
+    levels = groups.bit_length() - 1
+    table = np.zeros((levels, groups, groups), np.float32)
+    for level in range(levels):
+        for target in range(groups):
+            if target >> level & 1:
+                table[level, target, target >> (level + 1) << (level + 1) : target >> level << level] = 1.0
+    return jnp.asarray(table)
 
 
 def body(queries, key_vectors, value_vectors, grad_output, level_weights):
@@ -111,37 +121,28 @@
 
     running = quartered(running + arrived[0])
     pending = quartered(pending[1:] + arrived[2:])
-    grad_z = jnp.zeros_like(running)
-    cross_z = []
-    for z_bit in range(cross_levels - 3):
-        tree_bit = z_bit + 3
-        packet = jnp.concatenate([running[None], pending], axis=0)
-        arrived = swapped(packet, "z", z_bit)
-        cross_z.append(arrived[0] * upper_bits[tree_bit])
-        grad_z = grad_z + (1.0 - upper_bits[tree_bit]) * arrived[1]
-        running = running + arrived[0]
-        pending = pending[1:] + arrived[2:]
-
-    quarter = head_size // 4
-    pieces = jnp.concatenate(
-        [
-            jnp.stack([cross_x1, grad_x1]).reshape(8, quarter, head_size),
-            jnp.stack([cross_x2, grad_x2]).reshape(4, quarter, head_size),
-            jnp.stack(cross_z + [grad_z]),
-        ]
-    )
+    z_rows = lax.dynamic_index_in_dim(z_table(lax.axis_size("z")), lax.axis_index("z"), 1, keepdims=False)
+    group_sums = lax.all_gather(running, "z")
+    cross_z = jnp.einsum("jb,bpr->jpr", z_rows, group_sums, precision=lax.Precision.HIGHEST)
+    contributions = jnp.einsum("jb,jpr->bpr", z_rows, pending, precision=lax.Precision.HIGHEST)
+    grad_z = lax.psum_scatter(contributions, "z", scatter_dimension=0, tiled=False)
+    own_half = jnp.stack([cross_x2, grad_x2])
+    other_half = swapped(own_half, "x", 0)
+    even_first = x_index % 2 == 0
+    level_two = jnp.stack(
+        [jnp.where(even_first, own_half, other_half), jnp.where(even_first, other_half, own_half)], axis=2
+    ).reshape(2, head_size, head_size)
+    own_levels = jnp.concatenate([jnp.stack([cross_x1, grad_x1]), level_two])
+    other_levels = swapped(own_levels, "core", 0)
+    core_first = core_index == 0
+    near_levels = jnp.stack(
+        [jnp.where(core_first, own_levels, other_levels), jnp.where(core_first, other_levels, own_levels)]
+    )
+    pieces = jnp.concatenate([cross_z, grad_z[None]])
     gathered = lax.all_gather(pieces, ("x", "core")).reshape((4, 2) + pieces.shape)
-    own = lax.dynamic_index_in_dim(gathered, x_index, 0, keepdims=False)
-    level_one = own[:, :8].reshape(2, 2, head_size, head_size)
-    pair_first = lax.dynamic_index_in_dim(gathered, x_index - x_index % 2, 0, keepdims=False)
-    pair_second = lax.dynamic_index_in_dim(gathered, x_index - x_index % 2 + 1, 0, keepdims=False)
-    level_two = jnp.stack(
-        [pair_first[:, 8:12].reshape(2, 2, 2, quarter, head_size), pair_second[:, 8:12].reshape(2, 2, 2, quarter, head_size)],
-        axis=3,
-    ).reshape(2, 2, head_size, head_size)
-    z_levels = gathered[:, :, 12:].transpose(1, 2, 0, 3, 4).reshape(2, -1, head_size, head_size)
-    device_grad = grad_first + level_one[:, 1] + level_two[:, 1] + z_levels[:, -1]
-    cross_list = [cross_first, level_one[:, 0], level_two[:, 0]] + [
+    z_levels = gathered.transpose(1, 2, 0, 3, 4).reshape(2, -1, head_size, head_size)
+    device_grad = grad_first + near_levels[:, 1] + near_levels[:, 3] + z_levels[:, -1]
+    cross_list = [cross_first, near_levels[:, 0], near_levels[:, 2]] + [
         z_levels[:, level] for level in range(cross_levels - 3)
     ]
     level_table = bucket_table(per_dev, local_levels)

time: 214 us -> 225 us (1.051)
  blocking collectives: 0 us -> 61.5 us
  starting transfers between devices: 64 us -> 37.5 us
  waiting for transfers between devices: 63.1 us -> 50 us
  local copies, waits for them, and re-layouts: 38.8 us -> 31.9 us
  other arithmetic: 13.5 us -> 10.3 us
  between operations: 19.3 us -> 16.6 us
  matrix products: 13.6 us -> 15.9 us
    all_gather x0 -> x2, blocking collectives: none -> 61.5 us  [the longest x1 36.4 us: body(): group_sums = lax.all_gather(running, 'z')]
    all_gather x1 -> x0, waiting for transfers between devices: 26.6 us -> none  [body(): lax.all_gather(pieces, ('x', 'core')).reshape((4, 2) + pieces.shape)]
    ppermute x7 -> x5, starting transfers between devices: 56.3 us -> 29.9 us  [swapped(): return lax.ppermute(value, axis, pairs)]
    reduce_scatter x0 -> x1, waiting for transfers between devices: none -> 21.5 us  [body(): lax.psum_scatter(contributions, 'z', scatter_dimension=0, tiled=False)]
    ppermute x7 -> x5, waiting for transfers between devices: 20.6 us -> 13.1 us  [swapped(): return lax.ppermute(value, axis, pairs)]
    unnamed x56 -> x53, local copies, waits for them, and re-layouts: 15.6 us -> 10.9 us
    add x7 -> x0, other arithmetic: 3.42 us -> none  [the longest x3 1.87 us: body(): running = running + arrived[0]]
    dot_general x0 -> x2, matrix products: none -> 2.85 us  [the longest x1 1.7 us: body(): jnp.einsum('jb,bpr->jpr', z_rows, group_sums, precision=lax.Precision.HIG...]
  transfers between devices with their start and end apart: 9 -> 7, of which waited for: 8 -> 5; matrix products, arithmetic and copies ran while one was open for 5% -> 8% of each run, Pallas kernels for 0% -> 0%
where the time goes in v3:
time: 225 us; the launch traced here: 224 us
  blocking collectives  61.5 us (27%)
  waiting for transfers between devices  50 us (22%)
  starting transfers between devices  37.5 us (17%)
  local copies, waits for them, and re-layouts  31.9 us (14%)
  between operations  16.6 us (7%)
  matrix products  15.9 us (7%)
  other arithmetic  10.3 us (5%)
    all_gather x1, blocking collectives, body(): group_sums = lax.all_gather(running, 'z')  36.4 us
    ppermute x5, starting transfers between devices, swapped(): return lax.ppermute(value, axis, pairs)  29.9 us
    all_gather x1, blocking collectives, body(): lax.all_gather(pieces, ('x', 'core')).reshape((4, 2) + pieces.shape)  25.1 us
    reduce_scatter x1, waiting for transfers between devices, body(): lax.psum_scatter(contributions, 'z', scatter_dimension=0, tiled=False)  21.5 us
    all_to_all x1, waiting for transfers between devices, body(): lax.all_to_all(stacked, 'head', split_axis=2, concat_axis=0, tiled=True)  15.4 us
    ppermute x5, waiting for transfers between devices, swapped(): return lax.ppermute(value, axis, pairs)  13.1 us
    unnamed x53, local copies, waits for them, and re-layouts  10.9 us
    all_to_all x1, starting transfers between devices, body(): lax.all_to_all(stacked, 'head', split_axis=2, concat_axis=0, tiled=True)  7.65 us
  transfers between devices with their start and end apart: 7, of which 5 were waited for; matrix products, arithmetic and copies ran while one was open for 8% of the time, Pallas kernels for 0%

profile of v3, /device:TPU:1, one launch (start us, length us, event | category | flops | bytes accessed | tf_op | source)
XLA Modules:
  0.0 223.8 jit_solution(7736242482934969059)
XLA Ops:
  7.2 1.3 pad_maximum_fusion
  8.5 1.4 copy.242
  9.9 2.7 %reshape.92 = bf16[8,2,32768]{2,1,0:T(2,128)(2,1)} reshape(bf16[2048,4,64]{2,1,0:T(4,128)(2,1)S(1)} %bitcast.204) | data formatting | bytes 2097152
  12.6 7.7 %all-to-all-start = ((bf16[8,2,32768]{2,1,0:T(2,128)(2,1)}), bf16[8,2,32768]{2,1,0:T(2,128)(2,1)S(1)}, u32[]{:S(2)}, u32[]{:S(2)}) async-start(bf16[8,2,32768]{2,1,0:T(2,128)(2,1)} %reshape.92), calls=%async_computation | async-start | bytes 2097152 | tf_op jit(solution)/shard_map/all_to_all | solution.py:38
  21.7 15.4 %all-to-all-done = bf16[8,2,32768]{2,1,0:T(2,128)(2,1)S(1)} async-done(((bf16[8,2,32768]{2,1,0:T(2,128)(2,1)}), bf16[8,2,32768]{2,1,0:T(2,128)(2,1)S(1)}, u32[]{:S(2)}, u32[]{:S(2)}) %all-to-all-start) | async-done | bytes 1048608 | tf_op jit(solution)/shard_map/all_to_all | solution.py:38
  37.0 1.4 reshape.93
  38.5 1.2 copy.300
  42.5 1.2 copy.255
  43.7 1.9 fusion.64
  45.6 1.4 broadcast_multiply_fusion
  48.1 15.1 %collective-permute-start = (f32[8,2,128,128]{3,2,0,1:T(8,128)}, f32[8,2,128,128]{3,2,0,1:T(8,128)}, u32[]{:S(2)}, u32[]{:S(2)}) collective-permute-start(f32[8,2,128,128]{3,2,0,1:T(8,128)} %pad_maximum_fusion.1), channel_id=1, source_target_pairs={{0,8},{8,0},{1,9},{9,1},{2,10},{10,2},{3,11},{11,3},{4,12},{12,4},... | collective-permute-start | bytes 3145736 | tf_op jit(solution)/shard_map/ppermute | solution.py:13
  67.9 1.8 copy.280
  69.6 2.1 fusion.19
  73.4 1.4 fusion.8
  76.1 1.2 slice.156
  77.4 2.8 %collective-permute-start.1 = (f32[7,128,128]{2,1,0:T(8,128)S(1)}, f32[7,128,128]{2,1,0:T(8,128)S(1)}, u32[]{:S(2)}, u32[]{:S(2)}) collective-permute-start(f32[7,128,128]{2,1,0:T(8,128)S(1)} %pad_maximum_fusion.5), channel_id=1, source_target_pairs={{0,16},{16,0},{32,48},{48,32},{1,17},{17,1},{33,49},{49,33},{2,18}... | collective-permute-start | bytes 1376264 | tf_op jit(solution)/shard_map/ppermute | solution.py:13
  81.7 9.8 %collective-permute-done.1 = f32[7,128,128]{2,1,0:T(8,128)S(1)} collective-permute-done((f32[7,128,128]{2,1,0:T(8,128)S(1)}, f32[7,128,128]{2,1,0:T(8,128)S(1)}, u32[]{:S(2)}, u32[]{:S(2)}) %collective-permute-start.1) | collective-permute-done | bytes 458784 | tf_op jit(solution)/shard_map/ppermute | solution.py:13
  92.3 4.4 %collective-permute-start.2 = (f32[6,2,32,128]{3,2,1,0:T(8,128)S(1)}, f32[6,2,32,128]{3,2,1,0:T(8,128)S(1)}, u32[]{:S(2)}, u32[]{:S(2)}) collective-permute-start(f32[6,2,32,128]{3,2,1,0:T(8,128)S(1)} %pad_maximum_fusion.7), channel_id=1, source_target_pairs={{0,32},{16,48},{32,0},{48,16},{1,33},{17,49},{33,1},{49,17},{2,34}... | collective-permute-start | bytes 589832 | tf_op jit(solution)/shard_map/ppermute | solution.py:13
  96.7 1.5 fusion.51
  98.2 3.1 %collective-permute-done.2 = f32[6,2,32,128]{3,2,1,0:T(8,128)S(1)} collective-permute-done((f32[6,2,32,128]{3,2,1,0:T(8,128)S(1)}, f32[6,2,32,128]{3,2,1,0:T(8,128)S(1)}, u32[]{:S(2)}, u32[]{:S(2)}) %collective-permute-start.2) | collective-permute-done | bytes 196640 | tf_op jit(solution)/shard_map/ppermute | solution.py:13
  101.9 2.8 %collective-permute-start.3 = (f32[2,2,32,128]{3,2,1,0:T(8,128)S(1)}, f32[2,2,32,128]{3,2,1,0:T(8,128)S(1)}, u32[]{:S(2)}, u32[]{:S(2)}) collective-permute-start(f32[2,2,32,128]{3,2,1,0:T(8,128)S(1)} %pad_maximum_fusion.11), channel_id=1, source_target_pairs={{0,16},{16,0},{32,48},{48,32},{1,17},{17,1},{33,49},{49,33},{2,18}... | collective-permute-start | bytes 196616 | tf_op jit(solution)/shard_map/ppermute | solution.py:13
  107.0 4.7 %collective-permute-start.4 = (f32[4,128,128]{2,1,0:T(8,128)S(1)}, f32[4,128,128]{2,1,0:T(8,128)S(1)}, u32[]{:S(2)}, u32[]{:S(2)}) collective-permute-start(f32[4,128,128]{2,1,0:T(8,128)S(1)} %pad_maximum_fusion.6), channel_id=1, source_target_pairs={{0,8},{8,0},{1,9},{9,1},{2,10},{10,2},{3,11},{11,3},{4,12},{12,4},... | collective-permute-start | bytes 786440 | tf_op jit(solution)/shard_map/ppermute | solution.py:13
  111.8 36.4 %all_gather.10 = f32[16,32,128]{2,1,0:T(8,128)S(1)} all-gather(f32[1,32,128]{2,1,0:T(8,128)S(1)} %dynamic-slice_add_fusion.3), channel_id=1, replica_groups=mesh['z'=16,'x'=4,'core'=2,'head'=8] {'z'}, dimensions={0}, use_global_device_ids=true | all-gather | bytes 278528 | tf_op jit(solution)/shard_map/all_gather | solution.py:125
  148.2 1.7 fusion.22
  150.8 21.5 %reduce-scatter.2.cloned.1.call-done = f32[1,32,128]{2,1,0:T(8,128)} async-done(((f32[16,32,128]{2,1,0:T(8,128)}), f32[1,32,128]{2,1,0:T(8,128)}) %reduce-scatter.2.cloned.1.call-update) | async-done | bytes 16400 | tf_op jit(solution)/shard_map/reduce_scatter | solution.py:128
  173.2 25.1 %all-gather = f32[40,32,128]{2,1,0:T(8,128)S(1)} all-gather(f32[5,32,128]{2,1,0:T(8,128)S(1)} %copy.263), channel_id=2, replica_groups=mesh['z'=16,'x'=4,'core'=2,'head'=8] {'x','core'}, dimensions={0}, use_global_device_ids=true | all-gather | bytes 737280 | tf_op jit(solution)/shard_map/all_gather | solution.py:142
  200.2 2.0 fusion.20
  204.9 1.5 fusion.50
  206.4 1.5 fusion.49
  208.0 1.5 fusion.48
  209.5 1.5 fusion.47
  211.0 1.3 copy.269
  (122 shorter events, 26.7 us)
Async XLA Ops:
  9.9 10.4 %copy-start.21 = (s32[9,2,512]{2,1,0:T(2,128)S(1)}, s32[9,2,512]{2,1,0:T(2,128)}, u32[]{:S(2)}) copy-start(s32[9,2,512]{2,1,0:T(2,128)} %param.12) | copy-start | bytes 110596
  9.9 10.4 %copy-start.22 = (f32[9]{0:T(128)S(1)}, f32[9]{0:T(128)}, u32[]{:S(2)}) copy-start(f32[9]{0:T(128)} %constant.109) | copy-start | bytes 112
  12.6 24.4 %all-to-all-start = ((bf16[8,2,32768]{2,1,0:T(2,128)(2,1)}), bf16[8,2,32768]{2,1,0:T(2,128)(2,1)S(1)}, u32[]{:S(2)}, u32[]{:S(2)}) async-start(bf16[8,2,32768]{2,1,0:T(2,128)(2,1)} %reshape.92), calls=%async_computation | async-start | bytes 2097152 | tf_op jit(solution)/shard_map/all_to_all | solution.py:38
  20.2 152.1 %reduce-scatter.2.cloned.1.call-start = ((), (), s32[]{:S(2)}) async-start(), calls=%async_computation.2 | async-start | bytes 278528 | tf_op jit(solution)/shard_map/reduce_scatter | solution.py:128
  20.4 0.6 copy-start.16
  39.8 1.9 copy-start.17
  40.0 1.1 copy-start.4
  40.9 0.7 copy-start.1
  45.6 1.4 copy-start.11
  47.0 22.6 %copy-start = (f32[7,2,128,128]{3,2,0,1:T(8,128)}, f32[7,2,128,128]{3,2,0,1:T(8,128)S(1)}, u32[]{:S(2)}) copy-start(f32[7,2,128,128]{3,2,0,1:T(8,128)S(1)} %broadcast_multiply_fusion) | copy-start | bytes 2752516
  47.0 22.6 %copy-start.23 = (f32[2,2,1,1]{1,0,3,2:T(2,128)S(1)}, f32[2,2,1,1]{1,0,3,2:T(2,128)}, u32[]{:S(2)}) copy-start(f32[2,2,1,1]{1,0,3,2:T(2,128)} %constant.111) | copy-start | bytes 52
  48.1 27.0 %collective-permute-start = (f32[8,2,128,128]{3,2,0,1:T(8,128)}, f32[8,2,128,128]{3,2,0,1:T(8,128)}, u32[]{:S(2)}, u32[]{:S(2)}) collective-permute-start(f32[8,2,128,128]{3,2,0,1:T(8,128)} %pad_maximum_fusion.1), channel_id=1, source_target_pairs={{0,8},{8,0},{1,9},{9,1},{2,10},{10,2},{3,11},{11,3},{4,12},{12,4},... | collective-permute-start | bytes 3145736 | tf_op jit(solution)/shard_map/ppermute | solution.py:13
  69.6 5.2 %copy-start.9 = (bf16[2,256,2,128]{1,3,2,0:T(8,128)(2,1)S(1)}, bf16[2,256,2,128]{1,3,2,0:T(8,128)(2,1)}, u32[]{:S(2)}) copy-start(bf16[2,256,2,128]{1,3,2,0:T(8,128)(2,1)} %copy.288) | copy-start | bytes 786436
  72.5 3.5 %copy-start.12 = (f32[2,128,128]{2,1,0:T(8,128)S(1)}, f32[2,128,128]{2,1,0:T(8,128)}, u32[]{:S(2)}) copy-start(f32[2,128,128]{2,1,0:T(8,128)} %copy-done.11) | copy-start | bytes 393220
  73.4 3.9 %slice-start = ((f32[7,2,128,128]{3,2,0,1:T(8,128)}), f32[6,2,128,128]{3,2,0,1:T(8,128)S(1)}, s32[]{:S(2)}) async-start(f32[7,2,128,128]{3,2,0,1:T(8,128)} %copy-done), calls=%async_computation.3 | async-start | bytes 1572864 | tf_op jit(solution)/shard_map/slice | solution.py:102
  75.1 5.2 %copy-start.10 = (bf16[2,256,2,128]{1,3,2,0:T(8,128)(2,1)S(1)}, bf16[2,256,2,128]{1,3,2,0:T(8,128)(2,1)}, u32[]{:S(2)}) copy-start(bf16[2,256,2,128]{1,3,2,0:T(8,128)(2,1)} %copy.288) | copy-start | bytes 786436
  75.1 5.2 %copy-start.20 = (pred[256,256]{1,0:T(8,128)(4,1)S(1)}, pred[256,256]{1,0:T(8,128)(4,1)}, u32[]{:S(2)}) copy-start(pred[256,256]{1,0:T(8,128)(4,1)} %iota_compare_fusion) | copy-start | bytes 196612
  77.3 3.3 %copy-start.8 = (bf16[2,256,2,128]{1,3,2,0:T(8,128)(2,1)S(1)}, bf16[2,256,2,128]{1,3,2,0:T(8,128)(2,1)}, u32[]{:S(2)}) copy-start(bf16[2,256,2,128]{1,3,2,0:T(8,128)(2,1)} %copy.280) | copy-start | bytes 786436
  77.4 14.0 %collective-permute-start.1 = (f32[7,128,128]{2,1,0:T(8,128)S(1)}, f32[7,128,128]{2,1,0:T(8,128)S(1)}, u32[]{:S(2)}, u32[]{:S(2)}) collective-permute-start(f32[7,128,128]{2,1,0:T(8,128)S(1)} %pad_maximum_fusion.5), channel_id=1, source_target_pairs={{0,16},{16,0},{32,48},{48,32},{1,17},{17,1},{33,49},{49,33},{2,18}... | collective-permute-start | bytes 1376264 | tf_op jit(solution)/shard_map/ppermute | solution.py:13
  92.2 14.8 %copy-start.14 = (f32[1,128,128]{2,1,0:T(8,128)}, f32[1,128,128]{2,1,0:T(8,128)S(1)}, u32[]{:S(2)}) copy-start(f32[1,128,128]{2,1,0:T(8,128)S(1)} %get-tuple-element.12) | copy-start | bytes 196612
  92.3 9.0 %collective-permute-start.2 = (f32[6,2,32,128]{3,2,1,0:T(8,128)S(1)}, f32[6,2,32,128]{3,2,1,0:T(8,128)S(1)}, u32[]{:S(2)}, u32[]{:S(2)}) collective-permute-start(f32[6,2,32,128]{3,2,1,0:T(8,128)S(1)} %pad_maximum_fusion.7), channel_id=1, source_target_pairs={{0,32},{16,48},{32,0},{48,16},{1,33},{17,49},{33,1},{49,17},{2,34}... | collective-permute-start | bytes 589832 | tf_op jit(solution)/shard_map/ppermute | solution.py:13
  101.9 5.0 %collective-permute-start.3 = (f32[2,2,32,128]{3,2,1,0:T(8,128)S(1)}, f32[2,2,32,128]{3,2,1,0:T(8,128)S(1)}, u32[]{:S(2)}, u32[]{:S(2)}) collective-permute-start(f32[2,2,32,128]{3,2,1,0:T(8,128)S(1)} %pad_maximum_fusion.11), channel_id=1, source_target_pairs={{0,16},{16,0},{32,48},{48,32},{1,17},{17,1},{33,49},{49,33},{2,18}... | collective-permute-start | bytes 196616 | tf_op jit(solution)/shard_map/ppermute | solution.py:13
  107.0 42.8 %collective-permute-start.4 = (f32[4,128,128]{2,1,0:T(8,128)S(1)}, f32[4,128,128]{2,1,0:T(8,128)S(1)}, u32[]{:S(2)}, u32[]{:S(2)}) collective-permute-start(f32[4,128,128]{2,1,0:T(8,128)S(1)} %pad_maximum_fusion.6), channel_id=1, source_target_pairs={{0,8},{8,0},{1,9},{9,1},{2,10},{10,2},{3,11},{11,3},{4,12},{12,4},... | collective-permute-start | bytes 786440 | tf_op jit(solution)/shard_map/ppermute | solution.py:13
  149.9 22.5 %copy-start.15 = (f32[4,32,128]{2,0,1:T(4,128)S(1)}, f32[4,32,128]{2,0,1:T(4,128)}, u32[]{:S(2)}) copy-start(f32[4,32,128]{2,0,1:T(4,128)} %fusion.22) | copy-start | bytes 196612
  150.8 21.5 %copy-start.13 = (bf16[7,2,128,128]{3,2,1,0:T(8,128)(2,1)}, bf16[7,2,128,128]{3,2,1,0:T(8,128)(2,1)S(1)}, u32[]{:S(2)}) copy-start(bf16[7,2,128,128]{3,2,1,0:T(8,128)(2,1)S(1)} %fusion.45) | copy-start | bytes 1376260
  172.4 29.9 %copy-start.5 = (bf16[2,256,2,128]{3,2,1,0:T(2,128)(2,1)S(1)}, bf16[2,256,2,128]{3,2,1,0:T(2,128)(2,1)}, u32[]{:S(2)}) copy-start(bf16[2,256,2,128]{3,2,1,0:T(2,128)(2,1)} %copy-done.4) | copy-start | bytes 786436
  198.4 0.8 copy-start.7
  198.4 4.9 %copy-start.6 = (f32[2,2,128,256]{3,2,1,0:T(8,128)S(1)}, f32[2,2,128,256]{3,2,1,0:T(8,128)}, u32[]{:S(2)}) copy-start(f32[2,2,128,256]{3,2,1,0:T(8,128)} %fusion.65) | copy-start | bytes 1572868
  203.5 9.0 %copy-start.2 = (bf16[2,256,2,128]{3,2,1,0:T(2,128)(2,1)S(1)}, bf16[2,256,2,128]{3,2,1,0:T(2,128)(2,1)}, u32[]{:S(2)}) copy-start(bf16[2,256,2,128]{3,2,1,0:T(2,128)(2,1)} %copy-done.1) | copy-start | bytes 786436
  203.5 9.0 %copy-start.18 = (f32[8,2,2,256]{3,0,1,2:T(8,128)S(1)}, f32[8,2,2,256]{3,0,1,2:T(8,128)}, u32[]{:S(2)}) copy-start(f32[8,2,2,256]{3,0,1,2:T(8,128)} %copy.349) | copy-start | bytes 98308
  203.7 8.8 %copy-start.19 = (bf16[2,1,2,128,128]{3,4,1,2,0:T(8,128)(2,1)S(1)}, bf16[2,1,2,128,128]{3,4,1,2,0:T(8,128)(2,1)}, u32[]{:S(2)}) copy-start(bf16[2,1,2,128,128]{3,4,1,2,0:T(8,128)(2,1)} %copy.270) | copy-start | bytes 393220
  213.3 1.0 copy-start.3
Sparse Core Ops, SparseCore 0:
  106.9 65.4 reduce-scatter.1

commit v4 on v2

--- a/solution.py
+++ b/solution.py
@@ -122,27 +122,25 @@
         running = running + arrived[0]
         pending = pending[1:] + arrived[2:]
 
-    quarter = head_size // 4
-    pieces = jnp.concatenate(
-        [
-            jnp.stack([cross_x1, grad_x1]).reshape(8, quarter, head_size),
-            jnp.stack([cross_x2, grad_x2]).reshape(4, quarter, head_size),
-            jnp.stack(cross_z + [grad_z]),
-        ]
-    )
-    gathered = lax.all_gather(pieces, ("x", "core")).reshape((4, 2) + pieces.shape)
-    own = lax.dynamic_index_in_dim(gathered, x_index, 0, keepdims=False)
-    level_one = own[:, :8].reshape(2, 2, head_size, head_size)
-    pair_first = lax.dynamic_index_in_dim(gathered, x_index - x_index % 2, 0, keepdims=False)
-    pair_second = lax.dynamic_index_in_dim(gathered, x_index - x_index % 2 + 1, 0, keepdims=False)
-    level_two = jnp.stack(
-        [pair_first[:, 8:12].reshape(2, 2, 2, quarter, head_size), pair_second[:, 8:12].reshape(2, 2, 2, quarter, head_size)],
-        axis=3,
-    ).reshape(2, 2, head_size, head_size)
-    z_levels = gathered[:, :, 12:].transpose(1, 2, 0, 3, 4).reshape(2, -1, head_size, head_size)
-    device_grad = grad_first + level_one[:, 1] + level_two[:, 1] + z_levels[:, -1]
-    cross_list = [cross_first, level_one[:, 0], level_two[:, 0]] + [
-        z_levels[:, level] for level in range(cross_levels - 3)
+    z_part = jnp.concatenate([jnp.stack(cross_z), grad_z[None]])
+    odd_x = x_index % 2 == 1
+    high_x = x_index // 2 == 1
+    pair_part = swapped(jnp.concatenate([z_part, jnp.stack([cross_x2, grad_x2]).reshape(-1, head_size // 4, head_size)]), "x", 0)
+    z_levels = z_part.shape[0]
+
+    def ordered(own, other, other_first):
+        return jnp.stack([jnp.where(other_first, other, own), jnp.where(other_first, own, other)])
+
+    z_half = ordered(z_part, pair_part[:z_levels], odd_x)
+    level_two = ordered(jnp.stack([cross_x2, grad_x2]), pair_part[z_levels:].reshape(2, 2, head_size // 4, head_size), odd_x)
+    level_two = level_two.transpose(1, 2, 0, 3, 4).reshape(2, head_size, head_size)
+    z_full = ordered(z_half, swapped(z_half, "x", 1), high_x)
+    z_full = z_full.transpose(2, 0, 1, 3, 4).reshape(z_levels, head_size, head_size)
+    own_levels = jnp.concatenate([jnp.stack([cross_x1, grad_x1]), level_two, z_full])
+    both_heads = ordered(own_levels, swapped(own_levels, "core", 0), core_index == 1)
+    device_grad = grad_first + both_heads[:, 1] + both_heads[:, 3] + both_heads[:, -1]
+    cross_list = [cross_first, both_heads[:, 0], both_heads[:, 2]] + [
+        both_heads[:, 4 + level] for level in range(cross_levels - 3)
     ]
     level_table = bucket_table(per_dev, local_levels)
     local_buckets = jnp.einsum(

time: 214 us -> 198 us (0.925)
  waiting for transfers between devices: 63.1 us -> 29.7 us
  other arithmetic: 13.5 us -> 33.6 us
  starting transfers between devices: 64 us -> 81.9 us
  between operations: 19.3 us -> 5.92 us
  local copies, waits for them, and re-layouts: 38.8 us -> 27.8 us
  matrix products: 13.6 us -> 17.1 us
    all_gather x1 -> x0, waiting for transfers between devices: 26.6 us -> none  [body(): lax.all_gather(pieces, ('x', 'core')).reshape((4, 2) + pieces.shape)]
    ppermute x7 -> x10, starting transfers between devices: 56.3 us -> 74.2 us  [swapped(): return lax.ppermute(value, axis, pairs)]
    unnamed x1 -> x14, other arithmetic: 0.61 us -> 16.3 us
    unnamed x56 -> x76, local copies, waits for them, and re-layouts: 15.6 us -> 6.79 us
    ppermute x7 -> x10, waiting for transfers between devices: 20.6 us -> 13.7 us  [swapped(): return lax.ppermute(value, axis, pairs)]
    mul x0 -> x2, other arithmetic: none -> 4.17 us  [the longest x1 2.08 us: body(): cross_x1 = arrived[0] * upper_bits[1]]
    add x4 -> x0, other arithmetic: 3.39 us -> none  [the longest x3 1.87 us: body(): running = running + arrived[0]]
    another operation x6 -> x3, local copies, waits for them, and re-layouts: 5.4 us -> 2.14 us
  transfers between devices with their start and end apart: 9 -> 11, of which waited for: 8 -> 7; matrix products, arithmetic and copies ran while one was open for 5% -> 10% of each run, Pallas kernels for 0% -> 0%
where the time goes in v4:
time: 198 us; the launch traced here: 196 us
  starting transfers between devices  81.9 us (41%)
  other arithmetic  33.6 us (17%)
  waiting for transfers between devices  29.7 us (15%)
  local copies, waits for them, and re-layouts  27.8 us (14%)
  matrix products  17.1 us (9%)
  between operations  5.92 us (3%)
    ppermute x10, starting transfers between devices, swapped(): return lax.ppermute(value, axis, pairs)  74.2 us
    unnamed x14, other arithmetic  16.3 us
    all_to_all x1, waiting for transfers between devices, body(): lax.all_to_all(stacked, 'head', split_axis=2, concat_axis=0, tiled=True)  16 us
    ppermute x10, waiting for transfers between devices, swapped(): return lax.ppermute(value, axis, pairs)  13.7 us
    all_to_all x1, starting transfers between devices, body(): lax.all_to_all(stacked, 'head', split_axis=2, concat_axis=0, tiled=True)  7.65 us
    unnamed x76, local copies, waits for them, and re-layouts  6.79 us
  transfers between devices with their start and end apart: 11, of which 7 were waited for; matrix products, arithmetic and copies ran while one was open for 10% of the time, Pallas kernels for 0%

profile of v4, /device:TPU:1, one launch (start us, length us, event | category | flops | bytes accessed | tf_op | source)
XLA Modules:
  0.0 196.0 jit_solution(17460778881970739006)
XLA Ops:
  0.6 1.3 pad_maximum_fusion
  2.0 1.4 copy.210
  3.4 2.6 %reshape.166 = bf16[8,2,32768]{2,1,0:T(2,128)(2,1)} reshape(bf16[2048,4,64]{2,1,0:T(4,128)(2,1)S(1)} %bitcast.206) | data formatting | bytes 2097152
  6.0 7.7 %all-to-all-start = ((bf16[8,2,32768]{2,1,0:T(2,128)(2,1)}), bf16[8,2,32768]{2,1,0:T(2,128)(2,1)S(1)}, u32[]{:S(2)}, u32[]{:S(2)}) async-start(bf16[8,2,32768]{2,1,0:T(2,128)(2,1)} %reshape.166), calls=%async_computation | async-start | bytes 2097152 | tf_op jit(solution)/shard_map/all_to_all | solution.py:28
  14.5 16.0 %all-to-all-done = bf16[8,2,32768]{2,1,0:T(2,128)(2,1)S(1)} async-done(((bf16[8,2,32768]{2,1,0:T(2,128)(2,1)}), bf16[8,2,32768]{2,1,0:T(2,128)(2,1)S(1)}, u32[]{:S(2)}, u32[]{:S(2)}) %all-to-all-start) | async-done | bytes 1048608 | tf_op jit(solution)/shard_map/all_to_all | solution.py:28
  30.5 1.4 reshape.167
  39.1 1.3 broadcast_multiply_fusion
  40.4 2.1 %fusion.72 = (f32[2,128,128]{2,1,0:T(8,128)S(1)}, f32[2,2,128,128]{3,2,1,0:T(8,128)}) fusion(bf16[2,256,2,128]{1,3,2,0:T(8,128)(2,1)} %copy.218, bf16[2,256,2,128]{3,2,1,0:T(2,128)(2,1)S(1)} %reshape_squeeze.10), kind=kOutput, calls=%fused_computation.178 | convolution fusion | flops 33587200 | bytes 917504 | tf_op jit(solution)/shard_map/buhp,buhr->bhpr/dot_general | solution.py:74
  44.2 15.1 %collective-permute-start = (f32[8,2,128,128]{3,2,0,1:T(8,128)}, f32[8,2,128,128]{3,2,0,1:T(8,128)}, u32[]{:S(2)}, u32[]{:S(2)}) collective-permute-start(f32[8,2,128,128]{3,2,0,1:T(8,128)} %pad_maximum_fusion.1), channel_id=1, source_target_pairs={{0,8},{8,0},{1,9},{9,1},{2,10},{10,2},{3,11},{11,3},{4,12},{12,4},... | collective-permute-start | bytes 3145736 | tf_op jit(solution)/shard_map/ppermute | solution.py:13
  59.3 2.6 %collective-permute-done = f32[8,2,128,128]{3,2,0,1:T(8,128)} collective-permute-done((f32[8,2,128,128]{3,2,0,1:T(8,128)}, f32[8,2,128,128]{3,2,0,1:T(8,128)}, u32[]{:S(2)}, u32[]{:S(2)}) %collective-permute-start) | collective-permute-done | bytes 1048608 | tf_op jit(solution)/shard_map/ppermute | solution.py:13
  65.8 2.8 %collective-permute-start.1 = (f32[7,128,128]{2,1,0:T(8,128)}, f32[7,128,128]{2,1,0:T(8,128)}, u32[]{:S(2)}, u32[]{:S(2)}) collective-permute-start(f32[7,128,128]{2,1,0:T(8,128)} %pad_maximum_fusion.6), channel_id=1, source_target_pairs={{0,16},{16,0},{32,48},{48,32},{1,17},{17,1},{33,49},{49,33},{2,18}... | collective-permute-start | bytes 1376264 | tf_op jit(solution)/shard_map/ppermute | solution.py:13
  75.9 3.8 %collective-permute-done.1 = f32[7,128,128]{2,1,0:T(8,128)} collective-permute-done((f32[7,128,128]{2,1,0:T(8,128)}, f32[7,128,128]{2,1,0:T(8,128)}, u32[]{:S(2)}, u32[]{:S(2)}) %collective-permute-start.1) | collective-permute-done | bytes 458784 | tf_op jit(solution)/shard_map/ppermute | solution.py:13
  79.7 2.1 %slice_multiply_fusion.2 = (f32[1,128,128]{2,1,0:T(8,128)}, f32[1,128,128]{2,1,0:T(8,128)S(1)}, f32[1,128,128]{2,1,0:T(8,128)}) fusion(f32[7,128,128]{2,1,0:T(8,128)} %collective-permute-done.1, f32[]{:T(128)} %bitcast.23, f32[1,128,128]{2,1,0:T(8,128)S(1)} %dynamic-slice_add_fusion.2, f32[]{:T(128)S(6)} %sub.27), kind=kLoop, calls=%fused_computation.127 | loop fusion | flops 49152 | bytes 393224 | tf_op jit(solution)/shard_map/mul | solution.py:95
  84.2 4.4 %collective-permute-start.2 = (f32[6,2,32,128]{3,2,1,0:T(8,128)}, f32[6,2,32,128]{3,2,1,0:T(8,128)}, u32[]{:S(2)}, u32[]{:S(2)}) collective-permute-start(f32[6,2,32,128]{3,2,1,0:T(8,128)} %pad_maximum_fusion.7), channel_id=1, source_target_pairs={{0,32},{16,48},{32,0},{48,16},{1,33},{17,49},{33,1},{49,17},{2,34}... | collective-permute-start | bytes 589832 | tf_op jit(solution)/shard_map/ppermute | solution.py:13
  90.9 2.3 %collective-permute-done.2 = f32[6,2,32,128]{3,2,1,0:T(8,128)} collective-permute-done((f32[6,2,32,128]{3,2,1,0:T(8,128)}, f32[6,2,32,128]{3,2,1,0:T(8,128)}, u32[]{:S(2)}, u32[]{:S(2)}) %collective-permute-start.2) | collective-permute-done | bytes 196640 | tf_op jit(solution)/shard_map/ppermute | solution.py:13
  93.1 2.1 %slice_multiply_fusion.4 = (f32[1,2,32,128]{3,2,1,0:T(8,128)}, f32[1,2,32,128]{3,2,1,0:T(8,128)}, f32[2,32,128]{2,1,0:T(8,128)S(1)}) fusion(f32[6,2,32,128]{3,2,1,0:T(8,128)} %collective-permute-done.2, f32[]{:T(128)} %bitcast.38, f32[]{:T(128)S(6)} %sub.33), kind=kLoop, calls=%fused_computation.149 | loop fusion | flops 16384 | bytes 163848 | tf_op jit(solution)/shard_map/mul | solution.py:106
  96.2 3.7 %collective-permute-start.3 = (f32[5,32,128]{2,1,0:T(8,128)S(1)}, f32[5,32,128]{2,1,0:T(8,128)S(1)}, u32[]{:S(2)}, u32[]{:S(2)}) collective-permute-start(f32[5,32,128]{2,1,0:T(8,128)S(1)} %pad_maximum_fusion.10), channel_id=1, source_target_pairs={{0,64},{64,0},{128,192},{192,128},{256,320},{320,256},{384,448},{4... | collective-permute-start | bytes 245768 | tf_op jit(solution)/shard_map/ppermute | solution.py:13
  99.9 2.1 %fusion.73 = f32[2,2,128,256]{3,2,1,0:T(8,128)} fusion(bf16[2,256,2,128]{1,3,2,0:T(8,128)(2,1)S(1)} %copy.239, bf16[2,2,256,256]{3,2,1,0:T(8,128)(2,1)} %fusion.9), kind=kOutput, calls=%fused_computation.179 | convolution fusion | flops 67108864 | bytes 1310720 | tf_op jit(solution)/shard_map/bhtu,bthp->buhp/dot_general | solution.py:68
  103.3 5.9 %collective-permute-start.4 = (f32[4,32,128]{2,1,0:T(8,128)S(1)}, f32[4,32,128]{2,1,0:T(8,128)S(1)}, u32[]{:S(2)}, u32[]{:S(2)}) collective-permute-start(f32[4,32,128]{2,1,0:T(8,128)S(1)} %pad_maximum_fusion.11), channel_id=1, source_target_pairs={{0,128},{64,192},{128,0},{192,64},{256,384},{320,448},{384,256},{4... | collective-permute-start | bytes 196616 | tf_op jit(solution)/shard_map/ppermute | solution.py:13
  109.3 2.0 %fusion.8 = bf16[2,2,256,256]{3,2,1,0:T(8,128)(2,1)} fusion(bf16[2,256,2,128]{1,3,2,0:T(8,128)(2,1)S(1)} %copy.239, f32[2,2,256]{2,1,0:T(2,128)S(1)} %bitcast.238, pred[256,256]{1,0:T(8,128)(4,1)} %iota_compare_fusion, bf16[2,256,2,128]{3,2,1,0:T(2,128)(2,1)S(1)} %copy-done.5), kind=kOutput, calls=%fused_computation.30 | convolution fusion | flops 67895296 | bytes 1118208 | tf_op jit(solution)/shard_map/bthp,buhp->bhtu/dot_general | solution.py:56
  113.1 10.6 %collective-permute-start.5 = (f32[3,32,128]{2,1,0:T(8,128)}, f32[3,32,128]{2,1,0:T(8,128)S(1)}, u32[]{:S(2)}, u32[]{:S(2)}) collective-permute-start(f32[3,32,128]{2,1,0:T(8,128)} %pad_maximum_fusion.14), channel_id=1, source_target_pairs={{0,256},{64,320},{128,384},{192,448},{256,0},{320,64},{384,128},{4... | collective-permute-start | bytes 147464 | tf_op jit(solution)/shard_map/ppermute | solution.py:13
  125.4 2.0 %constant_dynamic-update-slice_fusion.3 = (f32[9,32,128]{2,1,0:T(8,128)}, f32[1,32,128]{2,1,0:T(8,128)S(1)}, f32[1,32,128]{2,1,0:T(8,128)S(1)}) fusion(f32[9,32,128]{2,1,0:T(8,128)} %get-tuple-element.27, f32[3,32,128]{2,1,0:T(8,128)S(1)} %collective-permute-done.5, f32[]{:T(128)} %bitcast.36, f32[1,32,128]{2,1,0:T(8,128)S(1)} %get-tuple-element.28, ...), kind=kLoop, calls=%fused_computation.136 | loop fusion | flops 12288 | bytes 115200
  127.4 13.1 %collective-permute-start.6 = (f32[2,32,128]{2,1,0:T(8,128)S(1)}, f32[2,32,128]{2,1,0:T(8,128)S(1)}, u32[]{:S(2)}, u32[]{:S(2)}) collective-permute-start(f32[2,32,128]{2,1,0:T(8,128)S(1)} %pad_maximum_fusion.15), channel_id=1, source_target_pairs={{0,512},{64,576},{128,640},{192,704},{256,768},{320,832},{384,896}... | collective-permute-start | bytes 98312 | tf_op jit(solution)/shard_map/ppermute | solution.py:13
  143.1 2.0 %constant_dynamic-update-slice_fusion.1 = (f32[9,32,128]{2,1,0:T(8,128)}, f32[1,32,128]{2,1,0:T(8,128)S(1)}, f32[5,32,128]{2,1,0:T(8,128)S(1)}) fusion(f32[9,32,128]{2,1,0:T(8,128)} %constant_dynamic-update-slice_fusion.2, f32[2,32,128]{2,1,0:T(8,128)S(1)} %collective-permute-done.6, f32[]{:T(128)S(6)} %sub.32, f32[3,32,128]{2,1,0:T(8,128)} %copy-done.31, ...), kind=kLoop, calls=%fused_computation.134 | loop fusion | flops 32767 | bytes 131600
  145.7 3.1 %collective-permute-start.7 = (f32[9,32,128]{2,1,0:T(8,128)}, f32[9,32,128]{2,1,0:T(8,128)S(1)}, u32[]{:S(2)}, u32[]{:S(2)}) collective-permute-start(f32[9,32,128]{2,1,0:T(8,128)} %constant_dynamic-update-slice_fusion), channel_id=1, source_target_pairs={{0,16},{16,0},{32,48},{48,32},{1,17},{17,1},{33,49},{49,33},{2,18}... | collective-permute-start | bytes 442376 | tf_op jit(solution)/shard_map/ppermute | solution.py:13
  150.1 1.4 constant_dynamic-update-slice_fusion.8
  152.2 4.5 %collective-permute-start.8 = (f32[2,5,32,128]{3,2,1,0:T(8,128)S(1)}, f32[2,5,32,128]{3,2,1,0:T(8,128)S(1)}, u32[]{:S(2)}, u32[]{:S(2)}) collective-permute-start(f32[2,5,32,128]{3,2,1,0:T(8,128)S(1)} %pad_maximum_fusion.8), channel_id=1, source_target_pairs={{0,32},{16,48},{32,0},{48,16},{1,33},{17,49},{33,1},{49,17},{2,34}... | collective-permute-start | bytes 491528 | tf_op jit(solution)/shard_map/ppermute | solution.py:13
  156.8 3.7 %collective-permute-done.8 = f32[2,5,32,128]{3,2,1,0:T(8,128)S(1)} collective-permute-done((f32[2,5,32,128]{3,2,1,0:T(8,128)S(1)}, f32[2,5,32,128]{3,2,1,0:T(8,128)S(1)}, u32[]{:S(2)}, u32[]{:S(2)}) %collective-permute-start.8) | collective-permute-done | bytes 163872 | tf_op jit(solution)/shard_map/ppermute | solution.py:13
  161.5 10.9 %collective-permute-start.9 = (f32[9,128,128]{2,1,0:T(8,128)}, f32[9,128,128]{2,1,0:T(8,128)}, u32[]{:S(2)}, u32[]{:S(2)}) collective-permute-start(f32[9,128,128]{2,1,0:T(8,128)} %pad_maximum_fusion.5), channel_id=1, source_target_pairs={{0,8},{8,0},{1,9},{9,1},{2,10},{10,2},{3,11},{11,3},{4,12},{12,4},... | collective-permute-start | bytes 1769480 | tf_op jit(solution)/shard_map/ppermute | solution.py:13
  175.4 2.2 %fusion.59 = bf16[7,2,128,128]{3,2,1,0:T(8,128)(2,1)} fusion(f32[8,2,128,128]{3,2,0,1:T(8,128)} %collective-permute-done, f32[]{:T(128)} %bitcast.20), kind=kLoop, calls=%fused_computation.115 | loop fusion | flops 32767 | bytes 262148
  180.9 1.3 fusion.17
  191.7 2.0 %fusion = f32[2,256,2,128]{1,3,2,0:T(8,128)S(1)} fusion(f32[2,8,256,2]{2,1,3,0:T(8,128)S(1)} %bitcast.236, bf16[2,7,2,128,128]{3,4,1,2,0:T(8,128)(2,1)} %copy-done.13, bf16[2,1,2,128,128]{3,4,1,2,0:T(8,128)(2,1)S(1)} %copy-done.28, bf16[2,256,2,128,1]{3,2,1,0,4:T(2,128)(2,1)S(1)} %bitcast.212), kind=kOutput, calls=%fused_computation.1 | convolution fusion | flops 272498688 | bytes 1867776 | tf_op jit(solution)/shard_map/bmhpr,bthr->bmthp/dot_general | solution.py:156
  (169 shorter events, 50.4 us)
Async XLA Ops:
  3.4 10.3 %copy-start.34 = (s32[9,2,512]{2,1,0:T(2,128)S(1)}, s32[9,2,512]{2,1,0:T(2,128)}, u32[]{:S(2)}) copy-start(s32[9,2,512]{2,1,0:T(2,128)} %param.11) | copy-start | bytes 110596
  3.4 10.3 %copy-start.35 = (f32[9]{0:T(128)S(1)}, f32[9]{0:T(128)}, u32[]{:S(2)}) copy-start(f32[9]{0:T(128)} %constant.103) | copy-start | bytes 112
  6.0 24.4 %all-to-all-start = ((bf16[8,2,32768]{2,1,0:T(2,128)(2,1)}), bf16[8,2,32768]{2,1,0:T(2,128)(2,1)S(1)}, u32[]{:S(2)}, u32[]{:S(2)}) async-start(bf16[8,2,32768]{2,1,0:T(2,128)(2,1)} %reshape.166), calls=%async_computation | async-start | bytes 2097152 | tf_op jit(solution)/shard_map/all_to_all | solution.py:28
  14.4 19.9 %copy-start.25 = (f32[8,2,2,256]{3,0,1,2:T(8,128)}, f32[8,2,2,256]{3,0,1,2:T(8,128)S(1)}, u32[]{:S(2)}) copy-start(f32[8,2,2,256]{3,0,1,2:T(8,128)S(1)} %copy.299) | copy-start | bytes 98308
  40.4 18.9 %copy-start = (f32[7,2,128,128]{3,2,0,1:T(8,128)}, f32[7,2,128,128]{3,2,0,1:T(8,128)S(1)}, u32[]{:S(2)}) copy-start(f32[7,2,128,128]{3,2,0,1:T(8,128)S(1)} %broadcast_multiply_fusion) | copy-start | bytes 2752516
  44.2 17.7 %collective-permute-start = (f32[8,2,128,128]{3,2,0,1:T(8,128)}, f32[8,2,128,128]{3,2,0,1:T(8,128)}, u32[]{:S(2)}, u32[]{:S(2)}) collective-permute-start(f32[8,2,128,128]{3,2,0,1:T(8,128)} %pad_maximum_fusion.1), channel_id=1, source_target_pairs={{0,8},{8,0},{1,9},{9,1},{2,10},{10,2},{3,11},{11,3},{4,12},{12,4},... | collective-permute-start | bytes 3145736 | tf_op jit(solution)/shard_map/ppermute | solution.py:13
  65.8 13.9 %collective-permute-start.1 = (f32[7,128,128]{2,1,0:T(8,128)}, f32[7,128,128]{2,1,0:T(8,128)}, u32[]{:S(2)}, u32[]{:S(2)}) collective-permute-start(f32[7,128,128]{2,1,0:T(8,128)} %pad_maximum_fusion.6), channel_id=1, source_target_pairs={{0,16},{16,0},{32,48},{48,32},{1,17},{17,1},{33,49},{49,33},{2,18}... | collective-permute-start | bytes 1376264 | tf_op jit(solution)/shard_map/ppermute | solution.py:13
  75.0 14.8 %copy-start.2 = (bf16[2,256,2,128]{3,2,1,0:T(2,128)(2,1)S(1)}, bf16[2,256,2,128]{3,2,1,0:T(2,128)(2,1)}, u32[]{:S(2)}) copy-start(bf16[2,256,2,128]{3,2,1,0:T(2,128)(2,1)} %copy-done.1) | copy-start | bytes 786436
  75.9 12.7 %copy-start.9 = (bf16[2,256,2,128]{1,3,2,0:T(8,128)(2,1)S(1)}, bf16[2,256,2,128]{1,3,2,0:T(8,128)(2,1)}, u32[]{:S(2)}) copy-start(bf16[2,256,2,128]{1,3,2,0:T(8,128)(2,1)} %copy.247) | copy-start | bytes 786436
  75.9 12.7 %copy-start.33 = (pred[256,256]{1,0:T(8,128)(4,1)S(1)}, pred[256,256]{1,0:T(8,128)(4,1)}, u32[]{:S(2)}) copy-start(pred[256,256]{1,0:T(8,128)(4,1)} %iota_compare_fusion) | copy-start | bytes 196612
  83.4 11.8 %copy-start.32 = (f32[2,32,128]{2,1,0:T(8,128)S(1)}, f32[2,32,128]{2,1,0:T(8,128)}, u32[]{:S(2)}) copy-start(f32[2,32,128]{2,1,0:T(8,128)} %get-tuple-element.29) | copy-start | bytes 98308
  84.2 8.9 %collective-permute-start.2 = (f32[6,2,32,128]{3,2,1,0:T(8,128)}, f32[6,2,32,128]{3,2,1,0:T(8,128)}, u32[]{:S(2)}, u32[]{:S(2)}) collective-permute-start(f32[6,2,32,128]{3,2,1,0:T(8,128)} %pad_maximum_fusion.7), channel_id=1, source_target_pairs={{0,32},{16,48},{32,0},{48,16},{1,33},{17,49},{33,1},{49,17},{2,34}... | collective-permute-start | bytes 589832 | tf_op jit(solution)/shard_map/ppermute | solution.py:13
  88.6 20.6 %copy-start.5 = (bf16[2,256,2,128]{3,2,1,0:T(2,128)(2,1)S(1)}, bf16[2,256,2,128]{3,2,1,0:T(2,128)(2,1)}, u32[]{:S(2)}) copy-start(bf16[2,256,2,128]{3,2,1,0:T(2,128)(2,1)} %copy-done.4) | copy-start | bytes 786436
  96.2 5.8 %collective-permute-start.3 = (f32[5,32,128]{2,1,0:T(8,128)S(1)}, f32[5,32,128]{2,1,0:T(8,128)S(1)}, u32[]{:S(2)}, u32[]{:S(2)}) collective-permute-start(f32[5,32,128]{2,1,0:T(8,128)S(1)} %pad_maximum_fusion.10), channel_id=1, source_target_pairs={{0,64},{64,0},{128,192},{192,128},{256,320},{320,256},{384,448},{4... | collective-permute-start | bytes 245768 | tf_op jit(solution)/shard_map/ppermute | solution.py:13
  103.3 53.4 %copy-start.19 = (f32[1,2,32,128]{3,2,1,0:T(8,128)S(1)}, f32[1,2,32,128]{3,2,1,0:T(8,128)}, u32[]{:S(2)}) copy-start(f32[1,2,32,128]{3,2,1,0:T(8,128)} %get-tuple-element.19) | copy-start | bytes 98308
  103.3 53.4 %copy-start.20 = (f32[1,2,32,128]{3,2,1,0:T(8,128)S(1)}, f32[1,2,32,128]{3,2,1,0:T(8,128)}, u32[]{:S(2)}) copy-start(f32[1,2,32,128]{3,2,1,0:T(8,128)} %get-tuple-element.20) | copy-start | bytes 98308
  103.3 7.9 %collective-permute-start.4 = (f32[4,32,128]{2,1,0:T(8,128)S(1)}, f32[4,32,128]{2,1,0:T(8,128)S(1)}, u32[]{:S(2)}, u32[]{:S(2)}) collective-permute-start(f32[4,32,128]{2,1,0:T(8,128)S(1)} %pad_maximum_fusion.11), channel_id=1, source_target_pairs={{0,128},{64,192},{128,0},{192,64},{256,384},{320,448},{384,256},{4... | collective-permute-start | bytes 196616 | tf_op jit(solution)/shard_map/ppermute | solution.py:13
  111.3 12.5 %copy-start.30 = (f32[4,32,128]{2,1,0:T(8,128)}, f32[4,32,128]{2,1,0:T(8,128)S(1)}, u32[]{:S(2)}) copy-start(f32[4,32,128]{2,1,0:T(8,128)S(1)} %collective-permute-done.4) | copy-start | bytes 196612
  113.1 12.3 %collective-permute-start.5 = (f32[3,32,128]{2,1,0:T(8,128)}, f32[3,32,128]{2,1,0:T(8,128)S(1)}, u32[]{:S(2)}, u32[]{:S(2)}) collective-permute-start(f32[3,32,128]{2,1,0:T(8,128)} %pad_maximum_fusion.14), channel_id=1, source_target_pairs={{0,256},{64,320},{128,384},{192,448},{256,0},{320,64},{384,128},{4... | collective-permute-start | bytes 147464 | tf_op jit(solution)/shard_map/ppermute | solution.py:13
  125.4 15.2 %copy-start.31 = (f32[3,32,128]{2,1,0:T(8,128)}, f32[3,32,128]{2,1,0:T(8,128)S(1)}, u32[]{:S(2)}) copy-start(f32[3,32,128]{2,1,0:T(8,128)S(1)} %collective-permute-done.5) | copy-start | bytes 147460
  127.4 33.2 %copy-start.15 = (f32[1,128,128]{2,1,0:T(8,128)S(1)}, f32[1,128,128]{2,1,0:T(8,128)}, u32[]{:S(2)}) copy-start(f32[1,128,128]{2,1,0:T(8,128)} %get-tuple-element.12) | copy-start | bytes 196612
  127.4 33.2 %copy-start.17 = (f32[1,128,128]{2,1,0:T(8,128)S(1)}, f32[1,128,128]{2,1,0:T(8,128)}, u32[]{:S(2)}) copy-start(f32[1,128,128]{2,1,0:T(8,128)} %get-tuple-element.14) | copy-start | bytes 196612
  127.4 14.5 %collective-permute-start.6 = (f32[2,32,128]{2,1,0:T(8,128)S(1)}, f32[2,32,128]{2,1,0:T(8,128)S(1)}, u32[]{:S(2)}, u32[]{:S(2)}) collective-permute-start(f32[2,32,128]{2,1,0:T(8,128)S(1)} %pad_maximum_fusion.15), channel_id=1, source_target_pairs={{0,512},{64,576},{128,640},{192,704},{256,768},{320,832},{384,896}... | collective-permute-start | bytes 98312 | tf_op jit(solution)/shard_map/ppermute | solution.py:13
  145.7 6.4 %collective-permute-start.7 = (f32[9,32,128]{2,1,0:T(8,128)}, f32[9,32,128]{2,1,0:T(8,128)S(1)}, u32[]{:S(2)}, u32[]{:S(2)}) collective-permute-start(f32[9,32,128]{2,1,0:T(8,128)} %constant_dynamic-update-slice_fusion), channel_id=1, source_target_pairs={{0,16},{16,0},{32,48},{48,32},{1,17},{17,1},{33,49},{49,33},{2,18}... | collective-permute-start | bytes 442376 | tf_op jit(solution)/shard_map/ppermute | solution.py:13
  152.2 20.3 %copy-start.21 = (f32[2,2,128,128]{3,2,1,0:T(8,128)S(1)}, f32[2,2,128,128]{3,2,1,0:T(8,128)}, u32[]{:S(2)}) copy-start(f32[2,2,128,128]{3,2,1,0:T(8,128)} %get-tuple-element.42) | copy-start | bytes 786436
  152.2 20.3 %copy-start.36 = (f32[2,2,1,1]{1,0,3,2:T(2,128)S(1)}, f32[2,2,1,1]{1,0,3,2:T(2,128)}, u32[]{:S(2)}) copy-start(f32[2,2,1,1]{1,0,3,2:T(2,128)} %constant.105) | copy-start | bytes 52
  152.2 8.3 %collective-permute-start.8 = (f32[2,5,32,128]{3,2,1,0:T(8,128)S(1)}, f32[2,5,32,128]{3,2,1,0:T(8,128)S(1)}, u32[]{:S(2)}, u32[]{:S(2)}) collective-permute-start(f32[2,5,32,128]{3,2,1,0:T(8,128)S(1)} %pad_maximum_fusion.8), channel_id=1, source_target_pairs={{0,32},{16,48},{32,0},{48,16},{1,33},{17,49},{33,1},{49,17},{2,34}... | collective-permute-start | bytes 491528 | tf_op jit(solution)/shard_map/ppermute | solution.py:13
  156.8 17.6 %copy-start.7 = (bf16[2,2,256,256]{3,2,1,0:T(8,128)(2,1)S(1)}, bf16[2,2,256,256]{3,2,1,0:T(8,128)(2,1)}, u32[]{:S(2)}) copy-start(bf16[2,2,256,256]{3,2,1,0:T(8,128)(2,1)} %fusion.8) | copy-start | bytes 1572868
  156.8 17.5 %copy-start.10 = (bf16[2,256,2,128]{1,3,2,0:T(8,128)(2,1)S(1)}, bf16[2,256,2,128]{1,3,2,0:T(8,128)(2,1)}, u32[]{:S(2)}) copy-start(bf16[2,256,2,128]{1,3,2,0:T(8,128)(2,1)} %copy.247) | copy-start | bytes 786436
  160.6 17.0 %copy-start.16 = (f32[1,128,128]{2,1,0:T(8,128)S(1)}, f32[1,128,128]{2,1,0:T(8,128)}, u32[]{:S(2)}) copy-start(f32[1,128,128]{2,1,0:T(8,128)} %get-tuple-element.12) | copy-start | bytes 196612
  160.6 17.0 %copy-start.18 = (f32[1,128,128]{2,1,0:T(8,128)S(1)}, f32[1,128,128]{2,1,0:T(8,128)}, u32[]{:S(2)}) copy-start(f32[1,128,128]{2,1,0:T(8,128)} %get-tuple-element.14) | copy-start | bytes 196612
  161.5 16.1 %collective-permute-start.9 = (f32[9,128,128]{2,1,0:T(8,128)}, f32[9,128,128]{2,1,0:T(8,128)}, u32[]{:S(2)}, u32[]{:S(2)}) collective-permute-start(f32[9,128,128]{2,1,0:T(8,128)} %pad_maximum_fusion.5), channel_id=1, source_target_pairs={{0,8},{8,0},{1,9},{9,1},{2,10},{10,2},{3,11},{11,3},{4,12},{12,4},... | collective-permute-start | bytes 1769480 | tf_op jit(solution)/shard_map/ppermute | solution.py:13
  (17 other events, 35.0 us)

commit v5 on v4

--- a/solution.py
+++ b/solution.py
@@ -21,6 +21,24 @@
             end_at = target >> level << level
             level_table[level, target, begin_at:end_at] = 1.0
     return jnp.asarray(level_table)
+
+
+def z_tables(groups):
+    levels = groups.bit_length() - 1
+    choice = np.zeros((groups, groups), np.int32)
+    forward_table = np.zeros((groups, levels, groups), np.float32)
+    backward_table = np.zeros((groups, groups), np.float32)
+    for own in range(groups):
+        for other in range(groups):
+            if other == own:
+                continue
+            level = (own ^ other).bit_length() - 1
+            choice[own, other] = 1 if other > own else 2 + level
+            if other < own:
+                forward_table[own, level, other] = 1.0
+            else:
+                backward_table[own, other] = 1.0
+    return jnp.asarray(choice), jnp.asarray(forward_table), jnp.asarray(backward_table)
 
 
 def body(queries, key_vectors, value_vectors, grad_output, level_weights):
@@ -111,17 +129,16 @@
 
     running = quartered(running + arrived[0])
     pending = quartered(pending[1:] + arrived[2:])
-    grad_z = jnp.zeros_like(running)
-    cross_z = []
-    for z_bit in range(cross_levels - 3):
-        tree_bit = z_bit + 3
-        packet = jnp.concatenate([running[None], pending], axis=0)
-        arrived = swapped(packet, "z", z_bit)
-        cross_z.append(arrived[0] * upper_bits[tree_bit])
-        grad_z = grad_z + (1.0 - upper_bits[tree_bit]) * arrived[1]
-        running = running + arrived[0]
-        pending = pending[1:] + arrived[2:]
-
+    z_count = lax.axis_size("z")
+    z_index = lax.axis_index("z")
+    choice, forward_table, backward_table = z_tables(z_count)
+    options = jnp.concatenate([jnp.zeros_like(running)[None], running[None], pending])
+    chunks = jnp.take(options, lax.dynamic_index_in_dim(choice, z_index, 0, keepdims=False), axis=0)
+    received = lax.all_to_all(chunks, "z", 0, 0, tiled=True)
+    forward_rows = lax.dynamic_index_in_dim(forward_table, z_index, 0, keepdims=False)
+    backward_row = lax.dynamic_index_in_dim(backward_table, z_index, 0, keepdims=False)
+    cross_z = list(jnp.einsum("jg,gpr->jpr", forward_rows, received, precision=lax.Precision.HIGHEST))
+    grad_z = jnp.einsum("g,gpr->pr", backward_row, received, precision=lax.Precision.HIGHEST)
     z_part = jnp.concatenate([jnp.stack(cross_z), grad_z[None]])
     odd_x = x_index % 2 == 1
     high_x = x_index // 2 == 1

time: 198 us -> 182 us (0.919)
  waiting for transfers between devices: 29.7 us -> 45.2 us
  starting transfers between devices: 81.9 us -> 67.2 us
  other arithmetic: 33.6 us -> 19.4 us
  between operations: 5.92 us -> 3.43 us
    ppermute x10 -> x6, starting transfers between devices: 74.2 us -> 41.2 us  [swapped(): return lax.ppermute(value, axis, pairs)]
    all_to_all x0 -> x1, starting transfers between devices: none -> 18.3 us  [body(): received = lax.all_to_all(chunks, 'z', 0, 0, tiled=True)]
    unnamed x14 -> x6, other arithmetic: 16.3 us -> 5.41 us
    ppermute x10 -> x6, waiting for transfers between devices: 13.7 us -> 23 us  [swapped(): return lax.ppermute(value, axis, pairs)]
    all_to_all x0 -> x1, waiting for transfers between devices: none -> 6.3 us  [body(): received = lax.all_to_all(chunks, 'z', 0, 0, tiled=True)]
    dot_general x0 -> x2, matrix products: none -> 2.17 us  [the longest x1 1.1 us: body(): jnp.einsum('g,gpr->pr', backward_row, received, precision=lax.Precision.H...]
    concatenate x7 -> x3, other arithmetic: 3.25 us -> 1.09 us  [body(): packet = jnp.concatenate([running[None], pending], axis=0)]
    unnamed x76 -> x55, local copies, waits for them, and re-layouts: 6.79 us -> 6.81 us
  transfers between devices with their start and end apart: 11 -> 8, of which waited for: 7 -> 7; matrix products, arithmetic and copies ran while one was open for 10% -> 9% of each run, Pallas kernels for 0% -> 0%
where the time goes in v5:
time: 182 us; the launch traced here: 181 us
  starting transfers between devices  67.2 us (37%)
  waiting for transfers between devices  45.2 us (25%)
  local copies, waits for them, and re-layouts  27 us (15%)
  other arithmetic  19.4 us (11%)
  matrix products  18.3 us (10%)
  between operations  3.43 us (2%)
    ppermute x6, starting transfers between devices, swapped(): return lax.ppermute(value, axis, pairs)  41.2 us
    ppermute x6, waiting for transfers between devices, swapped(): return lax.ppermute(value, axis, pairs)  23 us
    all_to_all x1, starting transfers between devices, body(): received = lax.all_to_all(chunks, 'z', 0, 0, tiled=True)  18.3 us
    all_to_all x1, waiting for transfers between devices, body(): lax.all_to_all(stacked, 'head', split_axis=2, concat_axis=0, tiled=True)  16 us
    all_to_all x1, starting transfers between devices, body(): lax.all_to_all(stacked, 'head', split_axis=2, concat_axis=0, tiled=True)  7.65 us
    unnamed x55, local copies, waits for them, and re-layouts  6.81 us
    all_to_all x1, waiting for transfers between devices, body(): received = lax.all_to_all(chunks, 'z', 0, 0, tiled=True)  6.3 us
    unnamed x6, other arithmetic  5.41 us
  transfers between devices with their start and end apart: 8, of which 7 were waited for; matrix products, arithmetic and copies ran while one was open for 9% of the time, Pallas kernels for 0%

profile of v5, /device:TPU:1, one launch (start us, length us, event | category | flops | bytes accessed | tf_op | source)
XLA Modules:
  0.0 180.6 jit_solution(3241368807457105997)
XLA Ops:
  0.6 1.3 pad_maximum_fusion
  2.0 1.4 copy.236
  3.4 2.6 %reshape.211 = bf16[8,2,32768]{2,1,0:T(2,128)(2,1)} reshape(bf16[2048,4,64]{2,1,0:T(4,128)(2,1)S(1)} %bitcast.220) | data formatting | bytes 2097152
  6.0 7.7 %all-to-all-start = ((bf16[8,2,32768]{2,1,0:T(2,128)(2,1)}), bf16[8,2,32768]{2,1,0:T(2,128)(2,1)S(1)}, u32[]{:S(2)}, u32[]{:S(2)}) async-start(bf16[8,2,32768]{2,1,0:T(2,128)(2,1)} %reshape.211), calls=%async_computation | async-start | bytes 2097152 | tf_op jit(solution)/shard_map/all_to_all | solution.py:46
  14.5 16.0 %all-to-all-done = bf16[8,2,32768]{2,1,0:T(2,128)(2,1)S(1)} async-done(((bf16[8,2,32768]{2,1,0:T(2,128)(2,1)}), bf16[8,2,32768]{2,1,0:T(2,128)(2,1)S(1)}, u32[]{:S(2)}, u32[]{:S(2)}) %all-to-all-start) | async-done | bytes 1048608 | tf_op jit(solution)/shard_map/all_to_all | solution.py:46
  30.5 1.4 reshape.212
  31.9 1.2 copy.291
  35.8 1.2 copy.249
  39.0 1.3 broadcast_multiply_fusion
  40.4 2.1 %fusion.80 = (f32[2,128,128]{2,1,0:T(8,128)S(1)}, f32[2,2,128,128]{3,2,1,0:T(8,128)}) fusion(bf16[2,256,2,128]{1,3,2,0:T(8,128)(2,1)} %copy.244, bf16[2,256,2,128]{3,2,1,0:T(2,128)(2,1)S(1)} %reshape_squeeze.10), kind=kOutput, calls=%fused_computation.168 | convolution fusion | flops 33587200 | bytes 917504 | tf_op jit(solution)/shard_map/buhp,buhr->bhpr/dot_general | solution.py:92
  44.2 15.1 %collective-permute-start = (f32[8,2,128,128]{3,2,0,1:T(8,128)}, f32[8,2,128,128]{3,2,0,1:T(8,128)}, u32[]{:S(2)}, u32[]{:S(2)}) collective-permute-start(f32[8,2,128,128]{3,2,0,1:T(8,128)} %pad_maximum_fusion.1), channel_id=1, source_target_pairs={{0,8},{8,0},{1,9},{9,1},{2,10},{10,2},{3,11},{11,3},{4,12},{12,4},... | collective-permute-start | bytes 3145736 | tf_op jit(solution)/shard_map/ppermute | solution.py:13
  59.3 2.6 %collective-permute-done = f32[8,2,128,128]{3,2,0,1:T(8,128)} collective-permute-done((f32[8,2,128,128]{3,2,0,1:T(8,128)}, f32[8,2,128,128]{3,2,0,1:T(8,128)}, u32[]{:S(2)}, u32[]{:S(2)}) %collective-permute-start) | collective-permute-done | bytes 1048608 | tf_op jit(solution)/shard_map/ppermute | solution.py:13
  65.0 2.8 %collective-permute-start.1 = (f32[7,128,128]{2,1,0:T(8,128)S(1)}, f32[7,128,128]{2,1,0:T(8,128)}, u32[]{:S(2)}, u32[]{:S(2)}) collective-permute-start(f32[7,128,128]{2,1,0:T(8,128)S(1)} %pad_maximum_fusion.7), channel_id=1, source_target_pairs={{0,16},{16,0},{32,48},{48,32},{1,17},{17,1},{33,49},{49,33},{2,18}... | collective-permute-start | bytes 1376264 | tf_op jit(solution)/shard_map/ppermute | solution.py:13
  71.2 7.5 %collective-permute-done.1 = f32[7,128,128]{2,1,0:T(8,128)} collective-permute-done((f32[7,128,128]{2,1,0:T(8,128)S(1)}, f32[7,128,128]{2,1,0:T(8,128)}, u32[]{:S(2)}, u32[]{:S(2)}) %collective-permute-start.1) | collective-permute-done | bytes 458784 | tf_op jit(solution)/shard_map/ppermute | solution.py:13
  78.7 2.2 %slice_multiply_fusion.2 = (f32[1,128,128]{2,1,0:T(8,128)}, f32[1,128,128]{2,1,0:T(8,128)S(1)}, f32[1,128,128]{2,1,0:T(8,128)}) fusion(f32[7,128,128]{2,1,0:T(8,128)} %collective-permute-done.1, f32[]{:T(128)} %bitcast.23, f32[1,128,128]{2,1,0:T(8,128)S(1)} %dynamic-slice_add_fusion.2, f32[]{:T(128)S(6)} %sub.15), kind=kLoop, calls=%fused_computation.138 | loop fusion | flops 49152 | bytes 393224 | tf_op jit(solution)/shard_map/mul | solution.py:113
  82.0 4.4 %collective-permute-start.2 = (f32[6,2,32,128]{3,2,1,0:T(8,128)S(1)}, f32[6,2,32,128]{3,2,1,0:T(8,128)S(1)}, u32[]{:S(2)}, u32[]{:S(2)}) collective-permute-start(f32[6,2,32,128]{3,2,1,0:T(8,128)S(1)} %pad_maximum_fusion.10), channel_id=1, source_target_pairs={{0,32},{16,48},{32,0},{48,16},{1,33},{17,49},{33,1},{49,17},{2,34}... | collective-permute-start | bytes 589832 | tf_op jit(solution)/shard_map/ppermute | solution.py:13
  86.4 4.2 %collective-permute-done.2 = f32[6,2,32,128]{3,2,1,0:T(8,128)S(1)} collective-permute-done((f32[6,2,32,128]{3,2,1,0:T(8,128)S(1)}, f32[6,2,32,128]{3,2,1,0:T(8,128)S(1)}, u32[]{:S(2)}, u32[]{:S(2)}) %collective-permute-start.2) | collective-permute-done | bytes 196640 | tf_op jit(solution)/shard_map/ppermute | solution.py:13
  92.7 18.3 %all-to-all-start.1 = ((f32[16,32,128]{2,1,0:T(8,128)}), f32[16,32,128]{2,1,0:T(8,128)S(1)}, u32[]{:S(2)}, u32[]{:S(2)}) async-start(f32[16,32,128]{2,1,0:T(8,128)} %broadcast_select_fusion), calls=%async_computation.1 | async-start | bytes 524288 | tf_op jit(solution)/shard_map/all_to_all | solution.py:137
  115.1 1.3 fusion.9
  117.5 6.3 %all-to-all-done.1 = f32[16,32,128]{2,1,0:T(8,128)S(1)} async-done(((f32[16,32,128]{2,1,0:T(8,128)}), f32[16,32,128]{2,1,0:T(8,128)S(1)}, u32[]{:S(2)}, u32[]{:S(2)}) %all-to-all-start.1) | async-done | bytes 262176 | tf_op jit(solution)/shard_map/all_to_all | solution.py:137
  126.1 3.1 %collective-permute-start.3 = (f32[9,32,128]{2,0,1:T(8,128)S(1)}, f32[9,32,128]{2,0,1:T(8,128)S(1)}, u32[]{:S(2)}, u32[]{:S(2)}) collective-permute-start(f32[9,32,128]{2,0,1:T(8,128)S(1)} %pad_maximum_fusion.8), channel_id=1, source_target_pairs={{0,16},{16,0},{32,48},{48,32},{1,17},{17,1},{33,49},{49,33},{2,18}... | collective-permute-start | bytes 442376 | tf_op jit(solution)/shard_map/ppermute | solution.py:13
  130.4 2.8 %collective-permute-done.3 = f32[9,32,128]{2,0,1:T(8,128)S(1)} collective-permute-done((f32[9,32,128]{2,0,1:T(8,128)S(1)}, f32[9,32,128]{2,0,1:T(8,128)S(1)}, u32[]{:S(2)}, u32[]{:S(2)}) %collective-permute-start.3) | collective-permute-done | bytes 147488 | tf_op jit(solution)/shard_map/ppermute | solution.py:13
  133.3 4.6 %collective-permute-start.4 = (f32[2,5,32,128]{3,1,2,0:T(8,128)S(1)}, f32[2,5,32,128]{3,1,2,0:T(8,128)S(1)}, u32[]{:S(2)}, u32[]{:S(2)}) collective-permute-start(f32[2,5,32,128]{3,1,2,0:T(8,128)S(1)} %pad_maximum_fusion.9), channel_id=1, source_target_pairs={{0,32},{16,48},{32,0},{48,16},{1,33},{17,49},{33,1},{49,17},{2,34}... | collective-permute-start | bytes 491528 | tf_op jit(solution)/shard_map/ppermute | solution.py:13
  138.1 5.9 %collective-permute-done.4 = f32[2,5,32,128]{3,1,2,0:T(8,128)S(1)} collective-permute-done((f32[2,5,32,128]{3,1,2,0:T(8,128)S(1)}, f32[2,5,32,128]{3,1,2,0:T(8,128)S(1)}, u32[]{:S(2)}, u32[]{:S(2)}) %collective-permute-start.4) | collective-permute-done | bytes 163872 | tf_op jit(solution)/shard_map/ppermute | solution.py:13
  144.2 11.2 %collective-permute-start.5 = (f32[9,128,128]{2,1,0:T(8,128)S(1)}, f32[9,128,128]{2,1,0:T(8,128)}, u32[]{:S(2)}, u32[]{:S(2)}) collective-permute-start(f32[9,128,128]{2,1,0:T(8,128)S(1)} %pad_maximum_fusion.5), channel_id=1, source_target_pairs={{0,8},{8,0},{1,9},{9,1},{2,10},{10,2},{3,11},{11,3},{4,12},{12,4},... | collective-permute-start | bytes 1769480 | tf_op jit(solution)/shard_map/ppermute | solution.py:13
  155.5 1.8 fusion.19
  157.2 1.7 copy.260
  159.9 2.3 %fusion.67 = bf16[7,2,128,128]{3,2,1,0:T(8,128)(2,1)} fusion(f32[8,2,128,128]{3,2,0,1:T(8,128)} %collective-permute-done, f32[]{:T(128)} %bitcast.20), kind=kLoop, calls=%fused_computation.127 | loop fusion | flops 32767 | bytes 262148
  165.5 1.3 fusion.17
  167.0 1.3 fusion.16
  172.9 1.3 copy.259
  176.3 2.0 %fusion = f32[2,256,2,128]{1,3,2,0:T(8,128)S(1)} fusion(f32[2,8,256,2]{2,1,3,0:T(8,128)S(1)} %bitcast.247, bf16[2,7,2,128,128]{3,4,1,2,0:T(8,128)(2,1)} %copy-done.12, bf16[2,1,2,128,128]{3,4,1,2,0:T(8,128)(2,1)S(1)} %copy-done.21, bf16[2,256,2,128,1]{3,2,1,0,4:T(2,128)(2,1)S(1)} %bitcast.224), kind=kOutput, calls=%fused_computation.2 | convolution fusion | flops 272498688 | bytes 1867776 | tf_op jit(solution)/shard_map/bmhpr,bthr->bmthp/dot_general | solution.py:173
  (136 shorter events, 37.0 us)
Async XLA Ops:
  3.4 10.3 %copy-start.23 = (s32[9,2,512]{2,1,0:T(2,128)S(1)}, s32[9,2,512]{2,1,0:T(2,128)}, u32[]{:S(2)}) copy-start(s32[9,2,512]{2,1,0:T(2,128)} %param.14) | copy-start | bytes 110596
  3.4 10.3 %copy-start.24 = (f32[9]{0:T(128)S(1)}, f32[9]{0:T(128)}, u32[]{:S(2)}) copy-start(f32[9]{0:T(128)} %constant.141) | copy-start | bytes 112
  6.0 24.4 %all-to-all-start = ((bf16[8,2,32768]{2,1,0:T(2,128)(2,1)}), bf16[8,2,32768]{2,1,0:T(2,128)(2,1)S(1)}, u32[]{:S(2)}, u32[]{:S(2)}) async-start(bf16[8,2,32768]{2,1,0:T(2,128)(2,1)} %reshape.211), calls=%async_computation | async-start | bytes 2097152 | tf_op jit(solution)/shard_map/all_to_all | solution.py:46
  14.5 19.9 %copy-start.19 = (f32[8,2,2,256]{3,0,1,2:T(8,128)}, f32[8,2,2,256]{3,0,1,2:T(8,128)S(1)}, u32[]{:S(2)}) copy-start(f32[8,2,2,256]{3,0,1,2:T(8,128)S(1)} %copy.338) | copy-start | bytes 98308
  35.7 1.4 copy-start.11
  37.2 0.9 copy-start.4
  40.4 18.9 %copy-start = (f32[7,2,128,128]{3,2,0,1:T(8,128)}, f32[7,2,128,128]{3,2,0,1:T(8,128)S(1)}, u32[]{:S(2)}) copy-start(f32[7,2,128,128]{3,2,0,1:T(8,128)S(1)} %broadcast_multiply_fusion) | copy-start | bytes 2752516
  44.2 17.7 %collective-permute-start = (f32[8,2,128,128]{3,2,0,1:T(8,128)}, f32[8,2,128,128]{3,2,0,1:T(8,128)}, u32[]{:S(2)}, u32[]{:S(2)}) collective-permute-start(f32[8,2,128,128]{3,2,0,1:T(8,128)} %pad_maximum_fusion.1), channel_id=1, source_target_pairs={{0,8},{8,0},{1,9},{9,1},{2,10},{10,2},{3,11},{11,3},{4,12},{12,4},... | collective-permute-start | bytes 3145736 | tf_op jit(solution)/shard_map/ppermute | solution.py:13
  61.9 3.0 %slice-start = ((f32[7,2,128,128]{3,2,0,1:T(8,128)}), f32[6,2,128,128]{3,2,0,1:T(8,128)S(1)}, s32[]{:S(2)}) async-start(f32[7,2,128,128]{3,2,0,1:T(8,128)} %copy-done), calls=%async_computation.2 | async-start | bytes 1572864 | tf_op jit(solution)/shard_map/slice | solution.py:110
  65.0 13.7 %collective-permute-start.1 = (f32[7,128,128]{2,1,0:T(8,128)S(1)}, f32[7,128,128]{2,1,0:T(8,128)}, u32[]{:S(2)}, u32[]{:S(2)}) collective-permute-start(f32[7,128,128]{2,1,0:T(8,128)S(1)} %pad_maximum_fusion.7), channel_id=1, source_target_pairs={{0,16},{16,0},{32,48},{48,32},{1,17},{17,1},{33,49},{49,33},{2,18}... | collective-permute-start | bytes 1376264 | tf_op jit(solution)/shard_map/ppermute | solution.py:13
  81.9 31.4 %copy-start.2 = (bf16[2,256,2,128]{3,2,1,0:T(2,128)(2,1)S(1)}, bf16[2,256,2,128]{3,2,1,0:T(2,128)(2,1)}, u32[]{:S(2)}) copy-start(bf16[2,256,2,128]{3,2,1,0:T(2,128)(2,1)} %copy-done.1) | copy-start | bytes 786436
  82.0 8.6 %collective-permute-start.2 = (f32[6,2,32,128]{3,2,1,0:T(8,128)S(1)}, f32[6,2,32,128]{3,2,1,0:T(8,128)S(1)}, u32[]{:S(2)}, u32[]{:S(2)}) collective-permute-start(f32[6,2,32,128]{3,2,1,0:T(8,128)S(1)} %pad_maximum_fusion.10), channel_id=1, source_target_pairs={{0,32},{16,48},{32,0},{48,16},{1,33},{17,49},{33,1},{49,17},{2,34}... | collective-permute-start | bytes 589832 | tf_op jit(solution)/shard_map/ppermute | solution.py:13
  92.7 31.1 %all-to-all-start.1 = ((f32[16,32,128]{2,1,0:T(8,128)}), f32[16,32,128]{2,1,0:T(8,128)S(1)}, u32[]{:S(2)}, u32[]{:S(2)}) async-start(f32[16,32,128]{2,1,0:T(8,128)} %broadcast_select_fusion), calls=%async_computation.1 | async-start | bytes 524288 | tf_op jit(solution)/shard_map/all_to_all | solution.py:137
  112.5 5.0 %copy-start.22 = (pred[256,256]{1,0:T(8,128)(4,1)}, pred[256,256]{1,0:T(8,128)(4,1)S(1)}, u32[]{:S(2)}) copy-start(pred[256,256]{1,0:T(8,128)(4,1)S(1)} %iota_compare_fusion) | copy-start | bytes 196612
  114.2 2.2 %copy-start.9 = (bf16[2,256,2,128]{1,3,2,0:T(8,128)(2,1)S(1)}, bf16[2,256,2,128]{1,3,2,0:T(8,128)(2,1)}, u32[]{:S(2)}) copy-start(bf16[2,256,2,128]{1,3,2,0:T(8,128)(2,1)} %copy.270) | copy-start | bytes 786436
  115.1 14.2 %copy-start.5 = (bf16[2,256,2,128]{3,2,1,0:T(2,128)(2,1)S(1)}, bf16[2,256,2,128]{3,2,1,0:T(2,128)(2,1)}, u32[]{:S(2)}) copy-start(bf16[2,256,2,128]{3,2,1,0:T(2,128)(2,1)} %copy-done.4) | copy-start | bytes 786436
  126.1 7.1 %collective-permute-start.3 = (f32[9,32,128]{2,0,1:T(8,128)S(1)}, f32[9,32,128]{2,0,1:T(8,128)S(1)}, u32[]{:S(2)}, u32[]{:S(2)}) collective-permute-start(f32[9,32,128]{2,0,1:T(8,128)S(1)} %pad_maximum_fusion.8), channel_id=1, source_target_pairs={{0,16},{16,0},{32,48},{48,32},{1,17},{17,1},{33,49},{49,33},{2,18}... | collective-permute-start | bytes 442376 | tf_op jit(solution)/shard_map/ppermute | solution.py:13
  130.4 28.5 %copy-start.6 = (bf16[2,2,256,256]{3,2,1,0:T(8,128)(2,1)}, bf16[2,2,256,256]{3,2,1,0:T(8,128)(2,1)S(1)}, u32[]{:S(2)}) copy-start(bf16[2,2,256,256]{3,2,1,0:T(8,128)(2,1)S(1)} %fusion.8) | copy-start | bytes 1572868
  133.3 10.9 %copy-start.14 = (f32[1,128,128]{2,1,0:T(8,128)S(1)}, f32[1,128,128]{2,1,0:T(8,128)}, u32[]{:S(2)}) copy-start(f32[1,128,128]{2,1,0:T(8,128)} %get-tuple-element.12) | copy-start | bytes 196612
  133.3 10.9 %copy-start.15 = (f32[1,128,128]{2,1,0:T(8,128)S(1)}, f32[1,128,128]{2,1,0:T(8,128)}, u32[]{:S(2)}) copy-start(f32[1,128,128]{2,1,0:T(8,128)} %get-tuple-element.14) | copy-start | bytes 196612
  133.3 10.6 %collective-permute-start.4 = (f32[2,5,32,128]{3,1,2,0:T(8,128)S(1)}, f32[2,5,32,128]{3,1,2,0:T(8,128)S(1)}, u32[]{:S(2)}, u32[]{:S(2)}) collective-permute-start(f32[2,5,32,128]{3,1,2,0:T(8,128)S(1)} %pad_maximum_fusion.9), channel_id=1, source_target_pairs={{0,32},{16,48},{32,0},{48,16},{1,33},{17,49},{33,1},{49,17},{2,34}... | collective-permute-start | bytes 491528 | tf_op jit(solution)/shard_map/ppermute | solution.py:13
  138.1 17.4 %copy-start.16 = (f32[2,2,128,128]{3,2,1,0:T(8,128)S(1)}, f32[2,2,128,128]{3,2,1,0:T(8,128)}, u32[]{:S(2)}) copy-start(f32[2,2,128,128]{3,2,1,0:T(8,128)} %get-tuple-element.30) | copy-start | bytes 786436
  138.1 17.4 %copy-start.25 = (f32[2,2,1,1]{1,0,3,2:T(2,128)S(1)}, f32[2,2,1,1]{1,0,3,2:T(2,128)}, u32[]{:S(2)}) copy-start(f32[2,2,1,1]{1,0,3,2:T(2,128)} %constant.143) | copy-start | bytes 52
  144.0 14.9 %copy-start.8 = (bf16[2,256,2,128]{1,3,2,0:T(8,128)(2,1)S(1)}, bf16[2,256,2,128]{1,3,2,0:T(8,128)(2,1)}, u32[]{:S(2)}) copy-start(bf16[2,256,2,128]{1,3,2,0:T(8,128)(2,1)} %copy.278) | copy-start | bytes 786436
  144.2 18.0 %collective-permute-start.5 = (f32[9,128,128]{2,1,0:T(8,128)S(1)}, f32[9,128,128]{2,1,0:T(8,128)}, u32[]{:S(2)}, u32[]{:S(2)}) collective-permute-start(f32[9,128,128]{2,1,0:T(8,128)S(1)} %pad_maximum_fusion.5), channel_id=1, source_target_pairs={{0,8},{8,0},{1,9},{9,1},{2,10},{10,2},{3,11},{11,3},{4,12},{12,4},... | collective-permute-start | bytes 1769480 | tf_op jit(solution)/shard_map/ppermute | solution.py:13
  159.9 4.4 %copy-start.17 = (f32[2,2,128,128]{3,0,2,1:T(2,128)S(1)}, f32[2,2,128,128]{3,0,2,1:T(2,128)}, u32[]{:S(2)}) copy-start(f32[2,2,128,128]{3,0,2,1:T(2,128)} %copy.271) | copy-start | bytes 786436
  171.7 2.8 %copy-start.20 = (f32[8,2,2,256]{3,0,1,2:T(8,128)S(1)}, f32[8,2,2,256]{3,0,1,2:T(8,128)}, u32[]{:S(2)}) copy-start(f32[8,2,2,256]{3,0,1,2:T(8,128)} %copy-done.19) | copy-start | bytes 98308
  171.7 2.8 %copy-start.21 = (bf16[2,1,2,128,128]{3,4,1,2,0:T(8,128)(2,1)S(1)}, bf16[2,1,2,128,128]{3,4,1,2,0:T(8,128)(2,1)}, u32[]{:S(2)}) copy-start(bf16[2,1,2,128,128]{3,4,1,2,0:T(8,128)(2,1)} %copy.260) | copy-start | bytes 393220
  174.5 0.9 copy-start.12
  174.5 1.4 copy-start.7
  176.2 2.2 %copy-start.3 = (bf16[2,256,2,128]{1,3,2,0:T(8,128)(2,1)S(1)}, bf16[2,256,2,128]{1,3,2,0:T(8,128)(2,1)}, u32[]{:S(2)}) copy-start(bf16[2,256,2,128]{1,3,2,0:T(8,128)(2,1)} %copy.244) | copy-start | bytes 786436
  176.3 2.5 %copy-start.10 = (bf16[2,256,2,128]{3,2,1,0:T(2,128)(2,1)S(1)}, bf16[2,256,2,128]{3,2,1,0:T(2,128)(2,1)}, u32[]{:S(2)}) copy-start(bf16[2,256,2,128]{3,2,1,0:T(2,128)(2,1)} %copy.281) | copy-start | bytes 786436
  (3 other events, 2.0 us)

commit v6 on v5

--- a/solution.py
+++ b/solution.py
@@ -139,25 +139,23 @@
     backward_row = lax.dynamic_index_in_dim(backward_table, z_index, 0, keepdims=False)
     cross_z = list(jnp.einsum("jg,gpr->jpr", forward_rows, received, precision=lax.Precision.HIGHEST))
     grad_z = jnp.einsum("g,gpr->pr", backward_row, received, precision=lax.Precision.HIGHEST)
-    z_part = jnp.concatenate([jnp.stack(cross_z), grad_z[None]])
     odd_x = x_index % 2 == 1
-    high_x = x_index // 2 == 1
-    pair_part = swapped(jnp.concatenate([z_part, jnp.stack([cross_x2, grad_x2]).reshape(-1, head_size // 4, head_size)]), "x", 0)
-    z_levels = z_part.shape[0]
 
     def ordered(own, other, other_first):
         return jnp.stack([jnp.where(other_first, other, own), jnp.where(other_first, own, other)])
 
-    z_half = ordered(z_part, pair_part[:z_levels], odd_x)
-    level_two = ordered(jnp.stack([cross_x2, grad_x2]), pair_part[z_levels:].reshape(2, 2, head_size // 4, head_size), odd_x)
+    half_two = jnp.stack([cross_x2, grad_x2])
+    level_two = ordered(half_two, swapped(half_two, "x", 0), odd_x)
     level_two = level_two.transpose(1, 2, 0, 3, 4).reshape(2, head_size, head_size)
-    z_full = ordered(z_half, swapped(z_half, "x", 1), high_x)
-    z_full = z_full.transpose(2, 0, 1, 3, 4).reshape(z_levels, head_size, head_size)
-    own_levels = jnp.concatenate([jnp.stack([cross_x1, grad_x1]), level_two, z_full])
-    both_heads = ordered(own_levels, swapped(own_levels, "core", 0), core_index == 1)
-    device_grad = grad_first + both_heads[:, 1] + both_heads[:, 3] + both_heads[:, -1]
-    cross_list = [cross_first, both_heads[:, 0], both_heads[:, 2]] + [
-        both_heads[:, 4 + level] for level in range(cross_levels - 3)
+    own_levels = jnp.concatenate([jnp.stack([cross_x1, grad_x1]), level_two])
+    near_levels = ordered(own_levels, swapped(own_levels, "core", 0), core_index == 1)
+    z_part = jnp.concatenate([jnp.stack(cross_z), grad_z[None]])
+    spread = jnp.broadcast_to(z_part[None], (8,) + z_part.shape)
+    z_levels = lax.all_to_all(spread, ("x", "core"), 0, 0, tiled=True).reshape((4, 2) + z_part.shape)
+    z_levels = z_levels.transpose(1, 2, 0, 3, 4).reshape(2, z_part.shape[0], head_size, head_size)
+    device_grad = grad_first + near_levels[:, 1] + near_levels[:, 3] + z_levels[:, -1]
+    cross_list = [cross_first, near_levels[:, 0], near_levels[:, 2]] + [
+        z_levels[:, level] for level in range(cross_levels - 3)
     ]
     level_table = bucket_table(per_dev, local_levels)
     local_buckets = jnp.einsum(

time: 182 us -> 170 us (0.934)
  waiting for transfers between devices: 45.2 us -> 36.4 us
  local copies, waits for them, and re-layouts: 27 us -> 32.6 us
  other arithmetic: 19.4 us -> 14.1 us
    ppermute x6 -> x5, starting transfers between devices: 41.2 us -> 29.5 us  [swapped(): return lax.ppermute(value, axis, pairs)]
    all_to_all x0 -> x1, starting transfers between devices: none -> 9.79 us  [body(): lax.all_to_all(spread, ('x', 'core'), 0, 0, tiled=True)]
    ppermute x6 -> x5, waiting for transfers between devices: 23 us -> 13.6 us  [swapped(): return lax.ppermute(value, axis, pairs)]
    all_to_all x0 -> x1, waiting for transfers between devices: none -> 7.39 us  [body(): lax.all_to_all(spread, ('x', 'core'), 0, 0, tiled=True)]
    all_to_all x1, waiting for transfers between devices: 6.3 us -> 0.01 us  [body(): received = lax.all_to_all(chunks, 'z', 0, 0, tiled=True)]
    unnamed x55 -> x56, local copies, waits for them, and re-layouts: 6.81 us -> 11.1 us
    another operation x4, local copies, waits for them, and re-layouts: 2.19 us -> 4.36 us
    unnamed x6 -> x3, other arithmetic: 5.41 us -> 3.43 us
  transfers between devices with their start and end apart: 8 -> 8, of which waited for: 7 -> 4; matrix products, arithmetic and copies ran while one was open for 9% -> 14% of each run, Pallas kernels for 0% -> 0%
where the time goes in v6:
time: 170 us; the launch traced here: 169 us
  starting transfers between devices  65.4 us (38%)
  waiting for transfers between devices  36.4 us (21%)
  local copies, waits for them, and re-layouts  32.6 us (19%)
  matrix products  17.3 us (10%)
  other arithmetic  14.1 us (8%)
  between operations  3.27 us (2%)
    ppermute x5, starting transfers between devices, swapped(): return lax.ppermute(value, axis, pairs)  29.5 us
    all_to_all x1, starting transfers between devices, body(): received = lax.all_to_all(chunks, 'z', 0, 0, tiled=True)  18.5 us
    all_to_all x1, waiting for transfers between devices, body(): lax.all_to_all(stacked, 'head', split_axis=2, concat_axis=0, tiled=True)  15.4 us
    ppermute x5, waiting for transfers between devices, swapped(): return lax.ppermute(value, axis, pairs)  13.6 us
    unnamed x56, local copies, waits for them, and re-layouts  11.1 us
    all_to_all x1, starting transfers between devices, body(): lax.all_to_all(spread, ('x', 'core'), 0, 0, tiled=True)  9.79 us
    all_to_all x1, starting transfers between devices, body(): lax.all_to_all(stacked, 'head', split_axis=2, concat_axis=0, tiled=True)  7.65 us
    all_to_all x1, waiting for transfers between devices, body(): lax.all_to_all(spread, ('x', 'core'), 0, 0, tiled=True)  7.39 us
  transfers between devices with their start and end apart: 8, of which 4 were waited for; matrix products, arithmetic and copies ran while one was open for 14% of the time, Pallas kernels for 0%

profile of v6, /device:TPU:1, one launch (start us, length us, event | category | flops | bytes accessed | tf_op | source)
XLA Modules:
  0.0 169.2 jit_solution(13312705914244783562)
XLA Ops:
  0.6 1.3 pad_maximum_fusion
  2.0 1.4 copy.239
  3.4 2.7 %reshape.136 = bf16[8,2,32768]{2,1,0:T(2,128)(2,1)} reshape(bf16[2048,4,64]{2,1,0:T(4,128)(2,1)S(1)} %bitcast.221) | data formatting | bytes 2097152
  6.0 7.7 %all-to-all-start = ((bf16[8,2,32768]{2,1,0:T(2,128)(2,1)}), bf16[8,2,32768]{2,1,0:T(2,128)(2,1)S(1)}, u32[]{:S(2)}, u32[]{:S(2)}) async-start(bf16[8,2,32768]{2,1,0:T(2,128)(2,1)} %reshape.136), calls=%async_computation | async-start | bytes 2097152 | tf_op jit(solution)/shard_map/all_to_all | solution.py:46
  15.1 15.4 %all-to-all-done = bf16[8,2,32768]{2,1,0:T(2,128)(2,1)S(1)} async-done(((bf16[8,2,32768]{2,1,0:T(2,128)(2,1)}), bf16[8,2,32768]{2,1,0:T(2,128)(2,1)S(1)}, u32[]{:S(2)}, u32[]{:S(2)}) %all-to-all-start) | async-done | bytes 1048608 | tf_op jit(solution)/shard_map/all_to_all | solution.py:46
  30.5 1.4 reshape.137
  31.9 1.2 copy.296
  35.9 1.2 copy.252
  37.2 1.9 %fusion.66 = (f32[2,128,128]{2,1,0:T(8,128)S(1)}, f32[2,2,128,128]{3,2,1,0:T(8,128)}) fusion(bf16[2,256,2,128]{1,3,2,0:T(8,128)(2,1)} %copy.247, bf16[2,256,2,128]{3,2,1,0:T(2,128)(2,1)S(1)} %reshape_squeeze.10), kind=kOutput, calls=%fused_computation.143 | convolution fusion | flops 33587200 | bytes 917504 | tf_op jit(solution)/shard_map/buhp,buhr->bhpr/dot_general | solution.py:92
  39.0 1.4 broadcast_multiply_fusion
  41.6 15.1 %collective-permute-start = (f32[8,2,128,128]{3,2,0,1:T(8,128)}, f32[8,2,128,128]{3,2,0,1:T(8,128)}, u32[]{:S(2)}, u32[]{:S(2)}) collective-permute-start(f32[8,2,128,128]{3,2,0,1:T(8,128)} %pad_maximum_fusion.1), channel_id=1, source_target_pairs={{0,8},{8,0},{1,9},{9,1},{2,10},{10,2},{3,11},{11,3},{4,12},{12,4},... | collective-permute-start | bytes 3145736 | tf_op jit(solution)/shard_map/ppermute | solution.py:13
  62.8 1.8 %copy.275 = bf16[2,256,2,128]{1,3,2,0:T(8,128)(2,1)} copy(bf16[2,256,2,128]{3,2,1,0:T(2,128)(2,1)} %copy-done.1) | data formatting | bytes 524288 | tf_op jit(solution)/shard_map/reshape;squeeze | solution.py:57
  64.6 1.5 fusion.8
  68.4 2.8 %collective-permute-start.1 = (f32[7,128,128]{2,1,0:T(8,128)S(1)}, f32[7,128,128]{2,1,0:T(8,128)S(1)}, u32[]{:S(2)}, u32[]{:S(2)}) collective-permute-start(f32[7,128,128]{2,1,0:T(8,128)S(1)} %pad_maximum_fusion.5), channel_id=1, source_target_pairs={{0,16},{16,0},{32,48},{48,32},{1,17},{17,1},{33,49},{49,33},{2,18}... | collective-permute-start | bytes 1376264 | tf_op jit(solution)/shard_map/ppermute | solution.py:13
  73.5 9.0 %collective-permute-done.1 = f32[7,128,128]{2,1,0:T(8,128)S(1)} collective-permute-done((f32[7,128,128]{2,1,0:T(8,128)S(1)}, f32[7,128,128]{2,1,0:T(8,128)S(1)}, u32[]{:S(2)}, u32[]{:S(2)}) %collective-permute-start.1) | collective-permute-done | bytes 458784 | tf_op jit(solution)/shard_map/ppermute | solution.py:13
  82.5 1.3 slice_multiply_fusion.2
  83.9 4.4 %collective-permute-start.2 = (f32[6,2,32,128]{3,2,1,0:T(8,128)S(1)}, f32[6,2,32,128]{3,2,1,0:T(8,128)S(1)}, u32[]{:S(2)}, u32[]{:S(2)}) collective-permute-start(f32[6,2,32,128]{3,2,1,0:T(8,128)S(1)} %pad_maximum_fusion.7), channel_id=1, source_target_pairs={{0,32},{16,48},{32,0},{48,16},{1,33},{17,49},{33,1},{49,17},{2,34}... | collective-permute-start | bytes 589832 | tf_op jit(solution)/shard_map/ppermute | solution.py:13
  88.3 4.6 %collective-permute-done.2 = f32[6,2,32,128]{3,2,1,0:T(8,128)S(1)} collective-permute-done((f32[6,2,32,128]{3,2,1,0:T(8,128)S(1)}, f32[6,2,32,128]{3,2,1,0:T(8,128)S(1)}, u32[]{:S(2)}, u32[]{:S(2)}) %collective-permute-start.2) | collective-permute-done | bytes 196640 | tf_op jit(solution)/shard_map/ppermute | solution.py:13
  95.6 18.5 %all-to-all-start.1 = ((f32[16,32,128]{2,1,0:T(8,128)}), f32[16,32,128]{2,1,0:T(8,128)S(1)}, u32[]{:S(2)}, u32[]{:S(2)}) async-start(f32[16,32,128]{2,1,0:T(8,128)} %broadcast_select_fusion), calls=%async_computation.1 | async-start | bytes 524288 | tf_op jit(solution)/shard_map/all_to_all | solution.py:137
  114.8 2.2 %fusion.67 = f32[2,2,128,256]{3,2,1,0:T(8,128)} fusion(bf16[2,256,2,128]{1,3,2,0:T(8,128)(2,1)} %copy.275, bf16[2,2,256,256]{3,2,1,0:T(8,128)(2,1)} %fusion.9), kind=kOutput, calls=%fused_computation.144 | convolution fusion | flops 67108864 | bytes 1310720 | tf_op jit(solution)/shard_map/bhtu,bthp->buhp/dot_general | solution.py:86
  117.0 3.1 %collective-permute-start.3 = (f32[2,2,32,128]{3,2,1,0:T(8,128)S(1)}, f32[2,2,32,128]{3,2,1,0:T(8,128)S(1)}, u32[]{:S(2)}, u32[]{:S(2)}) collective-permute-start(f32[2,2,32,128]{3,2,1,0:T(8,128)S(1)} %pad_maximum_fusion.11), channel_id=1, source_target_pairs={{0,16},{16,0},{32,48},{48,32},{1,17},{17,1},{33,49},{49,33},{2,18}... | collective-permute-start | bytes 196616 | tf_op jit(solution)/shard_map/ppermute | solution.py:13
  120.2 2.1 %fusion.19 = bf16[2,1,2,128,128]{4,0,3,2,1:T(2,128)(2,1)S(1)} fusion(f32[2,2,1,1]{1,0,3,2:T(2,128)S(1)} %copy-done.24, f32[2,2,128,128]{3,2,1,0:T(8,128)} %get-tuple-element.26), kind=kOutput, calls=%fused_computation.32 | convolution fusion | flops 1638400 | bytes 393232 | tf_op jit(solution)/shard_map/mji,ihpr->jmhpr/dot_general | solution.py:161
  124.0 4.2 %collective-permute-start.4 = (f32[4,128,128]{2,1,0:T(8,128)S(1)}, f32[4,128,128]{2,1,0:T(8,128)S(1)}, u32[]{:S(2)}, u32[]{:S(2)}) collective-permute-start(f32[4,128,128]{2,1,0:T(8,128)S(1)} %pad_maximum_fusion.6), channel_id=1, source_target_pairs={{0,8},{8,0},{1,9},{9,1},{2,10},{10,2},{3,11},{11,3},{4,12},{12,4},... | collective-permute-start | bytes 786440 | tf_op jit(solution)/shard_map/ppermute | solution.py:13
  131.3 9.8 %all-to-all-start.2 = ((f32[8,5,32,128]{3,2,1,0:T(8,128)}), f32[8,5,32,128]{3,2,1,0:T(8,128)S(1)}, u32[]{:S(2)}, u32[]{:S(2)}) async-start(f32[8,5,32,128]{3,2,1,0:T(8,128)} %broadcast_in_dim.59), calls=%async_computation.2 | async-start | bytes 1310720 | tf_op jit(solution)/shard_map/all_to_all | solution.py:154
  141.1 2.2 %fusion.53 = bf16[7,2,128,128]{3,2,1,0:T(8,128)(2,1)} fusion(f32[8,2,128,128]{3,2,0,1:T(8,128)} %collective-permute-done, f32[]{:T(128)} %bitcast.20), kind=kLoop, calls=%fused_computation.103 | loop fusion | flops 32767 | bytes 262148
  144.6 7.4 %all-to-all-done.2 = f32[8,5,32,128]{3,2,1,0:T(8,128)S(1)} async-done(((f32[8,5,32,128]{3,2,1,0:T(8,128)}), f32[8,5,32,128]{3,2,1,0:T(8,128)S(1)}, u32[]{:S(2)}, u32[]{:S(2)}) %all-to-all-start.2) | async-done | bytes 655392 | tf_op jit(solution)/shard_map/all_to_all | solution.py:154
  153.8 2.0 %fusion.20 = bf16[2,2,128,128]{3,0,2,1:T(2,128)(2,1)S(1)} fusion(f32[2,2,128,128]{3,0,2,1:T(2,128)} %copy.276, f32[2,2,1,1]{1,0,3,2:T(2,128)S(1)} %copy-done.24, f32[2,128,128]{2,1,0:T(8,128)S(1)} %fusion.41), kind=kOutput, calls=%fused_computation.33 | convolution fusion | flops 1703936 | bytes 524304 | tf_op jit(solution)/shard_map/mji,jmhpr->ihpr/dot_general | solution.py:175
  156.9 1.5 fusion.52
  158.4 1.5 fusion.51
  160.0 1.5 fusion.50
  161.5 1.5 fusion.49
  163.0 1.3 copy.264
  (130 shorter events, 31.1 us)
Async XLA Ops:
  3.4 10.3 %copy-start.22 = (s32[9,2,512]{2,1,0:T(2,128)S(1)}, s32[9,2,512]{2,1,0:T(2,128)}, u32[]{:S(2)}) copy-start(s32[9,2,512]{2,1,0:T(2,128)} %param.14) | copy-start | bytes 110596
  3.4 10.3 %copy-start.23 = (f32[9]{0:T(128)S(1)}, f32[9]{0:T(128)}, u32[]{:S(2)}) copy-start(f32[9]{0:T(128)} %constant.139) | copy-start | bytes 112
  6.0 24.4 %all-to-all-start = ((bf16[8,2,32768]{2,1,0:T(2,128)(2,1)}), bf16[8,2,32768]{2,1,0:T(2,128)(2,1)S(1)}, u32[]{:S(2)}, u32[]{:S(2)}) async-start(bf16[8,2,32768]{2,1,0:T(2,128)(2,1)} %reshape.136), calls=%async_computation | async-start | bytes 2097152 | tf_op jit(solution)/shard_map/all_to_all | solution.py:46
  33.2 1.9 %copy-start.18 = (f32[8,2,2,256]{3,0,1,2:T(8,128)S(1)}, f32[8,2,2,256]{3,0,1,2:T(8,128)}, u32[]{:S(2)}) copy-start(f32[8,2,2,256]{3,0,1,2:T(8,128)} %copy.346) | copy-start | bytes 98308
  33.5 1.1 copy-start.4
  39.0 1.4 copy-start.12
  40.4 24.2 %copy-start = (f32[7,2,128,128]{3,2,0,1:T(8,128)}, f32[7,2,128,128]{3,2,0,1:T(8,128)S(1)}, u32[]{:S(2)}) copy-start(f32[7,2,128,128]{3,2,0,1:T(8,128)S(1)} %broadcast_multiply_fusion) | copy-start | bytes 2752516
  41.6 24.5 %collective-permute-start = (f32[8,2,128,128]{3,2,0,1:T(8,128)}, f32[8,2,128,128]{3,2,0,1:T(8,128)}, u32[]{:S(2)}, u32[]{:S(2)}) collective-permute-start(f32[8,2,128,128]{3,2,0,1:T(8,128)} %pad_maximum_fusion.1), channel_id=1, source_target_pairs={{0,8},{8,0},{1,9},{9,1},{2,10},{10,2},{3,11},{11,3},{4,12},{12,4},... | collective-permute-start | bytes 3145736 | tf_op jit(solution)/shard_map/ppermute | solution.py:13
  64.6 2.5 %copy-start.13 = (f32[2,128,128]{2,1,0:T(8,128)S(1)}, f32[2,128,128]{2,1,0:T(8,128)}, u32[]{:S(2)}) copy-start(f32[2,128,128]{2,1,0:T(8,128)} %copy-done.12) | copy-start | bytes 393220
  64.6 3.7 %slice-start = ((f32[7,2,128,128]{3,2,0,1:T(8,128)}), f32[6,2,128,128]{3,2,0,1:T(8,128)S(1)}, s32[]{:S(2)}) async-start(f32[7,2,128,128]{3,2,0,1:T(8,128)} %copy-done), calls=%async_computation.3 | async-start | bytes 1572864 | tf_op jit(solution)/shard_map/slice | solution.py:110
  66.1 5.2 %copy-start.10 = (bf16[2,256,2,128]{1,3,2,0:T(8,128)(2,1)S(1)}, bf16[2,256,2,128]{1,3,2,0:T(8,128)(2,1)}, u32[]{:S(2)}) copy-start(bf16[2,256,2,128]{1,3,2,0:T(8,128)(2,1)} %copy.283) | copy-start | bytes 786436
  66.1 5.2 %copy-start.21 = (pred[256,256]{1,0:T(8,128)(4,1)S(1)}, pred[256,256]{1,0:T(8,128)(4,1)}, u32[]{:S(2)}) copy-start(pred[256,256]{1,0:T(8,128)(4,1)} %iota_compare_fusion) | copy-start | bytes 196612
  68.4 14.0 %collective-permute-start.1 = (f32[7,128,128]{2,1,0:T(8,128)S(1)}, f32[7,128,128]{2,1,0:T(8,128)S(1)}, u32[]{:S(2)}, u32[]{:S(2)}) collective-permute-start(f32[7,128,128]{2,1,0:T(8,128)S(1)} %pad_maximum_fusion.5), channel_id=1, source_target_pairs={{0,16},{16,0},{32,48},{48,32},{1,17},{17,1},{33,49},{49,33},{2,18}... | collective-permute-start | bytes 1376264 | tf_op jit(solution)/shard_map/ppermute | solution.py:13
  83.9 9.0 %collective-permute-start.2 = (f32[6,2,32,128]{3,2,1,0:T(8,128)S(1)}, f32[6,2,32,128]{3,2,1,0:T(8,128)S(1)}, u32[]{:S(2)}, u32[]{:S(2)}) collective-permute-start(f32[6,2,32,128]{3,2,1,0:T(8,128)S(1)} %pad_maximum_fusion.7), channel_id=1, source_target_pairs={{0,32},{16,48},{32,0},{48,16},{1,33},{17,49},{33,1},{49,17},{2,34}... | collective-permute-start | bytes 589832 | tf_op jit(solution)/shard_map/ppermute | solution.py:13
  92.9 27.2 %copy-start.24 = (f32[2,2,1,1]{1,0,3,2:T(2,128)S(1)}, f32[2,2,1,1]{1,0,3,2:T(2,128)}, u32[]{:S(2)}) copy-start(f32[2,2,1,1]{1,0,3,2:T(2,128)} %constant.141) | copy-start | bytes 52
  95.6 21.4 %copy-start.16 = (f32[1,2,32,128]{3,2,1,0:T(8,128)S(1)}, f32[1,2,32,128]{3,2,1,0:T(8,128)}, u32[]{:S(2)}) copy-start(f32[1,2,32,128]{3,2,1,0:T(8,128)} %get-tuple-element.17) | copy-start | bytes 98308
  95.6 32.5 %all-to-all-start.1 = ((f32[16,32,128]{2,1,0:T(8,128)}), f32[16,32,128]{2,1,0:T(8,128)S(1)}, u32[]{:S(2)}, u32[]{:S(2)}) async-start(f32[16,32,128]{2,1,0:T(8,128)} %broadcast_select_fusion), calls=%async_computation.1 | async-start | bytes 524288 | tf_op jit(solution)/shard_map/all_to_all | solution.py:137
  114.8 8.2 %copy-start.11 = (f32[2,2,128,128]{2,3,1,0:T(8,128)S(1)}, f32[2,2,128,128]{2,3,1,0:T(8,128)}, u32[]{:S(2)}) copy-start(f32[2,2,128,128]{2,3,1,0:T(8,128)} %slice_bitcast_fusion.1) | copy-start | bytes 786436
  114.8 9.1 %copy-start.14 = (f32[1,128,128]{2,1,0:T(8,128)S(1)}, f32[1,128,128]{2,1,0:T(8,128)}, u32[]{:S(2)}) copy-start(f32[1,128,128]{2,1,0:T(8,128)} %get-tuple-element.10) | copy-start | bytes 196612
  114.8 9.1 %copy-start.15 = (f32[1,128,128]{2,1,0:T(8,128)S(1)}, f32[1,128,128]{2,1,0:T(8,128)}, u32[]{:S(2)}) copy-start(f32[1,128,128]{2,1,0:T(8,128)} %get-tuple-element.12) | copy-start | bytes 196612
  117.0 6.8 %collective-permute-start.3 = (f32[2,2,32,128]{3,2,1,0:T(8,128)S(1)}, f32[2,2,32,128]{3,2,1,0:T(8,128)S(1)}, u32[]{:S(2)}, u32[]{:S(2)}) collective-permute-start(f32[2,2,32,128]{3,2,1,0:T(8,128)S(1)} %pad_maximum_fusion.11), channel_id=1, source_target_pairs={{0,16},{16,0},{32,48},{48,32},{1,17},{17,1},{33,49},{49,33},{2,18}... | collective-permute-start | bytes 196616 | tf_op jit(solution)/shard_map/ppermute | solution.py:13
  124.0 19.3 %collective-permute-start.4 = (f32[4,128,128]{2,1,0:T(8,128)S(1)}, f32[4,128,128]{2,1,0:T(8,128)S(1)}, u32[]{:S(2)}, u32[]{:S(2)}) collective-permute-start(f32[4,128,128]{2,1,0:T(8,128)S(1)} %pad_maximum_fusion.6), channel_id=1, source_target_pairs={{0,8},{8,0},{1,9},{9,1},{2,10},{10,2},{3,11},{11,3},{4,12},{12,4},... | collective-permute-start | bytes 786440 | tf_op jit(solution)/shard_map/ppermute | solution.py:13
  131.3 20.7 %all-to-all-start.2 = ((f32[8,5,32,128]{3,2,1,0:T(8,128)}), f32[8,5,32,128]{3,2,1,0:T(8,128)S(1)}, u32[]{:S(2)}, u32[]{:S(2)}) async-start(f32[8,5,32,128]{3,2,1,0:T(8,128)} %broadcast_in_dim.59), calls=%async_computation.2 | async-start | bytes 1310720 | tf_op jit(solution)/shard_map/all_to_all | solution.py:154
  143.3 12.7 %copy-start.5 = (bf16[2,256,2,128]{3,2,1,0:T(2,128)(2,1)S(1)}, bf16[2,256,2,128]{3,2,1,0:T(2,128)(2,1)}, u32[]{:S(2)}) copy-start(bf16[2,256,2,128]{3,2,1,0:T(2,128)(2,1)} %copy-done.4) | copy-start | bytes 786436
  143.3 12.7 %copy-start.7 = (f32[2,2,128,256]{3,2,1,0:T(8,128)S(1)}, f32[2,2,128,256]{3,2,1,0:T(8,128)}, u32[]{:S(2)}) copy-start(f32[2,2,128,256]{3,2,1,0:T(8,128)} %fusion.68) | copy-start | bytes 1572868
  152.0 4.3 %copy-start.8 = (f32[2,2,128,256]{3,2,1,0:T(8,128)S(1)}, f32[2,2,128,256]{3,2,1,0:T(8,128)}, u32[]{:S(2)}) copy-start(f32[2,2,128,256]{3,2,1,0:T(8,128)} %fusion.67) | copy-start | bytes 1572868
  152.0 0.8 copy-start.9
  156.5 8.1 %copy-start.2 = (bf16[2,256,2,128]{3,2,1,0:T(2,128)(2,1)S(1)}, bf16[2,256,2,128]{3,2,1,0:T(2,128)(2,1)}, u32[]{:S(2)}) copy-start(bf16[2,256,2,128]{3,2,1,0:T(2,128)(2,1)} %copy-done.1) | copy-start | bytes 786436
  156.5 8.1 %copy-start.19 = (f32[8,2,2,256]{3,0,1,2:T(8,128)S(1)}, f32[8,2,2,256]{3,0,1,2:T(8,128)}, u32[]{:S(2)}) copy-start(f32[8,2,2,256]{3,0,1,2:T(8,128)} %copy.346) | copy-start | bytes 98308
  156.5 8.1 %copy-start.20 = (bf16[2,1,2,128,128]{3,4,1,2,0:T(8,128)(2,1)S(1)}, bf16[2,1,2,128,128]{3,4,1,2,0:T(8,128)(2,1)}, u32[]{:S(2)}) copy-start(bf16[2,1,2,128,128]{3,4,1,2,0:T(8,128)(2,1)} %copy.265) | copy-start | bytes 393220
  165.3 1.0 copy-start.3
  165.3 1.1 copy-start.6
  (2 other events, 1.3 us)

commit v7 on v6

--- a/solution.py
+++ b/solution.py
@@ -108,27 +108,29 @@
     grad_first = (1.0 - upper_bits[0]) * arrived[1]
     running = lax.dynamic_index_in_dim(running + arrived[0], core_index, 0, keepdims=False)
     pending = lax.dynamic_index_in_dim(pending[1:] + arrived[2:], core_index, 1, keepdims=False)
-    packet = jnp.concatenate([running[None], pending], axis=0)
-    arrived = swapped(packet, "x", 0)
-    cross_x1 = arrived[0] * upper_bits[1]
-    grad_x1 = (1.0 - upper_bits[1]) * arrived[1]
-
-    def halved(matrix):
-        shaped = matrix.reshape(matrix.shape[:-2] + (2, 2, head_size // 4, head_size))
-        return lax.dynamic_index_in_dim(shaped, x_index % 2, shaped.ndim - 3, keepdims=False)
-
-    running = halved(running + arrived[0])
-    pending = halved(pending[1:] + arrived[2:])
-    packet = jnp.concatenate([running[None], pending], axis=0)
-    arrived = swapped(packet, "x", 1)
-    cross_x2 = arrived[0] * upper_bits[2]
-    grad_x2 = (1.0 - upper_bits[2]) * arrived[1]
-
-    def quartered(matrix):
-        return lax.dynamic_index_in_dim(matrix, x_index // 2, matrix.ndim - 3, keepdims=False)
-
-    running = quartered(running + arrived[0])
-    pending = quartered(pending[1:] + arrived[2:])
+    quarter = head_size // 4
+    x_choice, x_forward, x_backward = z_tables(lax.axis_size("x"))
+    x_options = jnp.concatenate([jnp.zeros_like(running)[None], running[None], pending[:2]])
+    near_chunks = jnp.take(x_options, lax.dynamic_index_in_dim(x_choice, x_index, 0, keepdims=False), axis=0)
+    far_chunks = jnp.concatenate([running[None], pending[2:]]).reshape(-1, 4, quarter, head_size)
+    x_send = jnp.concatenate([near_chunks.reshape(4, 4, quarter, head_size), far_chunks.transpose(1, 0, 2, 3)], axis=1)
+    x_received = lax.all_to_all(x_send, "x", 0, 0, tiled=True)
+    near_received = x_received[:, :4].reshape(4, head_size, head_size)
+    cross_x = jnp.einsum(
+        "jg,gpr->jpr",
+        lax.dynamic_index_in_dim(x_forward, x_index, 0, keepdims=False),
+        near_received,
+        precision=lax.Precision.HIGHEST,
+    )
+    grad_x = jnp.einsum(
+        "g,gpr->pr",
+        lax.dynamic_index_in_dim(x_backward, x_index, 0, keepdims=False),
+        near_received,
+        precision=lax.Precision.HIGHEST,
+    )
+    far_received = jnp.sum(x_received[:, 4:], axis=0)
+    running = far_received[0]
+    pending = far_received[1:]
     z_count = lax.axis_size("z")
     z_index = lax.axis_index("z")
     choice, forward_table, backward_table = z_tables(z_count)
@@ -139,22 +141,18 @@
     backward_row = lax.dynamic_index_in_dim(backward_table, z_index, 0, keepdims=False)
     cross_z = list(jnp.einsum("jg,gpr->jpr", forward_rows, received, precision=lax.Precision.HIGHEST))
     grad_z = jnp.einsum("g,gpr->pr", backward_row, received, precision=lax.Precision.HIGHEST)
-    odd_x = x_index % 2 == 1
 
     def ordered(own, other, other_first):
         return jnp.stack([jnp.where(other_first, other, own), jnp.where(other_first, own, other)])
 
-    half_two = jnp.stack([cross_x2, grad_x2])
-    level_two = ordered(half_two, swapped(half_two, "x", 0), odd_x)
-    level_two = level_two.transpose(1, 2, 0, 3, 4).reshape(2, head_size, head_size)
-    own_levels = jnp.concatenate([jnp.stack([cross_x1, grad_x1]), level_two])
+    own_levels = jnp.concatenate([cross_x, grad_x[None]])
     near_levels = ordered(own_levels, swapped(own_levels, "core", 0), core_index == 1)
     z_part = jnp.concatenate([jnp.stack(cross_z), grad_z[None]])
     spread = jnp.broadcast_to(z_part[None], (8,) + z_part.shape)
     z_levels = lax.all_to_all(spread, ("x", "core"), 0, 0, tiled=True).reshape((4, 2) + z_part.shape)
     z_levels = z_levels.transpose(1, 2, 0, 3, 4).reshape(2, z_part.shape[0], head_size, head_size)
-    device_grad = grad_first + near_levels[:, 1] + near_levels[:, 3] + z_levels[:, -1]
-    cross_list = [cross_first, near_levels[:, 0], near_levels[:, 2]] + [
+    device_grad = grad_first + near_levels[:, 2] + z_levels[:, -1]
+    cross_list = [cross_first, near_levels[:, 0], near_levels[:, 1]] + [
         z_levels[:, level] for level in range(cross_levels - 3)
     ]
     level_table = bucket_table(per_dev, local_levels)

time: 170 us -> 167 us (0.982)
  starting transfers between devices: 65.4 us -> 58.7 us
  local copies, waits for them, and re-layouts: 32.6 us -> 37.1 us
  matrix products: 17.3 us -> 20.4 us
  between operations: 3.27 us -> 1.32 us
  waiting for transfers between devices: 36.4 us -> 34.5 us
    ppermute x5 -> x2, waiting for transfers between devices: 13.6 us -> 0.01 us  [swapped(): return lax.ppermute(value, axis, pairs)]
    ppermute x5 -> x2, starting transfers between devices: 29.5 us -> 18.4 us  [swapped(): return lax.ppermute(value, axis, pairs)]
    all_to_all x0 -> x1, waiting for transfers between devices: none -> 6.17 us  [body(): x_received = lax.all_to_all(x_send, 'x', 0, 0, tiled=True)]
    all_to_all x1, waiting for transfers between devices: 0.01 us -> 5.19 us  [body(): received = lax.all_to_all(chunks, 'z', 0, 0, tiled=True)]
    all_to_all x0 -> x1, starting transfers between devices: none -> 3.73 us  [body(): x_received = lax.all_to_all(x_send, 'x', 0, 0, tiled=True)]
    unnamed x3 -> x0, other arithmetic: 3.43 us -> none
    another operation x2, other arithmetic: 0.05 us -> 2.12 us  [ordered(): jnp.stack([jnp.where(other_first, other, own), jnp.where(other_first, own...]
    unnamed x56 -> x55, local copies, waits for them, and re-layouts: 11.1 us -> 13.1 us
  transfers between devices with their start and end apart: 8 -> 6, of which waited for: 4 -> 4; matrix products, arithmetic and copies ran while one was open for 14% -> 16% of each run, Pallas kernels for 0% -> 0%
where the time goes in v7:
time: 167 us; the launch traced here: 166 us
  starting transfers between devices  58.7 us (35%)
  local copies, waits for them, and re-layouts  37.1 us (22%)
  waiting for transfers between devices  34.5 us (21%)
  matrix products  20.4 us (12%)
  other arithmetic  13.8 us (8%)
    all_to_all x1, starting transfers between devices, body(): received = lax.all_to_all(chunks, 'z', 0, 0, tiled=True)  18.6 us
    ppermute x2, starting transfers between devices, swapped(): return lax.ppermute(value, axis, pairs)  18.4 us
    all_to_all x1, waiting for transfers between devices, body(): lax.all_to_all(stacked, 'head', split_axis=2, concat_axis=0, tiled=True)  15.4 us
    unnamed x55, local copies, waits for them, and re-layouts  13.1 us
    all_to_all x1, starting transfers between devices, body(): lax.all_to_all(spread, ('x', 'core'), 0, 0, tiled=True)  10.4 us
    all_to_all x1, waiting for transfers between devices, body(): lax.all_to_all(spread, ('x', 'core'), 0, 0, tiled=True)  7.73 us
    all_to_all x1, starting transfers between devices, body(): lax.all_to_all(stacked, 'head', split_axis=2, concat_axis=0, tiled=True)  7.65 us
    all_to_all x1, waiting for transfers between devices, body(): x_received = lax.all_to_all(x_send, 'x', 0, 0, tiled=True)  6.17 us
  transfers between devices with their start and end apart: 6, of which 4 were waited for; matrix products, arithmetic and copies ran while one was open for 16% of the time, Pallas kernels for 0%

profile of v7, /device:TPU:1, one launch (start us, length us, event | category | flops | bytes accessed | tf_op | source)
XLA Modules:
  0.0 165.8 jit_solution(8682188100922639505)
XLA Ops:
  0.6 1.3 pad_maximum_fusion
  2.0 1.4 copy.166
  3.4 2.7 %reshape.179 = bf16[8,2,32768]{2,1,0:T(2,128)(2,1)} reshape(bf16[2048,4,64]{2,1,0:T(4,128)(2,1)S(1)} %bitcast.193) | data formatting | bytes 2097152
  6.1 7.7 %all-to-all-start = ((bf16[8,2,32768]{2,1,0:T(2,128)(2,1)}), bf16[8,2,32768]{2,1,0:T(2,128)(2,1)S(1)}, u32[]{:S(2)}, u32[]{:S(2)}) async-start(bf16[8,2,32768]{2,1,0:T(2,128)(2,1)} %reshape.179), calls=%async_computation | async-start | bytes 2097152 | tf_op jit(solution)/shard_map/all_to_all | solution.py:46
  15.1 15.4 %all-to-all-done = bf16[8,2,32768]{2,1,0:T(2,128)(2,1)S(1)} async-done(((bf16[8,2,32768]{2,1,0:T(2,128)(2,1)}), bf16[8,2,32768]{2,1,0:T(2,128)(2,1)S(1)}, u32[]{:S(2)}, u32[]{:S(2)}) %all-to-all-start) | async-done | bytes 1048608 | tf_op jit(solution)/shard_map/all_to_all | solution.py:46
  30.5 1.4 reshape.180
  37.2 1.9 %fusion.59 = (f32[2,128,128]{2,1,0:T(8,128)S(1)}, f32[2,2,128,128]{3,2,1,0:T(8,128)}) fusion(bf16[2,256,2,128]{1,3,2,0:T(8,128)(2,1)} %copy.174, bf16[2,256,2,128]{3,2,1,0:T(2,128)(2,1)S(1)} %reshape_squeeze.10), kind=kOutput, calls=%fused_computation.125 | convolution fusion | flops 33587200 | bytes 917504 | tf_op jit(solution)/shard_map/buhp,buhr->bhpr/dot_general | solution.py:92
  39.1 1.4 broadcast_multiply_fusion
  41.6 15.1 %collective-permute-start = (f32[8,2,128,128]{3,2,1,0:T(8,128)}, f32[8,2,128,128]{3,2,1,0:T(8,128)}, u32[]{:S(2)}, u32[]{:S(2)}) collective-permute-start(f32[8,2,128,128]{3,2,1,0:T(8,128)} %pad_maximum_fusion.1), channel_id=1, source_target_pairs={{0,8},{8,0},{1,9},{9,1},{2,10},{10,2},{3,11},{11,3},{4,12},{12,4},... | collective-permute-start | bytes 3145736 | tf_op jit(solution)/shard_map/ppermute | solution.py:13
  62.0 1.8 %copy.199 = bf16[2,256,2,128]{1,3,2,0:T(8,128)(2,1)} copy(bf16[2,256,2,128]{3,2,1,0:T(2,128)(2,1)} %copy-done.1) | data formatting | bytes 524288 | tf_op jit(solution)/shard_map/reshape;squeeze | solution.py:57
  63.8 2.8 %fusion.19 = bf16[2,1,2,128,128]{4,0,3,2,1:T(2,128)(2,1)} fusion(f32[2,2,1,1]{1,0,3,2:T(2,128)} %constant.139, f32[2,2,128,128]{3,2,1,0:T(8,128)} %get-tuple-element.16), kind=kOutput, calls=%fused_computation.33 | convolution fusion | flops 1638400 | bytes 393232 | tf_op jit(solution)/shard_map/mji,ihpr->jmhpr/dot_general | solution.py:159
  66.6 1.7 %copy.189 = bf16[2,1,2,128,128]{3,4,1,2,0:T(8,128)(2,1)} copy(bf16[2,1,2,128,128]{4,0,3,2,1:T(2,128)(2,1)} %fusion.19) | data formatting | bytes 262144 | tf_op jit(solution)/shard_map/mji,ihpr->jmhpr/transpose | solution.py:159
  73.0 3.7 %all-to-all-start.1 = ((f32[4,9,32,128]{3,2,1,0:T(8,128)}), f32[4,9,32,128]{3,2,1,0:T(8,128)S(1)}, u32[]{:S(2)}, u32[]{:S(2)}) async-start(f32[4,9,32,128]{3,2,1,0:T(8,128)} %pad_maximum_fusion.5), calls=%async_computation.1 | async-start | bytes 1179648 | tf_op jit(solution)/shard_map/all_to_all | solution.py:117
  77.4 1.8 %copy.200 = f32[2,2,128,128]{3,0,2,1:T(2,128)} copy(f32[2,2,128,128]{2,3,1,0:T(8,128)} %slice_bitcast_fusion) | data formatting | bytes 524288 | tf_op jit(solution)/shard_map/reshape.20
  79.3 1.3 fusion.8
  80.6 6.2 %all-to-all-done.1 = f32[4,9,32,128]{3,2,1,0:T(8,128)S(1)} async-done(((f32[4,9,32,128]{3,2,1,0:T(8,128)}), f32[4,9,32,128]{3,2,1,0:T(8,128)S(1)}, u32[]{:S(2)}, u32[]{:S(2)}) %all-to-all-start.1) | async-done | bytes 589856 | tf_op jit(solution)/shard_map/all_to_all | solution.py:117
  88.1 18.6 %all-to-all-start.2 = ((f32[16,32,128]{2,1,0:T(8,128)}), f32[16,32,128]{2,1,0:T(8,128)S(1)}, u32[]{:S(2)}, u32[]{:S(2)}) async-start(f32[16,32,128]{2,1,0:T(8,128)} %broadcast_select_fusion), calls=%async_computation.2 | async-start | bytes 524288 | tf_op jit(solution)/shard_map/all_to_all | solution.py:139
  108.3 1.3 convolution_bitcast_fusion.2
  111.0 3.3 %collective-permute-start.1 = (f32[3,128,128]{2,0,1:T(4,128)S(1)}, f32[3,128,128]{2,0,1:T(4,128)}, u32[]{:S(2)}, u32[]{:S(2)}) collective-permute-start(f32[3,128,128]{2,0,1:T(4,128)S(1)} %pad_maximum_fusion.7), channel_id=1, source_target_pairs={{0,8},{8,0},{1,9},{9,1},{2,10},{10,2},{3,11},{11,3},{4,12},{12,4},... | collective-permute-start | bytes 589832 | tf_op jit(solution)/shard_map/ppermute | solution.py:13
  114.3 5.2 %all-to-all-done.2 = f32[16,32,128]{2,1,0:T(8,128)S(1)} async-done(((f32[16,32,128]{2,1,0:T(8,128)}), f32[16,32,128]{2,1,0:T(8,128)S(1)}, u32[]{:S(2)}, u32[]{:S(2)}) %all-to-all-start.2) | async-done | bytes 262176 | tf_op jit(solution)/shard_map/all_to_all | solution.py:139
  122.7 10.4 %all-to-all-start.3 = ((f32[8,5,32,128]{3,2,1,0:T(8,128)}), f32[8,5,32,128]{3,2,1,0:T(8,128)S(1)}, u32[]{:S(2)}, u32[]{:S(2)}) async-start(f32[8,5,32,128]{3,2,1,0:T(8,128)} %broadcast_in_dim.71), calls=%async_computation.3 | async-start | bytes 1310720 | tf_op jit(solution)/shard_map/all_to_all | solution.py:152
  136.2 7.7 %all-to-all-done.3 = f32[8,5,32,128]{3,2,1,0:T(8,128)S(1)} async-done(((f32[8,5,32,128]{3,2,1,0:T(8,128)}), f32[8,5,32,128]{3,2,1,0:T(8,128)S(1)}, u32[]{:S(2)}, u32[]{:S(2)}) %all-to-all-start.3) | async-done | bytes 655392 | tf_op jit(solution)/shard_map/all_to_all | solution.py:152
  144.8 1.7 %fusion.37 = (f32[2,128,128]{2,1,0:T(8,128)S(1)}, bf16[7,2,128,128]{3,2,1,0:T(8,128)(2,1)}) fusion(f32[2,5,128,128]{3,2,0,1:T(8,128)S(1)} %bitcast.202, f32[1,2,128,128]{3,2,1,0:T(8,128)S(1)} %bitcast.217, f32[8,2,128,128]{3,2,1,0:T(8,128)} %collective-permute-done, f32[]{:T(128)S(6)} %sub.3, f32[]{:T(128)S(1)} %bitcast.228), kind=kLoop, calls=%fused_computation.71 | loop fusion | flops 131071 | bytes 786440 | tf_op jit(solution)/shard_map/add | solution.py:179
  146.5 2.0 %fusion.20 = bf16[2,2,128,128]{3,0,2,1:T(2,128)(2,1)S(1)} fusion(f32[2,2,128,128]{3,0,2,1:T(2,128)} %copy.200, f32[2,2,1,1]{1,0,3,2:T(2,128)S(1)} %copy-done.23, f32[2,128,128]{2,1,0:T(8,128)S(1)} %get-tuple-element.4), kind=kOutput, calls=%fused_computation.34 | convolution fusion | flops 1703936 | bytes 524304 | tf_op jit(solution)/shard_map/mji,jmhpr->ihpr/dot_general | solution.py:173
  148.9 1.3 fusion.17
  150.6 1.5 constant_dynamic-update-slice_fusion.1
  152.8 1.5 fusion.42
  154.3 1.5 fusion.41
  155.9 1.5 fusion.40
  157.4 1.5 fusion.39
  158.9 1.3 copy.188
  160.5 1.7 %fusion.1 = f32[2,256,2,128]{1,3,2,0:T(8,128)S(1)} fusion(f32[2,8,256,2]{2,1,3,0:T(8,128)S(1)} %bitcast.223, bf16[2,7,2,128,128]{3,4,1,2,0:T(8,128)(2,1)S(1)} %broadcast_in_dim.72, bf16[2,1,2,128,128]{3,4,1,2,0:T(8,128)(2,1)} %copy.189, bf16[2,256,2,128,1]{3,2,1,0,4:T(2,128)(2,1)S(1)} %bitcast.199), kind=kOutput, calls=%fused_computation.5 | convolution fusion | flops 270925824 | bytes 1867776 | tf_op jit(solution)/shard_map/bthp,bmhpr->bmthr/dot_general | solution.py:165
  (123 shorter events, 34.9 us)
Async XLA Ops:
  3.4 10.4 %copy-start.18 = (s32[9,2,512]{2,1,0:T(2,128)S(1)}, s32[9,2,512]{2,1,0:T(2,128)}, u32[]{:S(2)}) copy-start(s32[9,2,512]{2,1,0:T(2,128)} %param.17) | copy-start | bytes 110596
  3.4 10.4 %copy-start.20 = (f32[9]{0:T(128)S(1)}, f32[9]{0:T(128)}, u32[]{:S(2)}) copy-start(f32[9]{0:T(128)} %constant.137) | copy-start | bytes 112
  6.1 24.4 %all-to-all-start = ((bf16[8,2,32768]{2,1,0:T(2,128)(2,1)}), bf16[8,2,32768]{2,1,0:T(2,128)(2,1)S(1)}, u32[]{:S(2)}, u32[]{:S(2)}) async-start(bf16[8,2,32768]{2,1,0:T(2,128)(2,1)} %reshape.179), calls=%async_computation | async-start | bytes 2097152 | tf_op jit(solution)/shard_map/all_to_all | solution.py:46
  13.8 0.6 copy-start.13
  33.3 1.9 %copy-start.14 = (f32[8,2,2,256]{3,0,1,2:T(8,128)S(1)}, f32[8,2,2,256]{3,0,1,2:T(8,128)}, u32[]{:S(2)}) copy-start(f32[8,2,2,256]{3,0,1,2:T(8,128)} %copy.265) | copy-start | bytes 98308
  33.5 1.1 copy-start.4
  34.4 0.7 copy-start.1
  39.1 1.4 copy-start.10
  39.1 18.9 %copy-start.22 = (s32[4,4]{1,0:T(4,128)S(1)}, s32[4,4]{1,0:T(4,128)}, u32[]{:S(2)}) copy-start(s32[4,4]{1,0:T(4,128)} %constant.123.clone) | copy-start | bytes 196
  40.5 23.3 %copy-start = (f32[7,2,128,128]{3,2,1,0:T(8,128)}, f32[7,2,128,128]{3,2,1,0:T(8,128)S(1)}, u32[]{:S(2)}) copy-start(f32[7,2,128,128]{3,2,1,0:T(8,128)S(1)} %broadcast_multiply_fusion) | copy-start | bytes 2752516
  41.6 26.7 %collective-permute-start = (f32[8,2,128,128]{3,2,1,0:T(8,128)}, f32[8,2,128,128]{3,2,1,0:T(8,128)}, u32[]{:S(2)}, u32[]{:S(2)}) collective-permute-start(f32[8,2,128,128]{3,2,1,0:T(8,128)} %pad_maximum_fusion.1), channel_id=1, source_target_pairs={{0,8},{8,0},{1,9},{9,1},{2,10},{10,2},{3,11},{11,3},{4,12},{12,4},... | collective-permute-start | bytes 3145736 | tf_op jit(solution)/shard_map/ppermute | solution.py:13
  63.8 5.7 %slice-start = ((f32[7,2,128,128]{3,2,1,0:T(8,128)}), f32[6,2,128,128]{3,2,1,0:T(8,128)S(1)}, s32[]{:S(2)}) async-start(f32[7,2,128,128]{3,2,1,0:T(8,128)} %copy-done), calls=%async_computation.4 | async-start | bytes 1572864 | tf_op jit(solution)/shard_map/slice | solution.py:110
  66.6 3.9 %copy-start.11 = (f32[2,128,128]{2,1,0:T(8,128)S(1)}, f32[2,128,128]{2,1,0:T(8,128)}, u32[]{:S(2)}) copy-start(f32[2,128,128]{2,1,0:T(8,128)} %copy-done.10) | copy-start | bytes 393220
  68.3 2.3 %copy-start.21 = (f32[4]{0:T(128)S(1)}, f32[4]{0:T(128)}, u32[]{:S(2)}) copy-start(f32[4]{0:T(128)} %pad.13.clone) | copy-start | bytes 52
  71.3 8.0 %copy-start.5 = (bf16[2,256,2,128]{3,2,1,0:T(2,128)(2,1)S(1)}, bf16[2,256,2,128]{3,2,1,0:T(2,128)(2,1)}, u32[]{:S(2)}) copy-start(bf16[2,256,2,128]{3,2,1,0:T(2,128)(2,1)} %copy-done.4) | copy-start | bytes 786436
  71.3 8.0 %copy-start.17 = (pred[256,256]{1,0:T(8,128)(4,1)S(1)}, pred[256,256]{1,0:T(8,128)(4,1)}, u32[]{:S(2)}) copy-start(pred[256,256]{1,0:T(8,128)(4,1)} %iota_compare_fusion) | copy-start | bytes 196612
  73.0 13.8 %all-to-all-start.1 = ((f32[4,9,32,128]{3,2,1,0:T(8,128)}), f32[4,9,32,128]{3,2,1,0:T(8,128)S(1)}, u32[]{:S(2)}, u32[]{:S(2)}) async-start(f32[4,9,32,128]{3,2,1,0:T(8,128)} %pad_maximum_fusion.5), calls=%async_computation.1 | async-start | bytes 1179648 | tf_op jit(solution)/shard_map/all_to_all | solution.py:117
  76.7 10.6 %copy-start.19 = (pred[16]{0:T(512)(128)(4,1)S(1)}, pred[16]{0:T(512)(128)(4,1)}, u32[]{:S(2)}) copy-start(pred[16]{0:T(512)(128)(4,1)} %compare_and_fusion) | copy-start | bytes 52
  77.4 29.3 %copy-start.9 = (bf16[2,256,2,128]{1,3,2,0:T(8,128)(2,1)S(1)}, bf16[2,256,2,128]{1,3,2,0:T(8,128)(2,1)}, u32[]{:S(2)}) copy-start(bf16[2,256,2,128]{1,3,2,0:T(8,128)(2,1)} %copy.205) | copy-start | bytes 786436
  88.1 31.4 %all-to-all-start.2 = ((f32[16,32,128]{2,1,0:T(8,128)}), f32[16,32,128]{2,1,0:T(8,128)S(1)}, u32[]{:S(2)}, u32[]{:S(2)}) async-start(f32[16,32,128]{2,1,0:T(8,128)} %broadcast_select_fusion), calls=%async_computation.2 | async-start | bytes 524288 | tf_op jit(solution)/shard_map/all_to_all | solution.py:139
  108.3 24.7 %copy-start.8 = (bf16[2,256,2,128]{1,3,2,0:T(8,128)(2,1)S(1)}, bf16[2,256,2,128]{1,3,2,0:T(8,128)(2,1)}, u32[]{:S(2)}) copy-start(bf16[2,256,2,128]{1,3,2,0:T(8,128)(2,1)} %copy.199) | copy-start | bytes 786436
  111.0 23.1 %collective-permute-start.1 = (f32[3,128,128]{2,0,1:T(4,128)S(1)}, f32[3,128,128]{2,0,1:T(4,128)}, u32[]{:S(2)}, u32[]{:S(2)}) collective-permute-start(f32[3,128,128]{2,0,1:T(4,128)S(1)} %pad_maximum_fusion.7), channel_id=1, source_target_pairs={{0,8},{8,0},{1,9},{9,1},{2,10},{10,2},{3,11},{11,3},{4,12},{12,4},... | collective-permute-start | bytes 589832 | tf_op jit(solution)/shard_map/ppermute | solution.py:13
  122.7 21.3 %all-to-all-start.3 = ((f32[8,5,32,128]{3,2,1,0:T(8,128)}), f32[8,5,32,128]{3,2,1,0:T(8,128)S(1)}, u32[]{:S(2)}, u32[]{:S(2)}) async-start(f32[8,5,32,128]{3,2,1,0:T(8,128)} %broadcast_in_dim.71), calls=%async_computation.3 | async-start | bytes 1310720 | tf_op jit(solution)/shard_map/all_to_all | solution.py:152
  134.1 12.4 %copy-start.23 = (f32[2,2,1,1]{1,0,3,2:T(2,128)S(1)}, f32[2,2,1,1]{1,0,3,2:T(2,128)}, u32[]{:S(2)}) copy-start(f32[2,2,1,1]{1,0,3,2:T(2,128)} %constant.139) | copy-start | bytes 52
  135.2 13.4 %copy-start.6 = (f32[2,2,128,256]{3,2,1,0:T(8,128)S(1)}, f32[2,2,128,256]{3,2,1,0:T(8,128)}, u32[]{:S(2)}) copy-start(f32[2,2,128,256]{3,2,1,0:T(8,128)} %fusion.61) | copy-start | bytes 1572868
  144.0 0.8 copy-start.7
  148.5 3.6 %copy-start.12 = (f32[2,1,128,128]{3,1,2,0:T(1,128)S(1)}, f32[2,1,128,128]{3,1,2,0:T(1,128)}, u32[]{:S(2)}) copy-start(f32[2,1,128,128]{3,1,2,0:T(1,128)} %get-tuple-element.11) | copy-start | bytes 393220
  150.2 10.2 %copy-start.2 = (bf16[2,256,2,128]{3,2,1,0:T(2,128)(2,1)S(1)}, bf16[2,256,2,128]{3,2,1,0:T(2,128)(2,1)}, u32[]{:S(2)}) copy-start(bf16[2,256,2,128]{3,2,1,0:T(2,128)(2,1)} %copy-done.1) | copy-start | bytes 786436
  150.2 10.2 %copy-start.15 = (f32[8,2,2,256]{3,0,1,2:T(8,128)S(1)}, f32[8,2,2,256]{3,0,1,2:T(8,128)}, u32[]{:S(2)}) copy-start(f32[8,2,2,256]{3,0,1,2:T(8,128)} %copy.265) | copy-start | bytes 98308
  160.5 1.7 %copy-start.16 = (bf16[2,1,2,128,128]{3,4,1,2,0:T(8,128)(2,1)S(1)}, bf16[2,1,2,128,128]{3,4,1,2,0:T(8,128)(2,1)}, u32[]{:S(2)}) copy-start(bf16[2,1,2,128,128]{3,4,1,2,0:T(8,128)(2,1)} %copy.189) | copy-start | bytes 393220
  162.2 1.0 copy-start.3

commit v8 on v7

--- a/solution.py
+++ b/solution.py
@@ -152,24 +152,29 @@
     z_levels = lax.all_to_all(spread, ("x", "core"), 0, 0, tiled=True).reshape((4, 2) + z_part.shape)
     z_levels = z_levels.transpose(1, 2, 0, 3, 4).reshape(2, z_part.shape[0], head_size, head_size)
     device_grad = grad_first + near_levels[:, 2] + z_levels[:, -1]
-    cross_list = [cross_first, near_levels[:, 0], near_levels[:, 1]] + [
-        z_levels[:, level] for level in range(cross_levels - 3)
-    ]
+    cross_list = [cross_first, near_levels[:, 0], near_levels[:, 1]]
     level_table = bucket_table(per_dev, local_levels)
     local_buckets = jnp.einsum(
         "mji,ihpr->jmhpr", level_table, states, precision=lax.Precision.HIGHEST
     )
-    cross_stack = jnp.stack(cross_list)
-    cross_buckets = jnp.broadcast_to(cross_stack[None], (per_dev,) + cross_stack.shape)
-    buckets = jnp.concatenate([local_buckets, cross_buckets], axis=1).astype(jnp.bfloat16)
-    inter_out = jnp.einsum(
-        "bthp,bmhpr->bmthr", query_rows, buckets, preferred_element_type=jnp.float32
-    )
-    output = output + jnp.sum(inter_w * inter_out, axis=1)
-    inter_grad = jnp.einsum(
-        "bmhpr,bthr->bmthp", buckets, cotan_rows, preferred_element_type=jnp.float32
-    )
-    grad_query = grad_query + jnp.sum(inter_w * inter_grad, axis=1)
+    early_cross = jnp.stack(cross_list)
+    late_cross = z_levels[:, : cross_levels - 3].transpose(1, 0, 2, 3)
+    early_levels = local_levels + early_cross.shape[0]
+    bucket_groups = (
+        (jnp.concatenate([local_buckets, jnp.broadcast_to(early_cross[None], (per_dev,) + early_cross.shape)], axis=1), slice(0, early_levels)),
+        (jnp.broadcast_to(late_cross[None], (per_dev,) + late_cross.shape), slice(early_levels, None)),
+    )
+    for group, level_slice in bucket_groups:
+        buckets = group.astype(jnp.bfloat16)
+        group_w = inter_w[:, level_slice]
+        inter_out = jnp.einsum(
+            "bthp,bmhpr->bmthr", query_rows, buckets, preferred_element_type=jnp.float32
+        )
+        output = output + jnp.sum(group_w * inter_out, axis=1)
+        inter_grad = jnp.einsum(
+            "bmhpr,bthr->bmthp", buckets, cotan_rows, preferred_element_type=jnp.float32
+        )
+        grad_query = grad_query + jnp.sum(group_w * inter_grad, axis=1)
     local_grad = jnp.einsum(
         "mji,jmhpr->ihpr",
         level_table,

time: 167 us -> 155 us (0.928)
  local copies, waits for them, and re-layouts: 37.1 us -> 26.4 us
  waiting for transfers between devices: 34.5 us -> 30.4 us
  matrix products: 20.4 us -> 23.1 us
    unnamed x55 -> x68, local copies, waits for them, and re-layouts: 13.1 us -> 5.43 us
    all_to_all x1, waiting for transfers between devices: 15.4 us -> 11.7 us  [body(): lax.all_to_all(stacked, 'head', split_axis=2, concat_axis=0, tiled=True)]
    another operation x4 -> x3, local copies, waits for them, and re-layouts: 5.35 us -> 1.73 us
    all_to_all x1, waiting for transfers between devices: 5.19 us -> 2.73 us  [body(): received = lax.all_to_all(chunks, 'z', 0, 0, tiled=True)]
    all_to_all x1, waiting for transfers between devices: 6.17 us -> 7.97 us  [body(): x_received = lax.all_to_all(x_send, 'x', 0, 0, tiled=True)]
    dot_general x1 -> x2, matrix products: 0.78 us -> 2.54 us  [body(): jnp.einsum('bmhpr,bthr->bmthp', buckets, cotan_rows, preferred_element_ty...]
    dot_general x1, matrix products: 2.79 us -> 1.09 us  [body(): jnp.einsum('mji,ihpr->jmhpr', level_table, states, precision=lax.Precisio...]
  transfers between devices with their start and end apart: 6 -> 6, of which waited for: 4 -> 5; matrix products, arithmetic and copies ran while one was open for 16% -> 16% of each run, Pallas kernels for 0% -> 0%
where the time goes in v8:
time: 155 us; the launch traced here: 154 us
  starting transfers between devices  58.7 us (38%)
  waiting for transfers between devices  30.4 us (20%)
  local copies, waits for them, and re-layouts  26.4 us (17%)
  matrix products  23.1 us (15%)
  other arithmetic  14.2 us (9%)
    all_to_all x1, starting transfers between devices, body(): received = lax.all_to_all(chunks, 'z', 0, 0, tiled=True)  18.7 us
    ppermute x2, starting transfers between devices, swapped(): return lax.ppermute(value, axis, pairs)  18.3 us
    all_to_all x1, waiting for transfers between devices, body(): lax.all_to_all(stacked, 'head', split_axis=2, concat_axis=0, tiled=True)  11.7 us
    all_to_all x1, starting transfers between devices, body(): lax.all_to_all(spread, ('x', 'core'), 0, 0, tiled=True)  10.2 us
    all_to_all x1, waiting for transfers between devices, body(): x_received = lax.all_to_all(x_send, 'x', 0, 0, tiled=True)  7.97 us
    all_to_all x1, waiting for transfers between devices, body(): lax.all_to_all(spread, ('x', 'core'), 0, 0, tiled=True)  7.78 us
    all_to_all x1, starting transfers between devices, body(): lax.all_to_all(stacked, 'head', split_axis=2, concat_axis=0, tiled=True)  7.65 us
    unnamed x68, local copies, waits for them, and re-layouts  5.43 us
  transfers between devices with their start and end apart: 6, of which 5 were waited for; matrix products, arithmetic and copies ran while one was open for 16% of the time, Pallas kernels for 0%

profile of v8, /device:TPU:1, one launch (start us, length us, event | category | flops | bytes accessed | tf_op | source)
XLA Modules:
  0.0 154.2 jit_solution(12753035550514129227)
XLA Ops:
  0.6 1.3 pad_maximum_fusion
  2.0 1.4 copy.184
  3.4 2.7 %reshape.182 = bf16[8,2,32768]{2,1,0:T(2,128)(2,1)} reshape(bf16[2048,4,64]{2,1,0:T(4,128)(2,1)S(1)} %bitcast.206) | data formatting | bytes 2097152
  6.1 7.7 %all-to-all-start = ((bf16[8,2,32768]{2,1,0:T(2,128)(2,1)}), bf16[8,2,32768]{2,1,0:T(2,128)(2,1)S(1)}, u32[]{:S(2)}, u32[]{:S(2)}) async-start(bf16[8,2,32768]{2,1,0:T(2,128)(2,1)} %reshape.182), calls=%async_computation | async-start | bytes 2097152 | tf_op jit(solution)/shard_map/all_to_all | solution.py:46
  18.8 11.7 %all-to-all-done = bf16[8,2,32768]{2,1,0:T(2,128)(2,1)S(1)} async-done(((bf16[8,2,32768]{2,1,0:T(2,128)(2,1)}), bf16[8,2,32768]{2,1,0:T(2,128)(2,1)S(1)}, u32[]{:S(2)}, u32[]{:S(2)}) %all-to-all-start) | async-done | bytes 1048608 | tf_op jit(solution)/shard_map/all_to_all | solution.py:46
  30.5 1.4 reshape.183
  31.9 1.2 copy.245
  35.9 1.2 copy.197
  37.2 1.3 broadcast_multiply_fusion
  38.6 2.1 %fusion.64 = (f32[2,128,128]{2,1,0:T(8,128)S(1)}, f32[2,2,128,128]{3,2,1,0:T(8,128)}) fusion(bf16[2,256,2,128]{1,3,2,0:T(8,128)(2,1)} %copy.192, bf16[2,256,2,128]{3,2,1,0:T(2,128)(2,1)S(1)} %reshape_squeeze.10), kind=kOutput, calls=%fused_computation.131 | convolution fusion | flops 33587200 | bytes 917504 | tf_op jit(solution)/shard_map/buhp,buhr->bhpr/dot_general | solution.py:92
  42.4 15.1 %collective-permute-start = (f32[8,2,128,128]{3,2,1,0:T(8,128)}, f32[8,2,128,128]{3,2,1,0:T(8,128)}, u32[]{:S(2)}, u32[]{:S(2)}) collective-permute-start(f32[8,2,128,128]{3,2,1,0:T(8,128)} %pad_maximum_fusion.1), channel_id=1, source_target_pairs={{0,8},{8,0},{1,9},{9,1},{2,10},{10,2},{3,11},{11,3},{4,12},{12,4},... | collective-permute-start | bytes 3145736 | tf_op jit(solution)/shard_map/ppermute | solution.py:13
  57.5 1.3 compare_and_fusion
  60.2 1.8 %copy.222 = bf16[2,256,2,128]{1,3,2,0:T(8,128)(2,1)} copy(bf16[2,256,2,128]{3,2,1,0:T(2,128)(2,1)} %copy-done.1) | data formatting | bytes 524288 | tf_op jit(solution)/shard_map/reshape;squeeze | solution.py:57
  62.0 1.4 fusion.10
  65.7 1.2 slice.127
  68.9 1.6 %gather_fusion = f32[4,128,128]{2,1,0:T(8,128)S(1)} fusion(f32[4,128,128]{2,1,0:T(8,128)} %pad_maximum_fusion.6, s32[1024]{0:T(1024)} %pad_clamp_fusion.1), kind=kCustom, calls=%fused_computation | custom fusion | bytes 524304 | tf_op jit(solution)/shard_map/jit(_take)/gather | solution.py:114
  72.2 3.9 %all-to-all-start.1 = ((f32[4,9,32,128]{3,2,1,0:T(8,128)}), f32[4,9,32,128]{3,2,1,0:T(8,128)S(1)}, u32[]{:S(2)}, u32[]{:S(2)}) async-start(f32[4,9,32,128]{3,2,1,0:T(8,128)} %pad_maximum_fusion.2), calls=%async_computation.1 | async-start | bytes 1179648 | tf_op jit(solution)/shard_map/all_to_all | solution.py:117
  76.7 1.3 fusion.65
  78.1 8.0 %all-to-all-done.1 = f32[4,9,32,128]{3,2,1,0:T(8,128)S(1)} async-done(((f32[4,9,32,128]{3,2,1,0:T(8,128)}), f32[4,9,32,128]{3,2,1,0:T(8,128)S(1)}, u32[]{:S(2)}, u32[]{:S(2)}) %all-to-all-start.1) | async-done | bytes 589856 | tf_op jit(solution)/shard_map/all_to_all | solution.py:117
  87.6 18.7 %all-to-all-start.2 = ((f32[16,32,128]{2,1,0:T(8,128)}), f32[16,32,128]{2,1,0:T(8,128)S(1)}, u32[]{:S(2)}, u32[]{:S(2)}) async-start(f32[16,32,128]{2,1,0:T(8,128)} %broadcast_select_fusion), calls=%async_computation.2 | async-start | bytes 524288 | tf_op jit(solution)/shard_map/all_to_all | solution.py:139
  109.2 1.2 convolution_bitcast_fusion.2
  110.5 1.2 fusion.51
  111.9 3.3 %collective-permute-start.1 = (f32[3,128,128]{2,0,1:T(4,128)S(1)}, f32[3,128,128]{2,0,1:T(4,128)S(1)}, u32[]{:S(2)}, u32[]{:S(2)}) collective-permute-start(f32[3,128,128]{2,0,1:T(4,128)S(1)} %pad_maximum_fusion.7), channel_id=1, source_target_pairs={{0,8},{8,0},{1,9},{9,1},{2,10},{10,2},{3,11},{11,3},{4,12},{12,4},... | collective-permute-start | bytes 589832 | tf_op jit(solution)/shard_map/ppermute | solution.py:13
  116.5 2.7 %all-to-all-done.2 = f32[16,32,128]{2,1,0:T(8,128)S(1)} async-done(((f32[16,32,128]{2,1,0:T(8,128)}), f32[16,32,128]{2,1,0:T(8,128)S(1)}, u32[]{:S(2)}, u32[]{:S(2)}) %all-to-all-start.2) | async-done | bytes 262176 | tf_op jit(solution)/shard_map/all_to_all | solution.py:139
  122.4 10.2 %all-to-all-start.3 = ((f32[8,5,32,128]{3,2,1,0:T(8,128)}), f32[8,5,32,128]{3,2,1,0:T(8,128)S(1)}, u32[]{:S(2)}, u32[]{:S(2)}) async-start(f32[8,5,32,128]{3,2,1,0:T(8,128)} %broadcast_in_dim.81), calls=%async_computation.3 | async-start | bytes 1310720 | tf_op jit(solution)/shard_map/all_to_all | solution.py:152
  133.2 1.3 fusion.2
  134.5 1.2 fusion.4
  135.7 7.8 %all-to-all-done.3 = f32[8,5,32,128]{3,2,1,0:T(8,128)S(1)} async-done(((f32[8,5,32,128]{3,2,1,0:T(8,128)}), f32[8,5,32,128]{3,2,1,0:T(8,128)S(1)}, u32[]{:S(2)}, u32[]{:S(2)}) %all-to-all-start.3) | async-done | bytes 655392 | tf_op jit(solution)/shard_map/all_to_all | solution.py:152
  143.6 1.3 fusion.1
  144.8 1.3 fusion.3
  149.2 1.5 fusion.17
  151.0 1.3 fusion.16
  (140 shorter events, 32.0 us)
Async XLA Ops:
  3.4 10.4 %copy-start.22 = (s32[9,2,512]{2,1,0:T(2,128)S(1)}, s32[9,2,512]{2,1,0:T(2,128)}, u32[]{:S(2)}) copy-start(s32[9,2,512]{2,1,0:T(2,128)} %param.17) | copy-start | bytes 110596
  3.4 10.3 %copy-start.28 = (f32[9]{0:T(128)S(1)}, f32[9]{0:T(128)}, u32[]{:S(2)}) copy-start(f32[9]{0:T(128)} %constant.137) | copy-start | bytes 112
  3.4 12.3 %copy-start.30 = (s32[4,4]{1,0:T(4,128)S(1)}, s32[4,4]{1,0:T(4,128)}, u32[]{:S(2)}) copy-start(s32[4,4]{1,0:T(4,128)} %constant.123.clone) | copy-start | bytes 196
  6.1 24.4 %all-to-all-start = ((bf16[8,2,32768]{2,1,0:T(2,128)(2,1)}), bf16[8,2,32768]{2,1,0:T(2,128)(2,1)S(1)}, u32[]{:S(2)}, u32[]{:S(2)}) async-start(bf16[8,2,32768]{2,1,0:T(2,128)(2,1)} %reshape.182), calls=%async_computation | async-start | bytes 2097152 | tf_op jit(solution)/shard_map/all_to_all | solution.py:46
  15.1 22.1 %copy-start.25 = (f32[7]{0:T(128)}, f32[7]{0:T(128)S(1)}, u32[]{:S(2)}) copy-start(f32[7]{0:T(128)S(1)} %fusion.53) | copy-start | bytes 88
  37.2 21.6 %copy-start.17 = (f32[8,2,2,256]{3,0,1,2:T(8,128)S(1)}, f32[8,2,2,256]{3,0,1,2:T(8,128)}, u32[]{:S(2)}) copy-start(f32[8,2,2,256]{3,0,1,2:T(8,128)} %copy.307) | copy-start | bytes 98308
  38.5 23.5 %copy-start = (f32[7,2,128,128]{3,2,1,0:T(8,128)}, f32[7,2,128,128]{3,2,1,0:T(8,128)S(1)}, u32[]{:S(2)}) copy-start(f32[7,2,128,128]{3,2,1,0:T(8,128)S(1)} %broadcast_multiply_fusion) | copy-start | bytes 2752516
  42.4 23.3 %collective-permute-start = (f32[8,2,128,128]{3,2,1,0:T(8,128)}, f32[8,2,128,128]{3,2,1,0:T(8,128)}, u32[]{:S(2)}, u32[]{:S(2)}) collective-permute-start(f32[8,2,128,128]{3,2,1,0:T(8,128)} %pad_maximum_fusion.1), channel_id=1, source_target_pairs={{0,8},{8,0},{1,9},{9,1},{2,10},{10,2},{3,11},{11,3},{4,12},{12,4},... | collective-permute-start | bytes 3145736 | tf_op jit(solution)/shard_map/ppermute | solution.py:13
  63.5 3.5 %copy-start.8 = (bf16[2,2,256,256]{3,2,1,0:T(8,128)(2,1)}, bf16[2,2,256,256]{3,2,1,0:T(8,128)(2,1)S(1)}, u32[]{:S(2)}) copy-start(bf16[2,2,256,256]{3,2,1,0:T(8,128)(2,1)S(1)} %fusion.10) | copy-start | bytes 1572868
  63.5 3.5 %slice-start = ((f32[7,2,128,128]{3,2,1,0:T(8,128)}), f32[6,2,128,128]{3,2,1,0:T(8,128)S(1)}, s32[]{:S(2)}) async-start(f32[7,2,128,128]{3,2,1,0:T(8,128)} %copy-done), calls=%async_computation.4 | async-start | bytes 1572864 | tf_op jit(solution)/shard_map/slice | solution.py:110
  65.7 2.3 %copy-start.14 = (f32[2,128,128]{2,1,0:T(8,128)S(1)}, f32[2,128,128]{2,1,0:T(8,128)}, u32[]{:S(2)}) copy-start(f32[2,128,128]{2,1,0:T(8,128)} %copy-done.13) | copy-start | bytes 393220
  65.7 2.4 %copy-start.29 = (f32[4]{0:T(128)S(1)}, f32[4]{0:T(128)}, u32[]{:S(2)}) copy-start(f32[4]{0:T(128)} %pad.16.clone) | copy-start | bytes 52
  68.1 8.7 %copy-start.10 = (bf16[2,256,2,128]{1,3,2,0:T(8,128)(2,1)S(1)}, bf16[2,256,2,128]{1,3,2,0:T(8,128)(2,1)}, u32[]{:S(2)}) copy-start(bf16[2,256,2,128]{1,3,2,0:T(8,128)(2,1)} %copy.222) | copy-start | bytes 786436
  72.1 14.6 %copy-start.27 = (pred[16]{0:T(512)(128)(4,1)S(1)}, pred[16]{0:T(512)(128)(4,1)}, u32[]{:S(2)}) copy-start(pred[16]{0:T(512)(128)(4,1)} %compare_and_fusion) | copy-start | bytes 52
  72.2 13.9 %all-to-all-start.1 = ((f32[4,9,32,128]{3,2,1,0:T(8,128)}), f32[4,9,32,128]{3,2,1,0:T(8,128)S(1)}, u32[]{:S(2)}, u32[]{:S(2)}) async-start(f32[4,9,32,128]{3,2,1,0:T(8,128)} %pad_maximum_fusion.2), calls=%async_computation.1 | async-start | bytes 1179648 | tf_op jit(solution)/shard_map/all_to_all | solution.py:117
  76.0 30.3 %copy-start.31 = (f32[2,2,1,1]{1,0,3,2:T(2,128)S(1)}, f32[2,2,1,1]{1,0,3,2:T(2,128)}, u32[]{:S(2)}) copy-start(f32[2,2,1,1]{1,0,3,2:T(2,128)} %constant.139) | copy-start | bytes 52
  76.7 29.6 %copy-start.18 = (f32[2,2,128,128]{3,2,1,0:T(8,128)S(1)}, f32[2,2,128,128]{3,2,1,0:T(8,128)}, u32[]{:S(2)}) copy-start(f32[2,2,128,128]{3,2,1,0:T(8,128)} %get-tuple-element.18) | copy-start | bytes 786436
  76.7 31.5 %copy-start.12 = (f32[2,2,128,128]{2,3,1,0:T(8,128)S(1)}, f32[2,2,128,128]{2,3,1,0:T(8,128)}, u32[]{:S(2)}) copy-start(f32[2,2,128,128]{2,3,1,0:T(8,128)} %slice_bitcast_fusion) | copy-start | bytes 786436
  87.6 27.6 %copy-start.26 = (f32[7]{0:T(128)S(1)}, f32[7]{0:T(128)}, u32[]{:S(2)}) copy-start(f32[7]{0:T(128)} %copy-done.25) | copy-start | bytes 88
  87.6 31.6 %all-to-all-start.2 = ((f32[16,32,128]{2,1,0:T(8,128)}), f32[16,32,128]{2,1,0:T(8,128)S(1)}, u32[]{:S(2)}, u32[]{:S(2)}) async-start(f32[16,32,128]{2,1,0:T(8,128)} %broadcast_select_fusion), calls=%async_computation.2 | async-start | bytes 524288 | tf_op jit(solution)/shard_map/all_to_all | solution.py:139
  111.9 4.4 %collective-permute-start.1 = (f32[3,128,128]{2,0,1:T(4,128)S(1)}, f32[3,128,128]{2,0,1:T(4,128)S(1)}, u32[]{:S(2)}, u32[]{:S(2)}) collective-permute-start(f32[3,128,128]{2,0,1:T(4,128)S(1)} %pad_maximum_fusion.7), channel_id=1, source_target_pairs={{0,8},{8,0},{1,9},{9,1},{2,10},{10,2},{3,11},{11,3},{4,12},{12,4},... | collective-permute-start | bytes 589832 | tf_op jit(solution)/shard_map/ppermute | solution.py:13
  121.5 11.7 %copy-start.20 = (bf16[2,1,2,128,128]{3,4,1,2,0:T(8,128)(2,1)S(1)}, bf16[2,1,2,128,128]{3,4,1,2,0:T(8,128)(2,1)}, u32[]{:S(2)}) copy-start(bf16[2,1,2,128,128]{3,4,1,2,0:T(8,128)(2,1)} %copy.204) | copy-start | bytes 393220
  121.5 11.7 %copy-start.23 = (f32[2,4,256,2]{2,1,3,0:T(4,128)S(1)}, f32[2,4,256,2]{2,1,3,0:T(4,128)}, u32[]{:S(2)}) copy-start(f32[2,4,256,2]{2,1,3,0:T(4,128)} %get-tuple-element.13) | copy-start | bytes 49156
  122.4 21.1 %all-to-all-start.3 = ((f32[8,5,32,128]{3,2,1,0:T(8,128)}), f32[8,5,32,128]{3,2,1,0:T(8,128)S(1)}, u32[]{:S(2)}, u32[]{:S(2)}) async-start(f32[8,5,32,128]{3,2,1,0:T(8,128)} %broadcast_in_dim.81), calls=%async_computation.3 | async-start | bytes 1310720 | tf_op jit(solution)/shard_map/all_to_all | solution.py:152
  143.5 3.6 %copy-start.19 = (f32[2,2,128,128]{3,0,2,1:T(2,128)S(1)}, f32[2,2,128,128]{3,0,2,1:T(2,128)}, u32[]{:S(2)}) copy-start(f32[2,2,128,128]{3,0,2,1:T(2,128)} %copy.223) | copy-start | bytes 786436
  143.5 3.6 %copy-start.32 = (f32[2,2,1,1]{1,0,3,2:T(2,128)S(1)}, f32[2,2,1,1]{1,0,3,2:T(2,128)}, u32[]{:S(2)}) copy-start(f32[2,2,1,1]{1,0,3,2:T(2,128)} %constant.139) | copy-start | bytes 52
  143.6 4.8 %copy-start.4 = (bf16[2,256,2,128]{3,2,1,0:T(2,128)(2,1)S(1)}, bf16[2,256,2,128]{3,2,1,0:T(2,128)(2,1)}, u32[]{:S(2)}) copy-start(bf16[2,256,2,128]{3,2,1,0:T(2,128)(2,1)} %copy-done.3) | copy-start | bytes 786436
  143.6 4.8 %copy-start.6 = (f32[2,2,128,256]{3,2,1,0:T(8,128)S(1)}, f32[2,2,128,256]{3,2,1,0:T(8,128)}, u32[]{:S(2)}) copy-start(f32[2,2,128,256]{3,2,1,0:T(8,128)} %fusion.66) | copy-start | bytes 1572868
  147.1 2.1 %copy-start.9 = (bf16[2,2,256,256]{3,2,1,0:T(8,128)(2,1)S(1)}, bf16[2,2,256,256]{3,2,1,0:T(8,128)(2,1)}, u32[]{:S(2)}) copy-start(bf16[2,2,256,256]{3,2,1,0:T(8,128)(2,1)} %copy-done.8) | copy-start | bytes 1572868
  148.9 2.1 %copy-start.5 = (bf16[2,256,2,128]{1,3,2,0:T(8,128)(2,1)S(1)}, bf16[2,256,2,128]{1,3,2,0:T(8,128)(2,1)}, u32[]{:S(2)}) copy-start(bf16[2,256,2,128]{1,3,2,0:T(8,128)(2,1)} %copy.192) | copy-start | bytes 786436
  148.9 2.1 %copy-start.7 = (bf16[2,2,256,256]{3,2,1,0:T(8,128)(2,1)S(1)}, bf16[2,2,256,256]{3,2,1,0:T(8,128)(2,1)}, u32[]{:S(2)}) copy-start(bf16[2,2,256,256]{3,2,1,0:T(8,128)(2,1)} %fusion.11) | copy-start | bytes 1572868
  148.9 2.1 %copy-start.15 = (f32[2,256,2,128]{1,3,2,0:T(8,128)S(1)}, f32[2,256,2,128]{1,3,2,0:T(8,128)}, u32[]{:S(2)}) copy-start(f32[2,256,2,128]{1,3,2,0:T(8,128)} %fusion.2) | copy-start | bytes 1572868
  (8 other events, 10.6 us)

commit v9 on v8

--- a/solution.py
+++ b/solution.py
@@ -71,24 +71,6 @@
     inter_w = jnp.transpose(weights[1:], (2, 0, 3, 1))[..., None]
     position = jnp.arange(SPAN, dtype=jnp.int32)
     causal = position[:, None] >= position[None, :]
-    scores = jnp.einsum("bthp,buhp->bhtu", query_rows, key_rows, preferred_element_type=jnp.float32)
-    attention = jnp.where(causal, scores * intra_w, 0.0).astype(jnp.bfloat16)
-    cotan_scores = jnp.einsum(
-        "bthr,buhr->bhtu", cotan_rows, value_rows, preferred_element_type=jnp.float32
-    )
-    grad_scores = jnp.where(causal, cotan_scores * intra_w, 0.0).astype(jnp.bfloat16)
-    output = jnp.einsum(
-        "bhtu,buhr->bthr", attention, value_rows, preferred_element_type=jnp.float32
-    )
-    grad_query = jnp.einsum(
-        "bhtu,buhp->bthp", grad_scores, key_rows, preferred_element_type=jnp.float32
-    )
-    grad_key = jnp.einsum(
-        "bhtu,bthp->buhp", grad_scores, query_rows, preferred_element_type=jnp.float32
-    )
-    grad_value = jnp.einsum(
-        "bhtu,bthr->buhr", attention, cotan_rows, preferred_element_type=jnp.float32
-    )
     states = jnp.einsum("buhp,buhr->bhpr", key_rows, value_rows, preferred_element_type=jnp.float32)
     core_index = lax.axis_index("core")
     x_index = lax.axis_index("x")
@@ -137,6 +119,27 @@
     options = jnp.concatenate([jnp.zeros_like(running)[None], running[None], pending])
     chunks = jnp.take(options, lax.dynamic_index_in_dim(choice, z_index, 0, keepdims=False), axis=0)
     received = lax.all_to_all(chunks, "z", 0, 0, tiled=True)
+    late_query, late_key, late_value, late_cotan, _ = lax.optimization_barrier(
+        (query_rows, key_rows, value_rows, cotan_rows, received)
+    )
+    scores = jnp.einsum("bthp,buhp->bhtu", late_query, late_key, preferred_element_type=jnp.float32)
+    attention = jnp.where(causal, scores * intra_w, 0.0).astype(jnp.bfloat16)
+    cotan_scores = jnp.einsum(
+        "bthr,buhr->bhtu", late_cotan, late_value, preferred_element_type=jnp.float32
+    )
+    grad_scores = jnp.where(causal, cotan_scores * intra_w, 0.0).astype(jnp.bfloat16)
+    output = jnp.einsum(
+        "bhtu,buhr->bthr", attention, late_value, preferred_element_type=jnp.float32
+    )
+    grad_query = jnp.einsum(
+        "bhtu,buhp->bthp", grad_scores, late_key, preferred_element_type=jnp.float32
+    )
+    grad_key = jnp.einsum(
+        "bhtu,bthp->buhp", grad_scores, late_query, preferred_element_type=jnp.float32
+    )
+    grad_value = jnp.einsum(
+        "bhtu,bthr->buhr", attention, late_cotan, preferred_element_type=jnp.float32
+    )
     forward_rows = lax.dynamic_index_in_dim(forward_table, z_index, 0, keepdims=False)
     backward_row = lax.dynamic_index_in_dim(backward_table, z_index, 0, keepdims=False)
     cross_z = list(jnp.einsum("jg,gpr->jpr", forward_rows, received, precision=lax.Precision.HIGHEST))

time: 155 us -> 149 us (0.961)
  matrix products: 23.1 us -> 19.8 us
  local copies, waits for them, and re-layouts: 26.4 us -> 23.2 us
    dot_general x6, matrix products: 7.87 us -> 3.94 us  [the longest x1 1.54 us: body(): jnp.einsum('bhtu,buhr->bthr', attention, late_value, preferred_element_ty...]
    all_to_all x1, waiting for transfers between devices: 11.7 us -> 15.4 us  [body(): lax.all_to_all(stacked, 'head', split_axis=2, concat_axis=0, tiled=True)]
    another operation x5 -> x4, local copies, waits for them, and re-layouts: 2.83 us -> 0.27 us  [split_spans(): return matrix.reshape(per_dev, SPAN, heads_local, head_size)]
    all_to_all x1, waiting for transfers between devices: 7.97 us -> 5.62 us  [body(): x_received = lax.all_to_all(x_send, 'x', 0, 0, tiled=True)]
    another operation x5 -> x3, local copies, waits for them, and re-layouts: 2.64 us -> 1.03 us
    unnamed x68 -> x56, local copies, waits for them, and re-layouts: 5.43 us -> 5.88 us
  transfers between devices with their start and end apart: 6 -> 6, of which waited for: 5 -> 5; matrix products, arithmetic and copies ran while one was open for 16% -> 14% of each run, Pallas kernels for 0% -> 0%
where the time goes in v9:
time: 149 us; the launch traced here: 148 us
  starting transfers between devices  58.7 us (39%)
  waiting for transfers between devices  31.1 us (21%)
  local copies, waits for them, and re-layouts  23.2 us (16%)
  matrix products  19.8 us (13%)
  other arithmetic  13.4 us (9%)
    all_to_all x1, starting transfers between devices, body(): received = lax.all_to_all(chunks, 'z', 0, 0, tiled=True)  18.6 us
    ppermute x2, starting transfers between devices, swapped(): return lax.ppermute(value, axis, pairs)  18.4 us
    all_to_all x1, waiting for transfers between devices, body(): lax.all_to_all(stacked, 'head', split_axis=2, concat_axis=0, tiled=True)  15.4 us
    all_to_all x1, starting transfers between devices, body(): lax.all_to_all(spread, ('x', 'core'), 0, 0, tiled=True)  10.4 us
    all_to_all x1, waiting for transfers between devices, body(): lax.all_to_all(spread, ('x', 'core'), 0, 0, tiled=True)  8.2 us
    all_to_all x1, starting transfers between devices, body(): lax.all_to_all(stacked, 'head', split_axis=2, concat_axis=0, tiled=True)  7.65 us
    unnamed x56, local copies, waits for them, and re-layouts  5.88 us
    all_to_all x1, waiting for transfers between devices, body(): x_received = lax.all_to_all(x_send, 'x', 0, 0, tiled=True)  5.62 us
  transfers between devices with their start and end apart: 6, of which 5 were waited for; matrix products, arithmetic and copies ran while one was open for 14% of the time, Pallas kernels for 0%

profile of v9, /device:TPU:1, one launch (start us, length us, event | category | flops | bytes accessed | tf_op | source)
XLA Modules:
  0.0 147.7 jit_solution(1305252363134696906)
XLA Ops:
  0.6 1.3 pad_maximum_fusion
  2.0 1.4 copy.182
  3.4 2.7 %reshape.182 = bf16[8,2,32768]{2,1,0:T(2,128)(2,1)} reshape(bf16[2048,4,64]{2,1,0:T(4,128)(2,1)S(1)} %bitcast.206) | data formatting | bytes 2097152
  6.0 7.7 %all-to-all-start = ((bf16[8,2,32768]{2,1,0:T(2,128)(2,1)}), bf16[8,2,32768]{2,1,0:T(2,128)(2,1)S(1)}, u32[]{:S(2)}, u32[]{:S(2)}) async-start(bf16[8,2,32768]{2,1,0:T(2,128)(2,1)} %reshape.182), calls=%async_computation | async-start | bytes 2097152 | tf_op jit(solution)/shard_map/all_to_all | solution.py:46
  15.1 15.4 %all-to-all-done = bf16[8,2,32768]{2,1,0:T(2,128)(2,1)S(1)} async-done(((bf16[8,2,32768]{2,1,0:T(2,128)(2,1)}), bf16[8,2,32768]{2,1,0:T(2,128)(2,1)S(1)}, u32[]{:S(2)}, u32[]{:S(2)}) %all-to-all-start) | async-done | bytes 1048608 | tf_op jit(solution)/shard_map/all_to_all | solution.py:46
  30.5 1.4 reshape.183
  31.9 1.2 copy.243
  34.2 1.5 fusion.7
  35.8 1.2 copy.190
  38.1 1.4 broadcast_multiply_fusion
  40.5 15.1 %collective-permute-start = (f32[8,2,128,128]{3,2,1,0:T(8,128)}, f32[8,2,128,128]{3,2,1,0:T(8,128)}, u32[]{:S(2)}, u32[]{:S(2)}) collective-permute-start(f32[8,2,128,128]{3,2,1,0:T(8,128)} %pad_maximum_fusion.1), channel_id=1, source_target_pairs={{0,8},{8,0},{1,9},{9,1},{2,10},{10,2},{3,11},{11,3},{4,12},{12,4},... | collective-permute-start | bytes 3145736 | tf_op jit(solution)/shard_map/ppermute | solution.py:13
  55.6 1.3 slice.129
  60.0 1.4 slice_bitcast_fusion.5
  61.5 1.2 slice.125
  66.2 3.7 %all-to-all-start.1 = ((f32[4,9,32,128]{3,2,1,0:T(8,128)}), f32[4,9,32,128]{3,2,1,0:T(8,128)S(1)}, u32[]{:S(2)}, u32[]{:S(2)}) async-start(f32[4,9,32,128]{3,2,1,0:T(8,128)} %pad_maximum_fusion.2), calls=%async_computation.1 | async-start | bytes 1179648 | tf_op jit(solution)/shard_map/all_to_all | solution.py:99
  70.6 2.1 %fusion.23 = bf16[2,1,2,128,128]{4,0,3,2,1:T(2,128)(2,1)S(1)} fusion(f32[2,2,1,1]{1,0,3,2:T(2,128)S(1)} %copy-done.25, f32[2,2,128,128]{3,2,1,0:T(8,128)} %get-tuple-element.26), kind=kOutput, calls=%fused_computation.39 | convolution fusion | flops 1638400 | bytes 393232 | tf_op jit(solution)/shard_map/mji,ihpr->jmhpr/dot_general | solution.py:160
  74.3 5.6 %all-to-all-done.1 = f32[4,9,32,128]{3,2,1,0:T(8,128)S(1)} async-done(((f32[4,9,32,128]{3,2,1,0:T(8,128)}), f32[4,9,32,128]{3,2,1,0:T(8,128)S(1)}, u32[]{:S(2)}, u32[]{:S(2)}) %all-to-all-start.1) | async-done | bytes 589856 | tf_op jit(solution)/shard_map/all_to_all | solution.py:99
  81.7 18.6 %all-to-all-start.2 = ((f32[16,32,128]{2,1,0:T(8,128)}), f32[16,32,128]{2,1,0:T(8,128)S(1)}, u32[]{:S(2)}, u32[]{:S(2)}) async-start(f32[16,32,128]{2,1,0:T(8,128)} %broadcast_select_fusion), calls=%async_computation.2 | async-start | bytes 524288 | tf_op jit(solution)/shard_map/all_to_all | solution.py:121
  100.3 1.2 convolution_bitcast_fusion.2
  101.5 1.2 fusion.51
  102.9 3.3 %collective-permute-start.1 = (f32[3,128,128]{2,0,1:T(4,128)S(1)}, f32[3,128,128]{2,0,1:T(4,128)S(1)}, u32[]{:S(2)}, u32[]{:S(2)}) collective-permute-start(f32[3,128,128]{2,0,1:T(4,128)S(1)} %pad_maximum_fusion.7), channel_id=1, source_target_pairs={{0,8},{8,0},{1,9},{9,1},{2,10},{10,2},{3,11},{11,3},{4,12},{12,4},... | collective-permute-start | bytes 589832 | tf_op jit(solution)/shard_map/ppermute | solution.py:13
  108.8 1.3 fusion.2
  110.1 1.3 fusion.4
  111.4 1.7 %all-to-all-done.2 = f32[16,32,128]{2,1,0:T(8,128)S(1)} async-done(((f32[16,32,128]{2,1,0:T(8,128)}), f32[16,32,128]{2,1,0:T(8,128)S(1)}, u32[]{:S(2)}, u32[]{:S(2)}) %all-to-all-start.2) | async-done | bytes 262176 | tf_op jit(solution)/shard_map/all_to_all | solution.py:121
  113.0 1.1 fusion.29
  114.1 1.1 fusion.31
  116.7 10.4 %all-to-all-start.3 = ((f32[8,5,32,128]{3,2,1,0:T(8,128)}), f32[8,5,32,128]{3,2,1,0:T(8,128)S(1)}, u32[]{:S(2)}, u32[]{:S(2)}) async-start(f32[8,5,32,128]{3,2,1,0:T(8,128)} %broadcast_in_dim.81), calls=%async_computation.3 | async-start | bytes 1310720 | tf_op jit(solution)/shard_map/all_to_all | solution.py:155
  128.6 1.2 fusion.66
  129.8 8.2 %all-to-all-done.3 = f32[8,5,32,128]{3,2,1,0:T(8,128)S(1)} async-done(((f32[8,5,32,128]{3,2,1,0:T(8,128)}), f32[8,5,32,128]{3,2,1,0:T(8,128)S(1)}, u32[]{:S(2)}, u32[]{:S(2)}) %all-to-all-start.3) | async-done | bytes 655392 | tf_op jit(solution)/shard_map/all_to_all | solution.py:155
  138.1 1.3 fusion.1
  139.4 1.3 fusion.3
  143.7 1.5 %fusion.17 = bf16[2,256,2,128]{1,3,2,0:T(8,128)(2,1)S(1)} fusion(f32[2,256,2,128]{1,3,2,0:T(8,128)} %fusion.3, f32[2,256,2,128]{1,3,2,0:T(8,128)} %fusion.4, bf16[2,2,256,256]{3,2,1,0:T(8,128)(2,1)S(1)} %copy-done.5, bf16[2,256,2,128]{3,2,1,0:T(2,128)(2,1)S(1)} %reshape_squeeze.14), kind=kOutput, calls=%fused_computation.31 | convolution fusion | flops 67502080 | bytes 2097152 | tf_op jit(solution)/shard_map/bhtu,buhr->bthr/dot_general | solution.py:131
  (127 shorter events, 26.0 us)
Async XLA Ops:
  3.4 10.3 %copy-start.18 = (s32[9,2,512]{2,1,0:T(2,128)S(1)}, s32[9,2,512]{2,1,0:T(2,128)}, u32[]{:S(2)}) copy-start(s32[9,2,512]{2,1,0:T(2,128)} %param.17) | copy-start | bytes 110596
  3.4 10.3 %copy-start.23 = (f32[9]{0:T(128)S(1)}, f32[9]{0:T(128)}, u32[]{:S(2)}) copy-start(f32[9]{0:T(128)} %constant.137) | copy-start | bytes 112
  6.0 24.4 %all-to-all-start = ((bf16[8,2,32768]{2,1,0:T(2,128)(2,1)}), bf16[8,2,32768]{2,1,0:T(2,128)(2,1)S(1)}, u32[]{:S(2)}, u32[]{:S(2)}) async-start(bf16[8,2,32768]{2,1,0:T(2,128)(2,1)} %reshape.182), calls=%async_computation | async-start | bytes 2097152 | tf_op jit(solution)/shard_map/all_to_all | solution.py:46
  15.1 41.8 %copy-start.21 = (f32[7]{0:T(128)}, f32[7]{0:T(128)S(1)}, u32[]{:S(2)}) copy-start(f32[7]{0:T(128)S(1)} %fusion.53) | copy-start | bytes 88
  33.4 0.7 copy-start
  33.5 0.7 copy-start.2
  38.0 1.4 copy-start.9
  38.1 18.9 %copy-start.24 = (s32[4,4]{1,0:T(4,128)S(1)}, s32[4,4]{1,0:T(4,128)}, u32[]{:S(2)}) copy-start(s32[4,4]{1,0:T(4,128)} %constant.123.clone) | copy-start | bytes 196
  40.5 21.0 %collective-permute-start = (f32[8,2,128,128]{3,2,1,0:T(8,128)}, f32[8,2,128,128]{3,2,1,0:T(8,128)}, u32[]{:S(2)}, u32[]{:S(2)}) collective-permute-start(f32[8,2,128,128]{3,2,1,0:T(8,128)} %pad_maximum_fusion.1), channel_id=1, source_target_pairs={{0,8},{8,0},{1,9},{9,1},{2,10},{10,2},{3,11},{11,3},{4,12},{12,4},... | collective-permute-start | bytes 3145736 | tf_op jit(solution)/shard_map/ppermute | solution.py:13
  61.5 2.3 %copy-start.10 = (f32[2,128,128]{2,1,0:T(8,128)S(1)}, f32[2,128,128]{2,1,0:T(8,128)}, u32[]{:S(2)}) copy-start(f32[2,128,128]{2,1,0:T(8,128)} %copy-done.9) | copy-start | bytes 393220
  63.8 6.8 %copy-start.25 = (f32[2,2,1,1]{1,0,3,2:T(2,128)S(1)}, f32[2,2,1,1]{1,0,3,2:T(2,128)}, u32[]{:S(2)}) copy-start(f32[2,2,1,1]{1,0,3,2:T(2,128)} %constant.139) | copy-start | bytes 52
  66.2 13.8 %all-to-all-start.1 = ((f32[4,9,32,128]{3,2,1,0:T(8,128)}), f32[4,9,32,128]{3,2,1,0:T(8,128)S(1)}, u32[]{:S(2)}, u32[]{:S(2)}) async-start(f32[4,9,32,128]{3,2,1,0:T(8,128)} %pad_maximum_fusion.2), calls=%async_computation.1 | async-start | bytes 1179648 | tf_op jit(solution)/shard_map/all_to_all | solution.py:99
  74.3 31.9 %copy-start.22 = (f32[7]{0:T(128)S(1)}, f32[7]{0:T(128)}, u32[]{:S(2)}) copy-start(f32[7]{0:T(128)} %copy-done.21) | copy-start | bytes 88
  81.7 31.4 %all-to-all-start.2 = ((f32[16,32,128]{2,1,0:T(8,128)}), f32[16,32,128]{2,1,0:T(8,128)S(1)}, u32[]{:S(2)}, u32[]{:S(2)}) async-start(f32[16,32,128]{2,1,0:T(8,128)} %broadcast_select_fusion), calls=%async_computation.2 | async-start | bytes 524288 | tf_op jit(solution)/shard_map/all_to_all | solution.py:121
  102.8 6.0 %copy-start.1 = (bf16[2,256,2,128]{3,2,1,0:T(2,128)(2,1)S(1)}, bf16[2,256,2,128]{3,2,1,0:T(2,128)(2,1)}, u32[]{:S(2)}) copy-start(bf16[2,256,2,128]{3,2,1,0:T(2,128)(2,1)} %copy-done) | copy-start | bytes 786436
  102.8 6.0 %copy-start.16 = (bf16[2,1,2,128,128]{3,4,1,2,0:T(8,128)(2,1)S(1)}, bf16[2,1,2,128,128]{3,4,1,2,0:T(8,128)(2,1)}, u32[]{:S(2)}) copy-start(bf16[2,1,2,128,128]{3,4,1,2,0:T(8,128)(2,1)} %copy.202) | copy-start | bytes 393220
  102.8 6.0 %copy-start.19 = (f32[2,4,256,2]{2,1,3,0:T(4,128)S(1)}, f32[2,4,256,2]{2,1,3,0:T(4,128)}, u32[]{:S(2)}) copy-start(f32[2,4,256,2]{2,1,3,0:T(4,128)} %get-tuple-element.21) | copy-start | bytes 49156
  102.9 4.5 %collective-permute-start.1 = (f32[3,128,128]{2,0,1:T(4,128)S(1)}, f32[3,128,128]{2,0,1:T(4,128)S(1)}, u32[]{:S(2)}, u32[]{:S(2)}) collective-permute-start(f32[3,128,128]{2,0,1:T(4,128)S(1)} %pad_maximum_fusion.7), channel_id=1, source_target_pairs={{0,8},{8,0},{1,9},{9,1},{2,10},{10,2},{3,11},{11,3},{4,12},{12,4},... | collective-permute-start | bytes 589832 | tf_op jit(solution)/shard_map/ppermute | solution.py:13
  107.6 2.5 %copy-start.3 = (bf16[2,256,2,128]{3,2,1,0:T(2,128)(2,1)S(1)}, bf16[2,256,2,128]{3,2,1,0:T(2,128)(2,1)}, u32[]{:S(2)}) copy-start(bf16[2,256,2,128]{3,2,1,0:T(2,128)(2,1)} %copy-done.2) | copy-start | bytes 786436
  115.2 11.9 %copy-start.17 = (pred[256,256]{1,0:T(8,128)(4,1)S(1)}, pred[256,256]{1,0:T(8,128)(4,1)}, u32[]{:S(2)}) copy-start(pred[256,256]{1,0:T(8,128)(4,1)} %iota_compare_fusion) | copy-start | bytes 196612
  115.2 11.9 %copy-start.20 = (f32[1,2,512]{2,1,0:T(2,128)S(1)}, f32[1,2,512]{2,1,0:T(2,128)}, u32[]{:S(2)}) copy-start(f32[1,2,512]{2,1,0:T(2,128)} %slice.129) | copy-start | bytes 12292
  115.6 11.8 %copy-start.7 = (bf16[2,256,2,128]{1,3,2,0:T(8,128)(2,1)}, bf16[2,256,2,128]{1,3,2,0:T(8,128)(2,1)S(1)}, u32[]{:S(2)}) copy-start(bf16[2,256,2,128]{1,3,2,0:T(8,128)(2,1)S(1)} %copy.213) | copy-start | bytes 786436
  115.8 11.7 %copy-start.6 = (bf16[2,256,2,128]{1,3,2,0:T(8,128)(2,1)}, bf16[2,256,2,128]{1,3,2,0:T(8,128)(2,1)S(1)}, u32[]{:S(2)}) copy-start(bf16[2,256,2,128]{1,3,2,0:T(8,128)(2,1)S(1)} %copy.226) | copy-start | bytes 786436
  116.7 21.3 %all-to-all-start.3 = ((f32[8,5,32,128]{3,2,1,0:T(8,128)}), f32[8,5,32,128]{3,2,1,0:T(8,128)S(1)}, u32[]{:S(2)}, u32[]{:S(2)}) async-start(f32[8,5,32,128]{3,2,1,0:T(8,128)} %broadcast_in_dim.81), calls=%async_computation.3 | async-start | bytes 1310720 | tf_op jit(solution)/shard_map/all_to_all | solution.py:155
  127.8 0.8 copy-start.4
  138.1 2.6 %copy-start.11 = (f32[2,1,128,128]{3,1,2,0:T(1,128)S(1)}, f32[2,1,128,128]{3,1,2,0:T(1,128)}, u32[]{:S(2)}) copy-start(f32[2,1,128,128]{3,1,2,0:T(1,128)} %get-tuple-element.16) | copy-start | bytes 393220
  138.1 3.6 %copy-start.14 = (f32[2,2,128,128]{3,0,2,1:T(2,128)S(1)}, f32[2,2,128,128]{3,0,2,1:T(2,128)}, u32[]{:S(2)}) copy-start(f32[2,2,128,128]{3,0,2,1:T(2,128)} %copy.221) | copy-start | bytes 786436
  138.1 3.6 %copy-start.26 = (f32[2,2,1,1]{1,0,3,2:T(2,128)S(1)}, f32[2,2,1,1]{1,0,3,2:T(2,128)}, u32[]{:S(2)}) copy-start(f32[2,2,1,1]{1,0,3,2:T(2,128)} %constant.139) | copy-start | bytes 52
  141.6 2.1 %copy-start.5 = (bf16[2,2,256,256]{3,2,1,0:T(8,128)(2,1)S(1)}, bf16[2,2,256,256]{3,2,1,0:T(8,128)(2,1)}, u32[]{:S(2)}) copy-start(bf16[2,2,256,256]{3,2,1,0:T(8,128)(2,1)} %copy-done.4) | copy-start | bytes 1572868
  143.4 2.1 %copy-start.8 = (bf16[2,256,2,128]{1,3,2,0:T(8,128)(2,1)S(1)}, bf16[2,256,2,128]{1,3,2,0:T(8,128)(2,1)}, u32[]{:S(2)}) copy-start(bf16[2,256,2,128]{1,3,2,0:T(8,128)(2,1)} %copy-done.7) | copy-start | bytes 786436
  143.4 2.1 %copy-start.12 = (f32[2,256,2,128]{1,3,2,0:T(8,128)S(1)}, f32[2,256,2,128]{1,3,2,0:T(8,128)}, u32[]{:S(2)}) copy-start(f32[2,256,2,128]{1,3,2,0:T(8,128)} %fusion.2) | copy-start | bytes 1572868
  143.4 2.1 %copy-start.13 = (f32[2,256,2,128]{1,3,2,0:T(8,128)S(1)}, f32[2,256,2,128]{1,3,2,0:T(8,128)}, u32[]{:S(2)}) copy-start(f32[2,256,2,128]{1,3,2,0:T(8,128)} %fusion.1) | copy-start | bytes 1572868
  (1 other events, 0.6 us)

commit v10 on v9

--- a/solution.py
+++ b/solution.py
@@ -42,9 +42,13 @@
 
 
 def body(queries, key_vectors, value_vectors, grad_output, level_weights):
-    stacked = jnp.stack([queries, key_vectors, value_vectors, grad_output], axis=1)
-    exchanged = lax.all_to_all(stacked, "head", split_axis=2, concat_axis=0, tiled=True)
-    query_in, key_in, value_in, cotan_in = (exchanged[:, index] for index in range(4))
+    head_groups = lax.axis_size("head")
+    stacked = jnp.stack(
+        [matrix.reshape(matrix.shape[0], head_groups, -1) for matrix in (queries, key_vectors, value_vectors, grad_output)],
+        axis=0,
+    )
+    exchanged = lax.all_to_all(stacked, "head", split_axis=2, concat_axis=1, tiled=True)
+    query_in, key_in, value_in, cotan_in = (exchanged[index].reshape(exchanged.shape[1], -1) for index in range(4))
     tokens_dev = query_in.shape[0]
     heads_local = level_weights.shape[1]
     head_size = query_in.shape[1] // heads_local

time: 149 us -> 146 us (0.980)
  other arithmetic: 13.4 us -> 11.7 us
    unnamed x56 -> x60, local copies, waits for them, and re-layouts: 5.88 us -> 5.83 us
where the time goes in v10:
time: 146 us; the launch traced here: 145 us
  starting transfers between devices  58.7 us (40%)
  waiting for transfers between devices  32 us (22%)
  local copies, waits for them, and re-layouts  22 us (15%)
  matrix products  18.8 us (13%)
  other arithmetic  11.7 us (8%)
  between operations  1.49 us (1%)
    all_to_all x1, starting transfers between devices, body(): received = lax.all_to_all(chunks, 'z', 0, 0, tiled=True)  18.6 us
    ppermute x2, starting transfers between devices, swapped(): return lax.ppermute(value, axis, pairs)  18.4 us
    all_to_all x1, waiting for transfers between devices, body(): lax.all_to_all(stacked, 'head', split_axis=2, concat_axis=1, tiled=True)  16 us
    all_to_all x1, starting transfers between devices, body(): lax.all_to_all(spread, ('x', 'core'), 0, 0, tiled=True)  10.4 us
    all_to_all x1, waiting for transfers between devices, body(): lax.all_to_all(spread, ('x', 'core'), 0, 0, tiled=True)  9.16 us
    all_to_all x1, starting transfers between devices, body(): lax.all_to_all(stacked, 'head', split_axis=2, concat_axis=1, tiled=True)  7.65 us
    unnamed x60, local copies, waits for them, and re-layouts  5.83 us
    all_to_all x1, waiting for transfers between devices, body(): x_received = lax.all_to_all(x_send, 'x', 0, 0, tiled=True)  5.02 us
  transfers between devices with their start and end apart: 6, of which 5 were waited for; matrix products, arithmetic and copies ran while one was open for 14% of the time, Pallas kernels for 0%

profile of v10, /device:TPU:1, one launch (start us, length us, event | category | flops | bytes accessed | tf_op | source)
XLA Modules:
  0.0 144.8 jit_solution(3107919399797465512)
XLA Ops:
  1.6 1.0 copy.207
  2.6 1.0 copy.208
  4.8 1.2 copy.135
  6.0 7.7 %all-to-all-start = ((bf16[4,64,8,256]{3,1,0,2:T(8,128)(2,1)}), bf16[4,64,8,256]{3,1,0,2:T(8,128)(2,1)S(1)}, u32[]{:S(2)}, u32[]{:S(2)}) async-start(bf16[4,64,8,256]{3,1,0,2:T(8,128)(2,1)} %copy.135), calls=%async_computation | async-start | bytes 2097152 | tf_op jit(solution)/shard_map/all_to_all | solution.py:50
  14.5 16.0 %all-to-all-done = bf16[4,64,8,256]{3,1,0,2:T(8,128)(2,1)S(1)} async-done(((bf16[4,64,8,256]{3,1,0,2:T(8,128)(2,1)}), bf16[4,64,8,256]{3,1,0,2:T(8,128)(2,1)S(1)}, u32[]{:S(2)}, u32[]{:S(2)}) %all-to-all-start) | async-done | bytes 1048608 | tf_op jit(solution)/shard_map/all_to_all | solution.py:50
  32.4 1.2 copy.141
  34.7 1.4 broadcast_multiply_fusion
  36.1 1.0 pad_maximum_fusion.1
  37.1 15.1 %collective-permute-start = (f32[8,2,128,128]{3,2,1,0:T(8,128)}, f32[8,2,128,128]{3,2,1,0:T(8,128)}, u32[]{:S(2)}, u32[]{:S(2)}) collective-permute-start(f32[8,2,128,128]{3,2,1,0:T(8,128)} %pad_maximum_fusion.1), channel_id=1, source_target_pairs={{0,8},{8,0},{1,9},{9,1},{2,10},{10,2},{3,11},{11,3},{4,12},{12,4},... | collective-permute-start | bytes 3145736 | tf_op jit(solution)/shard_map/ppermute | solution.py:13
  52.2 1.3 slice.133
  56.7 1.4 slice_bitcast_fusion.5
  58.2 1.2 slice.129
  62.3 3.7 %all-to-all-start.1 = ((f32[4,9,32,128]{3,2,1,0:T(8,128)}), f32[4,9,32,128]{3,2,1,0:T(8,128)S(1)}, u32[]{:S(2)}, u32[]{:S(2)}) async-start(f32[4,9,32,128]{3,2,1,0:T(8,128)} %pad_maximum_fusion.2), calls=%async_computation.1 | async-start | bytes 1179648 | tf_op jit(solution)/shard_map/all_to_all | solution.py:103
  66.7 1.8 %fusion.23 = bf16[2,1,2,128,128]{4,0,3,2,1:T(2,128)(2,1)} fusion(f32[2,2,1,1]{1,0,3,2:T(2,128)S(1)} %copy-done.26, f32[2,2,128,128]{3,2,1,0:T(8,128)S(1)} %copy-done.13), kind=kOutput, calls=%fused_computation.39 | convolution fusion | flops 1638400 | bytes 393232 | tf_op jit(solution)/shard_map/mji,ihpr->jmhpr/dot_general | solution.py:164
  68.5 1.7 %copy.153 = bf16[2,1,2,128,128]{3,4,1,2,0:T(8,128)(2,1)} copy(bf16[2,1,2,128,128]{4,0,3,2,1:T(2,128)(2,1)} %fusion.23) | data formatting | bytes 262144 | tf_op jit(solution)/shard_map/mji,ihpr->jmhpr/transpose | solution.py:164
  71.0 5.0 %all-to-all-done.1 = f32[4,9,32,128]{3,2,1,0:T(8,128)S(1)} async-done(((f32[4,9,32,128]{3,2,1,0:T(8,128)}), f32[4,9,32,128]{3,2,1,0:T(8,128)S(1)}, u32[]{:S(2)}, u32[]{:S(2)}) %all-to-all-start.1) | async-done | bytes 589856 | tf_op jit(solution)/shard_map/all_to_all | solution.py:103
  77.8 18.6 %all-to-all-start.2 = ((f32[16,32,128]{2,1,0:T(8,128)}), f32[16,32,128]{2,1,0:T(8,128)S(1)}, u32[]{:S(2)}, u32[]{:S(2)}) async-start(f32[16,32,128]{2,1,0:T(8,128)} %broadcast_select_fusion), calls=%async_computation.2 | async-start | bytes 524288 | tf_op jit(solution)/shard_map/all_to_all | solution.py:125
  96.4 1.2 convolution_bitcast_fusion.2
  97.6 1.2 fusion.51
  99.0 3.3 %collective-permute-start.1 = (f32[3,128,128]{2,0,1:T(4,128)S(1)}, f32[3,128,128]{2,0,1:T(4,128)S(1)}, u32[]{:S(2)}, u32[]{:S(2)}) collective-permute-start(f32[3,128,128]{2,0,1:T(4,128)S(1)} %pad_maximum_fusion.7), channel_id=1, source_target_pairs={{0,8},{8,0},{1,9},{9,1},{2,10},{10,2},{3,11},{11,3},{4,12},{12,4},... | collective-permute-start | bytes 589832 | tf_op jit(solution)/shard_map/ppermute | solution.py:13
  104.9 1.3 fusion.2
  106.2 1.2 fusion.4
  107.5 1.7 %all-to-all-done.2 = f32[16,32,128]{2,1,0:T(8,128)S(1)} async-done(((f32[16,32,128]{2,1,0:T(8,128)}), f32[16,32,128]{2,1,0:T(8,128)S(1)}, u32[]{:S(2)}, u32[]{:S(2)}) %all-to-all-start.2) | async-done | bytes 262176 | tf_op jit(solution)/shard_map/all_to_all | solution.py:125
  109.1 1.1 fusion.29
  110.2 1.1 fusion.31
  112.8 10.4 %all-to-all-start.3 = ((f32[8,5,32,128]{3,2,1,0:T(8,128)}), f32[8,5,32,128]{3,2,1,0:T(8,128)S(1)}, u32[]{:S(2)}, u32[]{:S(2)}) async-start(f32[8,5,32,128]{3,2,1,0:T(8,128)} %broadcast_in_dim.81), calls=%async_computation.3 | async-start | bytes 1310720 | tf_op jit(solution)/shard_map/all_to_all | solution.py:159
  125.0 9.2 %all-to-all-done.3 = f32[8,5,32,128]{3,2,1,0:T(8,128)S(1)} async-done(((f32[8,5,32,128]{3,2,1,0:T(8,128)}), f32[8,5,32,128]{3,2,1,0:T(8,128)S(1)}, u32[]{:S(2)}, u32[]{:S(2)}) %all-to-all-start.3) | async-done | bytes 655392 | tf_op jit(solution)/shard_map/all_to_all | solution.py:159
  134.2 1.2 fusion.1
  135.4 1.3 fusion.3
  137.7 1.1 fusion.24
  139.8 1.5 %fusion.17 = bf16[2,256,2,128]{1,3,2,0:T(8,128)(2,1)S(1)} fusion(f32[2,256,2,128]{1,3,2,0:T(8,128)} %fusion.3, f32[2,256,2,128]{1,3,2,0:T(8,128)} %fusion.4, bf16[2,2,256,256]{3,2,1,0:T(8,128)(2,1)S(1)} %copy-done.5, bf16[2,256,2,128]{3,2,1,0:T(2,128)(2,1)S(1)} %reshape_reshape_squeeze.14), kind=kOutput, calls=%fused_computation.31 | convolution fusion | flops 67502080 | bytes 2097152 | tf_op jit(solution)/shard_map/bhtu,buhr->bthr/dot_general | solution.py:135
  141.5 1.3 fusion.16
  (130 shorter events, 24.8 us)
Async XLA Ops:
  4.8 8.9 %copy-start.18 = (s32[9,2,512]{2,1,0:T(2,128)S(1)}, s32[9,2,512]{2,1,0:T(2,128)}, u32[]{:S(2)}) copy-start(s32[9,2,512]{2,1,0:T(2,128)} %param.17) | copy-start | bytes 110596
  4.8 8.9 %copy-start.23 = (f32[9]{0:T(128)S(1)}, f32[9]{0:T(128)}, u32[]{:S(2)}) copy-start(f32[9]{0:T(128)} %constant.137) | copy-start | bytes 112
  6.0 24.4 %all-to-all-start = ((bf16[4,64,8,256]{3,1,0,2:T(8,128)(2,1)}), bf16[4,64,8,256]{3,1,0,2:T(8,128)(2,1)S(1)}, u32[]{:S(2)}, u32[]{:S(2)}) async-start(bf16[4,64,8,256]{3,1,0,2:T(8,128)(2,1)} %copy.135), calls=%async_computation | async-start | bytes 2097152 | tf_op jit(solution)/shard_map/all_to_all | solution.py:50
  14.5 17.0 %copy-start.12 = (f32[8,2,2,256]{3,0,1,2:T(8,128)}, f32[8,2,2,256]{3,0,1,2:T(8,128)S(1)}, u32[]{:S(2)}) copy-start(f32[8,2,2,256]{3,0,1,2:T(8,128)S(1)} %copy.260) | copy-start | bytes 98308
  14.5 38.9 %copy-start.21 = (f32[7]{0:T(128)}, f32[7]{0:T(128)S(1)}, u32[]{:S(2)}) copy-start(f32[7]{0:T(128)S(1)} %fusion.53) | copy-start | bytes 88
  30.8 0.7 copy-start
  34.7 1.4 copy-start.8
  34.7 18.8 %copy-start.25 = (s32[4,4]{1,0:T(4,128)S(1)}, s32[4,4]{1,0:T(4,128)}, u32[]{:S(2)}) copy-start(s32[4,4]{1,0:T(4,128)} %constant.123.clone) | copy-start | bytes 196
  37.1 21.0 %collective-permute-start = (f32[8,2,128,128]{3,2,1,0:T(8,128)}, f32[8,2,128,128]{3,2,1,0:T(8,128)}, u32[]{:S(2)}, u32[]{:S(2)}) collective-permute-start(f32[8,2,128,128]{3,2,1,0:T(8,128)} %pad_maximum_fusion.1), channel_id=1, source_target_pairs={{0,8},{8,0},{1,9},{9,1},{2,10},{10,2},{3,11},{11,3},{4,12},{12,4},... | collective-permute-start | bytes 3145736 | tf_op jit(solution)/shard_map/ppermute | solution.py:13
  58.2 2.3 %copy-start.9 = (f32[2,128,128]{2,1,0:T(8,128)S(1)}, f32[2,128,128]{2,1,0:T(8,128)}, u32[]{:S(2)}) copy-start(f32[2,128,128]{2,1,0:T(8,128)} %copy-done.8) | copy-start | bytes 393220
  59.4 1.9 %copy-start.24 = (pred[4]{0:T(512)(128)(4,1)S(1)}, pred[4]{0:T(512)(128)(4,1)}, u32[]{:S(2)}) copy-start(pred[4]{0:T(512)(128)(4,1)} %compare_and_fusion) | copy-start | bytes 16
  60.5 6.2 %copy-start.26 = (f32[2,2,1,1]{1,0,3,2:T(2,128)S(1)}, f32[2,2,1,1]{1,0,3,2:T(2,128)}, u32[]{:S(2)}) copy-start(f32[2,2,1,1]{1,0,3,2:T(2,128)} %constant.139) | copy-start | bytes 52
  61.3 5.4 %copy-start.13 = (f32[2,2,128,128]{3,2,1,0:T(8,128)S(1)}, f32[2,2,128,128]{3,2,1,0:T(8,128)}, u32[]{:S(2)}) copy-start(f32[2,2,128,128]{3,2,1,0:T(8,128)} %get-tuple-element.26) | copy-start | bytes 786436
  62.3 13.8 %all-to-all-start.1 = ((f32[4,9,32,128]{3,2,1,0:T(8,128)}), f32[4,9,32,128]{3,2,1,0:T(8,128)S(1)}, u32[]{:S(2)}, u32[]{:S(2)}) async-start(f32[4,9,32,128]{3,2,1,0:T(8,128)} %pad_maximum_fusion.2), calls=%async_computation.1 | async-start | bytes 1179648 | tf_op jit(solution)/shard_map/all_to_all | solution.py:103
  71.0 31.3 %copy-start.22 = (f32[7]{0:T(128)S(1)}, f32[7]{0:T(128)}, u32[]{:S(2)}) copy-start(f32[7]{0:T(128)} %copy-done.21) | copy-start | bytes 88
  77.8 31.4 %all-to-all-start.2 = ((f32[16,32,128]{2,1,0:T(8,128)}), f32[16,32,128]{2,1,0:T(8,128)S(1)}, u32[]{:S(2)}, u32[]{:S(2)}) async-start(f32[16,32,128]{2,1,0:T(8,128)} %broadcast_select_fusion), calls=%async_computation.2 | async-start | bytes 524288 | tf_op jit(solution)/shard_map/all_to_all | solution.py:125
  98.9 6.0 %copy-start.1 = (bf16[2,256,2,128]{3,2,1,0:T(2,128)(2,1)S(1)}, bf16[2,256,2,128]{3,2,1,0:T(2,128)(2,1)}, u32[]{:S(2)}) copy-start(bf16[2,256,2,128]{3,2,1,0:T(2,128)(2,1)} %copy-done) | copy-start | bytes 786436
  98.9 6.0 %copy-start.16 = (bf16[2,1,2,128,128]{3,4,1,2,0:T(8,128)(2,1)S(1)}, bf16[2,1,2,128,128]{3,4,1,2,0:T(8,128)(2,1)}, u32[]{:S(2)}) copy-start(bf16[2,1,2,128,128]{3,4,1,2,0:T(8,128)(2,1)} %copy.153) | copy-start | bytes 393220
  98.9 6.0 %copy-start.19 = (f32[2,4,256,2]{2,1,3,0:T(4,128)S(1)}, f32[2,4,256,2]{2,1,3,0:T(4,128)}, u32[]{:S(2)}) copy-start(f32[2,4,256,2]{2,1,3,0:T(4,128)} %get-tuple-element.21) | copy-start | bytes 49156
  99.0 4.5 %collective-permute-start.1 = (f32[3,128,128]{2,0,1:T(4,128)S(1)}, f32[3,128,128]{2,0,1:T(4,128)S(1)}, u32[]{:S(2)}, u32[]{:S(2)}) collective-permute-start(f32[3,128,128]{2,0,1:T(4,128)S(1)} %pad_maximum_fusion.7), channel_id=1, source_target_pairs={{0,8},{8,0},{1,9},{9,1},{2,10},{10,2},{3,11},{11,3},{4,12},{12,4},... | collective-permute-start | bytes 589832 | tf_op jit(solution)/shard_map/ppermute | solution.py:13
  103.7 2.6 %copy-start.3 = (bf16[2,256,2,128]{3,2,1,0:T(2,128)(2,1)S(1)}, bf16[2,256,2,128]{3,2,1,0:T(2,128)(2,1)}, u32[]{:S(2)}) copy-start(bf16[2,256,2,128]{3,2,1,0:T(2,128)(2,1)} %copy-done.2) | copy-start | bytes 786436
  111.3 11.9 %copy-start.17 = (pred[256,256]{1,0:T(8,128)(4,1)S(1)}, pred[256,256]{1,0:T(8,128)(4,1)}, u32[]{:S(2)}) copy-start(pred[256,256]{1,0:T(8,128)(4,1)} %iota_compare_fusion) | copy-start | bytes 196612
  111.3 11.9 %copy-start.20 = (f32[1,2,512]{2,1,0:T(2,128)S(1)}, f32[1,2,512]{2,1,0:T(2,128)}, u32[]{:S(2)}) copy-start(f32[1,2,512]{2,1,0:T(2,128)} %slice.133) | copy-start | bytes 12292
  111.7 12.2 %copy-start.6 = (bf16[2,256,2,128]{1,3,2,0:T(8,128)(2,1)}, bf16[2,256,2,128]{1,3,2,0:T(8,128)(2,1)S(1)}, u32[]{:S(2)}) copy-start(bf16[2,256,2,128]{1,3,2,0:T(8,128)(2,1)S(1)} %copy.164) | copy-start | bytes 786436
  112.8 21.3 %all-to-all-start.3 = ((f32[8,5,32,128]{3,2,1,0:T(8,128)}), f32[8,5,32,128]{3,2,1,0:T(8,128)S(1)}, u32[]{:S(2)}, u32[]{:S(2)}) async-start(f32[8,5,32,128]{3,2,1,0:T(8,128)} %broadcast_in_dim.81), calls=%async_computation.3 | async-start | bytes 1310720 | tf_op jit(solution)/shard_map/all_to_all | solution.py:159
  123.9 0.8 copy-start.4
  134.2 2.6 %copy-start.10 = (f32[2,1,128,128]{3,1,2,0:T(1,128)S(1)}, f32[2,1,128,128]{3,1,2,0:T(1,128)}, u32[]{:S(2)}) copy-start(f32[2,1,128,128]{3,1,2,0:T(1,128)} %get-tuple-element.16) | copy-start | bytes 393220
  134.2 3.5 %copy-start.14 = (f32[2,2,128,128]{3,0,2,1:T(2,128)S(1)}, f32[2,2,128,128]{3,0,2,1:T(2,128)}, u32[]{:S(2)}) copy-start(f32[2,2,128,128]{3,0,2,1:T(2,128)} %copy.172) | copy-start | bytes 786436
  134.2 3.5 %copy-start.27 = (f32[2,2,1,1]{1,0,3,2:T(2,128)S(1)}, f32[2,2,1,1]{1,0,3,2:T(2,128)}, u32[]{:S(2)}) copy-start(f32[2,2,1,1]{1,0,3,2:T(2,128)} %constant.139) | copy-start | bytes 52
  137.7 2.1 %copy-start.5 = (bf16[2,2,256,256]{3,2,1,0:T(8,128)(2,1)S(1)}, bf16[2,2,256,256]{3,2,1,0:T(8,128)(2,1)}, u32[]{:S(2)}) copy-start(bf16[2,2,256,256]{3,2,1,0:T(8,128)(2,1)} %copy-done.4) | copy-start | bytes 1572868
  139.5 2.1 %copy-start.7 = (bf16[2,256,2,128]{1,3,2,0:T(8,128)(2,1)S(1)}, bf16[2,256,2,128]{1,3,2,0:T(8,128)(2,1)}, u32[]{:S(2)}) copy-start(bf16[2,256,2,128]{1,3,2,0:T(8,128)(2,1)} %copy-done.6) | copy-start | bytes 786436
  139.5 2.1 %copy-start.11 = (f32[2,256,2,128]{1,3,2,0:T(8,128)S(1)}, f32[2,256,2,128]{1,3,2,0:T(8,128)}, u32[]{:S(2)}) copy-start(f32[2,256,2,128]{1,3,2,0:T(8,128)} %fusion.2) | copy-start | bytes 1572868
  (2 other events, 1.3 us)

commit v11 on v10

--- a/solution.py
+++ b/solution.py
@@ -124,7 +124,7 @@
     chunks = jnp.take(options, lax.dynamic_index_in_dim(choice, z_index, 0, keepdims=False), axis=0)
     received = lax.all_to_all(chunks, "z", 0, 0, tiled=True)
     late_query, late_key, late_value, late_cotan, _ = lax.optimization_barrier(
-        (query_rows, key_rows, value_rows, cotan_rows, received)
+        (query_rows, key_rows, value_rows, cotan_rows, chunks)
     )
     scores = jnp.einsum("bthp,buhp->bhtu", late_query, late_key, preferred_element_type=jnp.float32)
     attention = jnp.where(causal, scores * intra_w, 0.0).astype(jnp.bfloat16)

time: 146 us -> 153 us (1.048)
  other arithmetic: 11.7 us -> 15.7 us
  local copies, waits for them, and re-layouts: 22 us -> 24.3 us
  matrix products: 18.8 us -> 20.8 us
  waiting for transfers between devices: 32 us -> 30.4 us
    all_to_all x1, waiting for transfers between devices: 9.16 us -> 2.48 us  [body(): lax.all_to_all(spread, ('x', 'core'), 0, 0, tiled=True)]
    all_to_all x1, waiting for transfers between devices: 5.02 us -> 7.57 us  [body(): x_received = lax.all_to_all(x_send, 'x', 0, 0, tiled=True)]
    all_to_all x1, waiting for transfers between devices: 1.68 us -> 3.73 us  [body(): received = lax.all_to_all(chunks, 'z', 0, 0, tiled=True)]
    another operation x2, other arithmetic: 1.12 us -> 3.09 us  [ordered(): jnp.stack([jnp.where(other_first, other, own), jnp.where(other_first, own...]
    unnamed x60 -> x62, local copies, waits for them, and re-layouts: 5.83 us -> 5 us
  transfers between devices with their start and end apart: 6 -> 6, of which waited for: 5 -> 4; matrix products, arithmetic and copies ran while one was open for 14% -> 19% of each run, Pallas kernels for 0% -> 0%
where the time goes in v11:
time: 153 us; the launch traced here: 151 us
  starting transfers between devices  58.8 us (38%)
  waiting for transfers between devices  30.4 us (20%)
  local copies, waits for them, and re-layouts  24.3 us (16%)
  matrix products  20.8 us (14%)
  other arithmetic  15.7 us (10%)
    all_to_all x1, starting transfers between devices, body(): received = lax.all_to_all(chunks, 'z', 0, 0, tiled=True)  18.7 us
    ppermute x2, starting transfers between devices, swapped(): return lax.ppermute(value, axis, pairs)  18.4 us
    all_to_all x1, waiting for transfers between devices, body(): lax.all_to_all(stacked, 'head', split_axis=2, concat_axis=1, tiled=True)  16.6 us
    all_to_all x1, starting transfers between devices, body(): lax.all_to_all(spread, ('x', 'core'), 0, 0, tiled=True)  10.4 us
    all_to_all x1, starting transfers between devices, body(): lax.all_to_all(stacked, 'head', split_axis=2, concat_axis=1, tiled=True)  7.65 us
    all_to_all x1, waiting for transfers between devices, body(): x_received = lax.all_to_all(x_send, 'x', 0, 0, tiled=True)  7.57 us
    unnamed x62, local copies, waits for them, and re-layouts  5 us
    all_to_all x1, starting transfers between devices, body(): x_received = lax.all_to_all(x_send, 'x', 0, 0, tiled=True)  3.74 us
  transfers between devices with their start and end apart: 6, of which 4 were waited for; matrix products, arithmetic and copies ran while one was open for 19% of the time, Pallas kernels for 0%

profile of v11, /device:TPU:1, one launch (start us, length us, event | category | flops | bytes accessed | tf_op | source)
XLA Modules:
  0.0 151.4 jit_solution(6928495727616401690)
XLA Ops:
  4.8 1.2 copy.135
  6.1 7.7 %all-to-all-start = ((bf16[4,64,8,256]{3,1,0,2:T(8,128)(2,1)}), bf16[4,64,8,256]{3,1,0,2:T(8,128)(2,1)S(1)}, u32[]{:S(2)}, u32[]{:S(2)}) async-start(bf16[4,64,8,256]{3,1,0,2:T(8,128)(2,1)} %copy.135), calls=%async_computation | async-start | bytes 2097152 | tf_op jit(solution)/shard_map/all_to_all | solution.py:50
  13.9 16.6 %all-to-all-done = bf16[4,64,8,256]{3,1,0,2:T(8,128)(2,1)S(1)} async-done(((bf16[4,64,8,256]{3,1,0,2:T(8,128)(2,1)}), bf16[4,64,8,256]{3,1,0,2:T(8,128)(2,1)S(1)}, u32[]{:S(2)}, u32[]{:S(2)}) %all-to-all-start) | async-done | bytes 1048608 | tf_op jit(solution)/shard_map/all_to_all | solution.py:50
  32.4 1.3 copy.141
  34.7 1.4 broadcast_multiply_fusion
  37.1 15.1 %collective-permute-start = (f32[8,2,128,128]{3,2,1,0:T(8,128)}, f32[8,2,128,128]{3,2,1,0:T(8,128)}, u32[]{:S(2)}, u32[]{:S(2)}) collective-permute-start(f32[8,2,128,128]{3,2,1,0:T(8,128)} %pad_maximum_fusion.1), channel_id=1, source_target_pairs={{0,8},{8,0},{1,9},{9,1},{2,10},{10,2},{3,11},{11,3},{4,12},{12,4},... | collective-permute-start | bytes 3145736 | tf_op jit(solution)/shard_map/ppermute | solution.py:13
  52.2 1.3 slice.133
  55.4 1.2 compare_and_fusion.1
  58.5 1.4 slice_bitcast_fusion.5
  60.8 2.8 %fusion.23 = bf16[2,1,2,128,128]{4,0,3,2,1:T(2,128)(2,1)} fusion(f32[2,2,1,1]{1,0,3,2:T(2,128)} %constant.139, f32[2,2,128,128]{3,2,1,0:T(8,128)} %get-tuple-element.26), kind=kOutput, calls=%fused_computation.39 | convolution fusion | flops 1638400 | bytes 393232 | tf_op jit(solution)/shard_map/mji,ihpr->jmhpr/dot_general | solution.py:164
  63.6 1.7 %copy.153 = bf16[2,1,2,128,128]{3,4,1,2,0:T(8,128)(2,1)} copy(bf16[2,1,2,128,128]{4,0,3,2,1:T(2,128)(2,1)} %fusion.23) | data formatting | bytes 262144 | tf_op jit(solution)/shard_map/mji,ihpr->jmhpr/transpose | solution.py:164
  65.4 1.2 slice.129
  69.5 3.7 %all-to-all-start.1 = ((f32[4,9,32,128]{3,2,1,0:T(8,128)}), f32[4,9,32,128]{3,2,1,0:T(8,128)S(1)}, u32[]{:S(2)}, u32[]{:S(2)}) async-start(f32[4,9,32,128]{3,2,1,0:T(8,128)} %pad_maximum_fusion.2), calls=%async_computation.1 | async-start | bytes 1179648 | tf_op jit(solution)/shard_map/all_to_all | solution.py:103
  74.1 1.6 %slice_multiply_fusion.1 = bf16[1,2,128,128]{3,2,1,0:T(8,128)(2,1)} fusion(f32[8,2,128,128]{3,2,1,0:T(8,128)} %collective-permute-done, f32[]{:T(128)S(1)} %bitcast.254), kind=kLoop, calls=%fused_computation.94 | loop fusion | flops 65536 | bytes 196612 | tf_op jit(solution)/shard_map/mul | solution.py:93
  75.7 7.6 %all-to-all-done.1 = f32[4,9,32,128]{3,2,1,0:T(8,128)S(1)} async-done(((f32[4,9,32,128]{3,2,1,0:T(8,128)}), f32[4,9,32,128]{3,2,1,0:T(8,128)S(1)}, u32[]{:S(2)}, u32[]{:S(2)}) %all-to-all-start.1) | async-done | bytes 589856 | tf_op jit(solution)/shard_map/all_to_all | solution.py:103
  84.8 18.7 %all-to-all-start.2 = ((f32[16,32,128]{2,1,0:T(8,128)}), f32[16,32,128]{2,1,0:T(8,128)S(1)}, u32[]{:S(2)}, u32[]{:S(2)}) async-start(f32[16,32,128]{2,1,0:T(8,128)} %broadcast_select_fusion), calls=%async_computation.2 | async-start | bytes 524288 | tf_op jit(solution)/shard_map/all_to_all | solution.py:125
  104.2 1.3 convolution_bitcast_fusion.2
  105.4 1.2 fusion.51
  106.8 3.3 %collective-permute-start.1 = (f32[3,128,128]{2,0,1:T(4,128)S(1)}, f32[3,128,128]{2,0,1:T(4,128)S(1)}, u32[]{:S(2)}, u32[]{:S(2)}) collective-permute-start(f32[3,128,128]{2,0,1:T(4,128)S(1)} %pad_maximum_fusion.7), channel_id=1, source_target_pairs={{0,8},{8,0},{1,9},{9,1},{2,10},{10,2},{3,11},{11,3},{4,12},{12,4},... | collective-permute-start | bytes 589832 | tf_op jit(solution)/shard_map/ppermute | solution.py:13
  112.5 3.7 %all-to-all-done.2 = f32[16,32,128]{2,1,0:T(8,128)S(1)} async-done(((f32[16,32,128]{2,1,0:T(8,128)}), f32[16,32,128]{2,1,0:T(8,128)S(1)}, u32[]{:S(2)}, u32[]{:S(2)}) %all-to-all-start.2) | async-done | bytes 262176 | tf_op jit(solution)/shard_map/all_to_all | solution.py:125
  116.3 1.1 fusion.29
  117.4 1.1 fusion.31
  119.5 10.4 %all-to-all-start.3 = ((f32[8,5,32,128]{3,2,1,0:T(8,128)}), f32[8,5,32,128]{3,2,1,0:T(8,128)S(1)}, u32[]{:S(2)}, u32[]{:S(2)}) async-start(f32[8,5,32,128]{3,2,1,0:T(8,128)} %broadcast_in_dim.81), calls=%async_computation.3 | async-start | bytes 1310720 | tf_op jit(solution)/shard_map/all_to_all | solution.py:159
  129.8 2.2 %pad_maximum_fusion.8 = (f32[2,1,128,128]{3,1,2,0:T(1,128)}, f32[2,1,128,128]{3,1,2,0:T(1,128)S(1)}, f32[2,1,128,128]{3,1,2,0:T(1,128)S(1)}) fusion(f32[1,3,128,128]{3,1,2,0:T(4,128)} %get-tuple-element.20, f32[1,3,128,128]{3,1,2,0:T(4,128)S(1)} %get-tuple-element.19), kind=kLoop, calls=%fused_computation.85 | loop fusion | flops 98304 | bytes 786432 | tf_op jit(solution)/shard_map/stack | solution.py:153
  134.8 2.2 %fusion.2 = f32[2,256,2,128]{1,3,2,0:T(8,128)} fusion(f32[2,4,256,2]{2,1,3,0:T(4,128)} %get-tuple-element.21, bf16[2,3,2,128,128]{3,4,1,2,0:T(8,128)(2,1)S(1)} %broadcast_in_dim.79, bf16[2,1,2,128,128]{3,4,1,2,0:T(8,128)(2,1)} %copy.153, bf16[2,256,2,128,1]{3,2,1,0,4:T(2,128)(2,1)S(1)} %bitcast.220), kind=kOutput, calls=%fused_computation.7 | convolution fusion | flops 136183808 | bytes 1327104 | tf_op jit(solution)/shard_map/bmhpr,bthr->bmthp/dot_general | solution.py:181
  137.0 1.2 fusion.4
  138.3 2.5 %all-to-all-done.3 = f32[8,5,32,128]{3,2,1,0:T(8,128)S(1)} async-done(((f32[8,5,32,128]{3,2,1,0:T(8,128)}), f32[8,5,32,128]{3,2,1,0:T(8,128)S(1)}, u32[]{:S(2)}, u32[]{:S(2)}) %all-to-all-start.3) | async-done | bytes 655392 | tf_op jit(solution)/shard_map/all_to_all | solution.py:159
  140.8 1.3 fusion.1
  142.1 1.3 fusion.3
  144.4 1.1 fusion.24
  146.5 1.5 fusion.17
  148.2 1.3 fusion.16
  (132 shorter events, 28.9 us)
Async XLA Ops:
  4.8 8.9 %copy-start.18 = (s32[9,2,512]{2,1,0:T(2,128)S(1)}, s32[9,2,512]{2,1,0:T(2,128)}, u32[]{:S(2)}) copy-start(s32[9,2,512]{2,1,0:T(2,128)} %param.17) | copy-start | bytes 110596
  4.8 8.9 %copy-start.24 = (f32[9]{0:T(128)S(1)}, f32[9]{0:T(128)}, u32[]{:S(2)}) copy-start(f32[9]{0:T(128)} %constant.137) | copy-start | bytes 112
  6.1 24.4 %all-to-all-start = ((bf16[4,64,8,256]{3,1,0,2:T(8,128)(2,1)}), bf16[4,64,8,256]{3,1,0,2:T(8,128)(2,1)S(1)}, u32[]{:S(2)}, u32[]{:S(2)}) async-start(bf16[4,64,8,256]{3,1,0,2:T(8,128)(2,1)} %copy.135), calls=%async_computation | async-start | bytes 2097152 | tf_op jit(solution)/shard_map/all_to_all | solution.py:50
  13.8 16.8 %copy-start.15 = (f32[9,2,512]{2,1,0:T(2,128)}, f32[9,2,512]{2,1,0:T(2,128)S(1)}, u32[]{:S(2)}) copy-start(f32[9,2,512]{2,1,0:T(2,128)S(1)} %convert_multiply_fusion) | copy-start | bytes 110596
  13.9 17.6 %copy-start.13 = (f32[8,2,2,256]{3,0,1,2:T(8,128)}, f32[8,2,2,256]{3,0,1,2:T(8,128)S(1)}, u32[]{:S(2)}) copy-start(f32[8,2,2,256]{3,0,1,2:T(8,128)S(1)} %copy.260) | copy-start | bytes 98308
  13.9 39.6 %copy-start.21 = (f32[7]{0:T(128)}, f32[7]{0:T(128)S(1)}, u32[]{:S(2)}) copy-start(f32[7]{0:T(128)S(1)} %fusion.53) | copy-start | bytes 88
  34.7 1.4 copy-start.9
  34.7 17.5 %copy-start.27 = (s32[4,4]{1,0:T(4,128)S(1)}, s32[4,4]{1,0:T(4,128)}, u32[]{:S(2)}) copy-start(s32[4,4]{1,0:T(4,128)} %constant.123.clone) | copy-start | bytes 196
  37.1 28.2 %collective-permute-start = (f32[8,2,128,128]{3,2,1,0:T(8,128)}, f32[8,2,128,128]{3,2,1,0:T(8,128)}, u32[]{:S(2)}, u32[]{:S(2)}) collective-permute-start(f32[8,2,128,128]{3,2,1,0:T(8,128)} %pad_maximum_fusion.1), channel_id=1, source_target_pairs={{0,8},{8,0},{1,9},{9,1},{2,10},{10,2},{3,11},{11,3},{4,12},{12,4},... | collective-permute-start | bytes 3145736 | tf_op jit(solution)/shard_map/ppermute | solution.py:13
  60.8 5.7 %copy-start.6 = (f32[6,2,128,128]{3,2,1,0:T(8,128)S(1)}, f32[6,2,128,128]{3,2,1,0:T(8,128)}, u32[]{:S(2)}) copy-start(f32[6,2,128,128]{3,2,1,0:T(8,128)} %slice.128) | copy-start | bytes 2359300
  63.6 4.0 %copy-start.10 = (f32[2,128,128]{2,1,0:T(8,128)S(1)}, f32[2,128,128]{2,1,0:T(8,128)}, u32[]{:S(2)}) copy-start(f32[2,128,128]{2,1,0:T(8,128)} %copy-done.9) | copy-start | bytes 393220
  65.3 2.3 %copy-start.26 = (f32[4]{0:T(128)S(1)}, f32[4]{0:T(128)}, u32[]{:S(2)}) copy-start(f32[4]{0:T(128)} %pad.16.clone) | copy-start | bytes 52
  66.6 1.8 %copy-start.25 = (pred[4]{0:T(512)(128)(4,1)S(1)}, pred[4]{0:T(512)(128)(4,1)}, u32[]{:S(2)}) copy-start(pred[4]{0:T(512)(128)(4,1)} %compare_and_fusion) | copy-start | bytes 16
  68.5 5.6 %copy-start.22 = (f32[7]{0:T(128)S(1)}, f32[7]{0:T(128)}, u32[]{:S(2)}) copy-start(f32[7]{0:T(128)} %copy-done.21) | copy-start | bytes 88
  68.6 15.4 %copy-start.23 = (pred[16]{0:T(512)(128)(4,1)S(1)}, pred[16]{0:T(512)(128)(4,1)}, u32[]{:S(2)}) copy-start(pred[16]{0:T(512)(128)(4,1)} %compare_and_fusion.1) | copy-start | bytes 52
  69.5 13.8 %all-to-all-start.1 = ((f32[4,9,32,128]{3,2,1,0:T(8,128)}), f32[4,9,32,128]{3,2,1,0:T(8,128)S(1)}, u32[]{:S(2)}, u32[]{:S(2)}) async-start(f32[4,9,32,128]{3,2,1,0:T(8,128)} %pad_maximum_fusion.2), calls=%async_computation.1 | async-start | bytes 1179648 | tf_op jit(solution)/shard_map/all_to_all | solution.py:103
  73.2 30.5 %copy-start.3 = (bf16[2,256,2,128]{3,2,1,0:T(2,128)(2,1)S(1)}, bf16[2,256,2,128]{3,2,1,0:T(2,128)(2,1)}, u32[]{:S(2)}) copy-start(bf16[2,256,2,128]{3,2,1,0:T(2,128)(2,1)} %copy-done.2) | copy-start | bytes 786436
  75.6 28.4 %copy-start.1 = (bf16[2,256,2,128]{3,2,1,0:T(2,128)(2,1)S(1)}, bf16[2,256,2,128]{3,2,1,0:T(2,128)(2,1)}, u32[]{:S(2)}) copy-start(bf16[2,256,2,128]{3,2,1,0:T(2,128)(2,1)} %copy-done) | copy-start | bytes 786436
  84.8 25.4 %copy-start.17 = (pred[256,256]{1,0:T(8,128)(4,1)S(1)}, pred[256,256]{1,0:T(8,128)(4,1)}, u32[]{:S(2)}) copy-start(pred[256,256]{1,0:T(8,128)(4,1)} %iota_compare_fusion) | copy-start | bytes 196612
  84.8 25.4 %copy-start.20 = (f32[1,2,512]{2,1,0:T(2,128)S(1)}, f32[1,2,512]{2,1,0:T(2,128)}, u32[]{:S(2)}) copy-start(f32[1,2,512]{2,1,0:T(2,128)} %slice.133) | copy-start | bytes 12292
  84.8 31.5 %all-to-all-start.2 = ((f32[16,32,128]{2,1,0:T(8,128)}), f32[16,32,128]{2,1,0:T(8,128)S(1)}, u32[]{:S(2)}, u32[]{:S(2)}) async-start(f32[16,32,128]{2,1,0:T(8,128)} %broadcast_select_fusion), calls=%async_computation.2 | async-start | bytes 524288 | tf_op jit(solution)/shard_map/all_to_all | solution.py:125
  104.0 6.8 %copy-start.7 = (bf16[2,256,2,128]{1,3,2,0:T(8,128)(2,1)}, bf16[2,256,2,128]{1,3,2,0:T(8,128)(2,1)S(1)}, u32[]{:S(2)}) copy-start(bf16[2,256,2,128]{1,3,2,0:T(8,128)(2,1)S(1)} %copy.164) | copy-start | bytes 786436
  106.8 4.5 %collective-permute-start.1 = (f32[3,128,128]{2,0,1:T(4,128)S(1)}, f32[3,128,128]{2,0,1:T(4,128)S(1)}, u32[]{:S(2)}, u32[]{:S(2)}) collective-permute-start(f32[3,128,128]{2,0,1:T(4,128)S(1)} %pad_maximum_fusion.7), channel_id=1, source_target_pairs={{0,8},{8,0},{1,9},{9,1},{2,10},{10,2},{3,11},{11,3},{4,12},{12,4},... | collective-permute-start | bytes 589832 | tf_op jit(solution)/shard_map/ppermute | solution.py:13
  119.5 21.3 %all-to-all-start.3 = ((f32[8,5,32,128]{3,2,1,0:T(8,128)}), f32[8,5,32,128]{3,2,1,0:T(8,128)S(1)}, u32[]{:S(2)}, u32[]{:S(2)}) async-start(f32[8,5,32,128]{3,2,1,0:T(8,128)} %broadcast_in_dim.81), calls=%async_computation.3 | async-start | bytes 1310720 | tf_op jit(solution)/shard_map/all_to_all | solution.py:159
  132.1 5.0 %copy-start.19 = (f32[2,4,256,2]{2,1,3,0:T(4,128)S(1)}, f32[2,4,256,2]{2,1,3,0:T(4,128)}, u32[]{:S(2)}) copy-start(f32[2,4,256,2]{2,1,3,0:T(4,128)} %get-tuple-element.21) | copy-start | bytes 49156
  133.8 3.3 %copy-start.16 = (bf16[2,1,2,128,128]{3,4,1,2,0:T(8,128)(2,1)S(1)}, bf16[2,1,2,128,128]{3,4,1,2,0:T(8,128)(2,1)}, u32[]{:S(2)}) copy-start(bf16[2,1,2,128,128]{3,4,1,2,0:T(8,128)(2,1)} %copy.153) | copy-start | bytes 393220
  140.8 2.6 %copy-start.11 = (f32[2,1,128,128]{3,1,2,0:T(1,128)S(1)}, f32[2,1,128,128]{3,1,2,0:T(1,128)}, u32[]{:S(2)}) copy-start(f32[2,1,128,128]{3,1,2,0:T(1,128)} %get-tuple-element.16) | copy-start | bytes 393220
  140.8 3.5 %copy-start.14 = (f32[2,2,128,128]{3,0,2,1:T(2,128)S(1)}, f32[2,2,128,128]{3,0,2,1:T(2,128)}, u32[]{:S(2)}) copy-start(f32[2,2,128,128]{3,0,2,1:T(2,128)} %copy.172) | copy-start | bytes 786436
  140.8 3.5 %copy-start.28 = (f32[2,2,1,1]{1,0,3,2:T(2,128)S(1)}, f32[2,2,1,1]{1,0,3,2:T(2,128)}, u32[]{:S(2)}) copy-start(f32[2,2,1,1]{1,0,3,2:T(2,128)} %constant.139) | copy-start | bytes 52
  144.4 2.1 %copy-start.5 = (bf16[2,2,256,256]{3,2,1,0:T(8,128)(2,1)S(1)}, bf16[2,2,256,256]{3,2,1,0:T(8,128)(2,1)}, u32[]{:S(2)}) copy-start(bf16[2,2,256,256]{3,2,1,0:T(8,128)(2,1)} %copy-done.4) | copy-start | bytes 1572868
  146.1 2.1 %copy-start.8 = (bf16[2,256,2,128]{1,3,2,0:T(8,128)(2,1)S(1)}, bf16[2,256,2,128]{1,3,2,0:T(8,128)(2,1)}, u32[]{:S(2)}) copy-start(bf16[2,256,2,128]{1,3,2,0:T(8,128)(2,1)} %copy-done.7) | copy-start | bytes 786436
  146.3 1.9 %copy-start.12 = (f32[2,256,2,128]{1,3,2,0:T(8,128)S(1)}, f32[2,256,2,128]{1,3,2,0:T(8,128)}, u32[]{:S(2)}) copy-start(f32[2,256,2,128]{1,3,2,0:T(8,128)} %fusion.2) | copy-start | bytes 1572868
  (3 other events, 2.2 us)
